TPU v7x, 32 devices: a whole 2x2x4 slice. The times are simulated.
32 devices in a mesh: kv: 4 (over z), blk: 8 (over y, x, core).
Axes of the slice: x: 2, y: 2, z: 4, core: 2. Of those that a mesh axis runs over, the one named last changes fastest.
Arguments:
- queries: bfloat16 [640, 2048], P('blk', 'kv'), may hold values from -32 to 32, as said below
- keys: bfloat16 [640, 512], P('blk', 'kv'), may hold values from -7 to 7, as said below
- values: bfloat16 [640, 512], P('blk', 'kv'), may hold values from -6 to 6
- lengths: int32 [4], replicated, may hold values from 1 to 80, 128 in all
- out_weight: bfloat16 [4096, 2048], P('blk', 'kv'), may hold values from -0.125 to 0.125
Outputs:
- hidden: bfloat16 [640, 4096], P('blk', 'kv')
- cache_keys: bfloat16 [640, 512], P('blk', 'kv')
Inputs may be any that keep to these rules, and one draw needn't show every extreme that they name: `queries`: rotary inputs of order one; in some rows a query head may be a multiple of its key head. `keys`: key projections of order one. `lengths`: each short prompt is 1 to 80 tokens long, one of them exactly 80; their sum is 128.
All inputs are finite; a program needn't handle non-finite values.
Results may differ from a plain program's by a relative error of at most 0.0095.
Values may be sent and summed in bfloat16 or wider, within the bound.
No kernel may reach another device: no remote copies, remote signals or barrier semaphores. Data moves between devices by JAX's collectives and lax.ppermute only.
A program may use at most 64 MiB of HBM per device.

v0:
```python
import jax
import jax.numpy as jnp
from jax import lax
from jax.sharding import PartitionSpec as P

rope_base = 500000.0


def locate(index, starts):
    hit = starts[None, :] <= index[:, None]
    segment = jnp.sum(hit.astype(jnp.int32), axis=1) - 1
    offset = jnp.max(jnp.where(hit, starts[None, :], 0), axis=1)
    return (segment, offset)


def rotate(field, positions):
    half = field.shape[-1] // 2
    steps = jnp.arange(half).astype(jnp.float32) * (2.0 / field.shape[-1])
    inverse = jnp.power(jnp.float32(rope_base), -steps)
    angle = positions.astype(jnp.float32)[:, None, None] * inverse[None, None, :]
    cosine = jnp.cos(angle)
    sine = jnp.sin(angle)
    first = field[..., :half].astype(jnp.float32)
    second = field[..., half:].astype(jnp.float32)
    return jnp.concatenate(
        [first * cosine - second * sine, second * cosine + first * sine], axis=-1
    )


def body(queries, keys, values, lengths, out_weight):
    tok_rows = queries.shape[0]
    head_size = keys.shape[1]
    groups = queries.shape[1] // head_size
    total_len = tok_rows * lax.axis_size("blk")
    long_len = total_len - jnp.sum(lengths)
    shifted = jnp.concatenate([jnp.zeros((1,), jnp.int32), jnp.cumsum(lengths)[:-1]])
    starts = jnp.concatenate([jnp.zeros((1,), jnp.int32), long_len + shifted])
    first_tok = lax.axis_index("blk") * tok_rows
    query_idx = first_tok + jnp.arange(tok_rows)
    query_seg, query_off = locate(query_idx, starts)
    positions = query_idx - query_off
    rot_keys = (
        rotate(keys.reshape(tok_rows, 1, head_size), positions)
        .astype(jnp.bfloat16)
        .reshape(tok_rows, head_size)
    )
    rot_queries = rotate(queries.reshape(tok_rows, groups, head_size), positions).astype(
        jnp.bfloat16
    )
    query_rows = jnp.transpose(rot_queries, (1, 0, 2)).reshape(groups * tok_rows, head_size)
    row_idx = jnp.tile(query_idx, groups)
    row_seg = jnp.tile(query_seg, groups)
    scale = 1.0 / head_size**0.5
    row_count = groups * tok_rows
    key_piece = lax.all_gather(rot_keys, "blk", axis=0, tiled=True)
    value_piece = lax.all_gather(values, "blk", axis=0, tiled=True)
    row_max = jnp.full((row_count,), -1e30, jnp.float32)
    span = key_piece.shape[0]
    key_idx = jnp.arange(span)
    key_seg, key_off = locate(key_idx, starts)
    live = (key_seg[None, :] == row_seg[:, None]) & (key_idx[None, :] <= row_idx[:, None])
    scores = (
        jnp.einsum("rd,nd->rn", query_rows, key_piece, preferred_element_type=jnp.float32) * scale
    )
    scores = jnp.where(live, scores, -1e30)
    new_max = jnp.maximum(row_max, jnp.max(scores, axis=1))
    probs = jnp.where(live, jnp.exp(scores - new_max[:, None]), 0.0)
    new_sum = jnp.sum(probs, axis=1)
    new_weighted = jnp.dot(
        probs.astype(jnp.bfloat16), value_piece, preferred_element_type=jnp.float32
    )
    attended = (new_weighted / new_sum[:, None]).astype(jnp.bfloat16)
    attended = jnp.transpose(attended.reshape(groups, tok_rows, head_size), (1, 0, 2)).reshape(
        tok_rows, groups * head_size
    )
    terms = jnp.einsum(
        "tk,nk->tn",
        attended,
        lax.all_gather(out_weight, "blk", axis=0, tiled=True),
        preferred_element_type=jnp.float32,
    )
    hidden = lax.psum_scatter(terms.astype(jnp.bfloat16), "kv", scatter_dimension=1, tiled=True)
    return (hidden, rot_keys)


def solution(mesh):
    return jax.shard_map(
        body,
        mesh=mesh,
        in_specs=(P("blk", "kv"), P("blk", "kv"), P("blk", "kv"), P(), P("blk", "kv")),
        out_specs=(P("blk", "kv"), P("blk", "kv")),
        check_vma=False,
    )
```

profile of v0, /device:TPU:0, one launch (start us, length us, event | category | flops | bytes accessed | tf_op | source)
XLA Modules:
  0.0 83.1 jit_solution(14492427191002520922)
XLA Ops:
  7.2 0.7 all-gather.2.cloned.1.call-update
  7.9 0.0 reduce-scatter.2.cloned.1.call-start
  7.9 1.3 %reduce_sum.36 = s32[]{:T(128)} reduce(s32[4]{0:T(128)} %param.8, s32[]{:T(128)} %constant.15.clone.1), dimensions={0}, to_apply=%region_0.0 | reduce | flops 3 | bytes 24 | tf_op jit(solution)/shard_map/reduce_sum | solution.py:35
  9.2 0.8 reduce-window.4
  10.1 0.9 %reshape.179 = bf16[80,4,128]{2,1,0:T(4,128)(2,1)S(1)} reshape(bf16[80,512]{1,0:T(8,128)(2,1)} %param.5) | data formatting | bytes 163840 | tf_op jit(solution)/shard_map/reshape | solution.py:47
  11.7 0.1 add_add_fusion
  11.7 0.1 pad_add_fusion
  11.8 0.1 fusion.27
  11.9 0.2 multiply_cosine_fusion.1
  12.2 0.2 fusion.12
  12.3 0.1 maximum_bitcast_fusion
  12.5 0.1 eq.16
  12.6 0.1 le.48
  12.7 1.0 %fusion.26 = (bf16[80,64]{1,0:T(8,128)(2,1)S(1)}, bf16[80,64]{1,0:T(8,128)(2,1)S(1)}) fusion(f32[64]{0:T(128)S(1)} %negate_power_fusion, f32[80]{0:T(128)S(1)} %get-tuple-element.12, bf16[80,1,128]{2,0,1:T(8,128)(2,1)} %bitcast.24), kind=kLoop, calls=%fused_computation.39 | loop fusion | flops 56320 | bytes 41536 | tf_op jit(solution)/shard_map/concatenate | solution.py:25
  13.7 0.1 pad_maximum_fusion
  13.8 10.7 %all_gather.9 = bf16[640,128]{1,0:T(8,128)(2,1)S(1)} all-gather(bf16[80,128]{1,0:T(8,128)(2,1)S(1)} %pad_maximum_fusion), channel_id=1, replica_groups=mesh['kv'=4,'blk'=8] {'blk'}, dimensions={0}, use_global_device_ids=true | all-gather | bytes 184320 | tf_op jit(solution)/shard_map/all_gather | solution.py:55
  24.5 9.6 %all_gather.10 = bf16[640,128]{1,0:T(8,128)(2,1)S(1)} all-gather(bf16[80,128]{1,0:T(8,128)(2,1)} %param.7), channel_id=1, replica_groups=mesh['kv'=4,'blk'=8] {'blk'}, dimensions={0}, use_global_device_ids=true | all-gather | bytes 184320 | tf_op jit(solution)/shard_map/all_gather | solution.py:56
  34.1 0.1 convert_reduce_fusion
  34.2 0.4 fusion.30
  34.7 0.4 fusion.3
  35.1 0.4 fusion.1
  35.5 14.0 %all-gather.2.cloned.1.call-done = bf16[4096,512]{1,0:T(8,128)(2,1)} async-done(((bf16[512,512]{1,0:T(8,128)(2,1)}), bf16[4096,512]{1,0:T(8,128)(2,1)}) %all-gather.2.cloned.1.call-update) | async-done | bytes 4194320 | tf_op jit(solution)/shard_map/all_gather | solution.py:79
  49.5 4.4 %convolution_convert_fusion = bf16[80,4096]{1,0:T(8,128)(2,1)} fusion(bf16[4096,512]{1,0:T(8,128)(2,1)} %all-gather.2.cloned.1.call-done, bf16[10,8,4,128]{3,2,1,0:T(4,128)(2,1)S(1)} %bitcast.21), kind=kOutput, calls=%fused_computation | convolution fusion | flops 335872000 | bytes 4931584 | tf_op jit(solution)/shard_map/tk,nk->tn/dot_general | solution.py:76
  54.0 22.3 %reduce-scatter.2.cloned.1.call-done = bf16[80,1024]{1,0:T(8,128)(2,1)} async-done(((bf16[80,4096]{1,0:T(8,128)(2,1)}), bf16[80,1024]{1,0:T(8,128)(2,1)}) %reduce-scatter.2.cloned.1.call-update) | async-done | bytes 163856 | tf_op jit(solution)/shard_map/reduce_scatter | solution.py:82
  (14 shorter events, 0.1 us)
Async XLA Ops:
  7.2 42.3 %all-gather.2.cloned.1.call-start = ((), (), s32[]{:S(2)}) async-start(), calls=%async_computation.1 | async-start | bytes 4718592 | tf_op jit(solution)/shard_map/all_gather | solution.py:79
  7.9 68.4 %reduce-scatter.2.cloned.1.call-start = ((), (), s32[]{:S(2)}) async-start(), calls=%async_computation.2 | async-start | bytes 819200 | tf_op jit(solution)/shard_map/reduce_scatter | solution.py:82
  13.8 40.1 %copy-start = (bf16[80,128]{1,0:T(8,128)(2,1)}, bf16[80,128]{1,0:T(8,128)(2,1)S(1)}, u32[]{:S(2)}) copy-start(bf16[80,128]{1,0:T(8,128)(2,1)S(1)} %pad_maximum_fusion) | copy-start | bytes 61444
Sparse Core Ops, SparseCore 0:
  9.9 39.5 all-gather.1
  54.1 22.1 reduce-scatter.1
where the time goes:
time: 83.5 us; the launch traced here: 83.1 us
  waiting for transfers between devices  37 us (44%)
  blocking collectives  20.3 us (24%)
  between operations  14.8 us (18%)
  matrix products  5.27 us (6%)
  other arithmetic  4.53 us (5%)
  local copies, waits for them, and re-layouts  1.14 us (1%)
    reduce_scatter x1, waiting for transfers between devices, body(): lax.psum_scatter(terms.astype(jnp.bfloat16), 'kv', scatter_dimension=1, t...  22.3 us
    all_gather x1, waiting for transfers between devices, body(): lax.all_gather(out_weight, 'blk', axis=0, tiled=True)  14 us
    all_gather x1, blocking collectives, body(): key_piece = lax.all_gather(rot_keys, 'blk', axis=0, tiled=True)  10.7 us
    all_gather x1, blocking collectives, body(): value_piece = lax.all_gather(values, 'blk', axis=0, tiled=True)  9.6 us
    dot_general x1, matrix products, body(): jnp.einsum('tk,nk->tn', attended, lax.all_gather(out_weight, 'blk', axis=...  4.42 us
  transfers between devices with their start and end apart: 2, of which 2 were waited for; matrix products, arithmetic and copies ran while one was open for 8% of the time, Pallas kernels for 0%

commit v1 on v0

--- a/solution.py
+++ b/solution.py
@@ -1,9 +1,11 @@
 import jax
 import jax.numpy as jnp
 from jax import lax
+from jax.sharding import Mesh
 from jax.sharding import PartitionSpec as P
 
 rope_base = 500000.0
+BLK = ("chip", "core")
 
 
 def locate(index, starts):
@@ -31,11 +33,13 @@
     tok_rows = queries.shape[0]
     head_size = keys.shape[1]
     groups = queries.shape[1] // head_size
-    total_len = tok_rows * lax.axis_size("blk")
+    cores = lax.axis_size("core")
+    total_len = tok_rows * lax.axis_size("chip") * cores
     long_len = total_len - jnp.sum(lengths)
     shifted = jnp.concatenate([jnp.zeros((1,), jnp.int32), jnp.cumsum(lengths)[:-1]])
     starts = jnp.concatenate([jnp.zeros((1,), jnp.int32), long_len + shifted])
-    first_tok = lax.axis_index("blk") * tok_rows
+    blk_idx = lax.axis_index("chip") * cores + lax.axis_index("core")
+    first_tok = blk_idx * tok_rows
     query_idx = first_tok + jnp.arange(tok_rows)
     query_seg, query_off = locate(query_idx, starts)
     positions = query_idx - query_off
@@ -47,14 +51,16 @@
     rot_queries = rotate(queries.reshape(tok_rows, groups, head_size), positions).astype(
         jnp.bfloat16
     )
+    w_share = lax.all_gather(out_weight, "chip", axis=0, tiled=True)
     query_rows = jnp.transpose(rot_queries, (1, 0, 2)).reshape(groups * tok_rows, head_size)
     row_idx = jnp.tile(query_idx, groups)
     row_seg = jnp.tile(query_seg, groups)
     scale = 1.0 / head_size**0.5
-    row_count = groups * tok_rows
-    key_piece = lax.all_gather(rot_keys, "blk", axis=0, tiled=True)
-    value_piece = lax.all_gather(values, "blk", axis=0, tiled=True)
-    row_max = jnp.full((row_count,), -1e30, jnp.float32)
+    kv_pair = lax.all_gather(
+        jnp.concatenate([rot_keys, values], axis=1), BLK, axis=0, tiled=True
+    )
+    key_piece = kv_pair[:, :head_size]
+    value_piece = kv_pair[:, head_size:]
     span = key_piece.shape[0]
     key_idx = jnp.arange(span)
     key_seg, key_off = locate(key_idx, starts)
@@ -63,7 +69,7 @@
         jnp.einsum("rd,nd->rn", query_rows, key_piece, preferred_element_type=jnp.float32) * scale
     )
     scores = jnp.where(live, scores, -1e30)
-    new_max = jnp.maximum(row_max, jnp.max(scores, axis=1))
+    new_max = jnp.max(scores, axis=1)
     probs = jnp.where(live, jnp.exp(scores - new_max[:, None]), 0.0)
     new_sum = jnp.sum(probs, axis=1)
     new_weighted = jnp.dot(
@@ -73,21 +79,22 @@
     attended = jnp.transpose(attended.reshape(groups, tok_rows, head_size), (1, 0, 2)).reshape(
         tok_rows, groups * head_size
     )
+    chip_att = lax.all_gather(attended, "core", axis=0, tiled=True)
     terms = jnp.einsum(
-        "tk,nk->tn",
-        attended,
-        lax.all_gather(out_weight, "blk", axis=0, tiled=True),
-        preferred_element_type=jnp.float32,
-    )
-    hidden = lax.psum_scatter(terms.astype(jnp.bfloat16), "kv", scatter_dimension=1, tiled=True)
+        "tk,nk->tn", chip_att, w_share, preferred_element_type=jnp.float32
+    ).astype(jnp.bfloat16)
+    summed = lax.psum_scatter(terms, "kv", scatter_dimension=1, tiled=True)
+    hidden = lax.all_to_all(summed, "core", 0, 1, tiled=True)
     return (hidden, rot_keys)
 
 
 def solution(mesh):
+    kv_size, blk_size = mesh.devices.shape
+    sub = Mesh(mesh.devices.reshape(kv_size, blk_size // 2, 2), ("kv",) + BLK)
     return jax.shard_map(
         body,
-        mesh=mesh,
-        in_specs=(P("blk", "kv"), P("blk", "kv"), P("blk", "kv"), P(), P("blk", "kv")),
-        out_specs=(P("blk", "kv"), P("blk", "kv")),
+        mesh=sub,
+        in_specs=(P(BLK, "kv"), P(BLK, "kv"), P(BLK, "kv"), P(), P(BLK, "kv")),
+        out_specs=(P(BLK, "kv"), P(BLK, "kv")),
         check_vma=False,
     )

time: 83.5 us -> 87 us (1.042)
  waiting for transfers between devices: 37 us -> 41.4 us
  blocking collectives: 20.3 us -> 18.4 us
  other arithmetic: 4.53 us -> 5.94 us
  matrix products: 5.27 us -> 4.12 us
    all_gather x2, blocking collectives: 20.3 us -> 13.5 us  [the longest x1 11.6 us: body(): lax.all_gather(jnp.concatenate([rot_keys, values], axis=1), BLK, axis=0,...]
    all_gather x1, waiting for transfers between devices: 14 us -> 19.1 us  [body(): w_share = lax.all_gather(out_weight, 'chip', axis=0, tiled=True)]
    all_to_all x0 -> x1, blocking collectives: none -> 4.89 us  [body(): hidden = lax.all_to_all(summed, 'core', 0, 1, tiled=True)]
    dot_general x1, matrix products: 4.42 us -> 3.26 us  [body(): jnp.einsum('tk,nk->tn', chip_att, w_share, preferred_element_type=jnp.flo...]
  transfers between devices with their start and end apart: 2 -> 2, of which waited for: 2 -> 2; matrix products, arithmetic and copies ran while one was open for 8% -> 9% of each run, Pallas kernels for 0% -> 0%
where the time goes in v1:
time: 87 us; the launch traced here: 86.5 us
  waiting for transfers between devices  41.4 us (48%)
  blocking collectives  18.4 us (21%)
  between operations  14.8 us (17%)
  other arithmetic  5.94 us (7%)
  matrix products  4.12 us (5%)
  local copies, waits for them, and re-layouts  1.83 us (2%)
    reduce_scatter x1, waiting for transfers between devices, body(): summed = lax.psum_scatter(terms, 'kv', scatter_dimension=1, tiled=True)  21.6 us
    all_gather x1, waiting for transfers between devices, body(): w_share = lax.all_gather(out_weight, 'chip', axis=0, tiled=True)  19.1 us
    all_gather x1, blocking collectives, body(): lax.all_gather(jnp.concatenate([rot_keys, values], axis=1), BLK, axis=0,...  11.6 us
    all_to_all x1, blocking collectives, body(): hidden = lax.all_to_all(summed, 'core', 0, 1, tiled=True)  4.89 us
    dot_general x1, matrix products, body(): jnp.einsum('tk,nk->tn', chip_att, w_share, preferred_element_type=jnp.flo...  3.26 us
    all_gather x1, blocking collectives, body(): chip_att = lax.all_gather(attended, 'core', axis=0, tiled=True)  1.92 us
  transfers between devices with their start and end apart: 2, of which 2 were waited for; matrix products, arithmetic and copies ran while one was open for 9% of the time, Pallas kernels for 0%

profile of v1, /device:TPU:0, one launch (start us, length us, event | category | flops | bytes accessed | tf_op | source)
XLA Modules:
  0.0 86.5 jit_solution(13936938048549829163)
XLA Ops:
  7.2 0.7 all-gather.2.cloned.1.call-update
  7.9 1.3 %reduce_sum.36 = s32[]{:T(128)} reduce(s32[4]{0:T(128)} %param.8, s32[]{:T(128)} %constant.17.clone.1), dimensions={0}, to_apply=%region_0.0 | reduce | flops 3 | bytes 24 | tf_op jit(solution)/shard_map/reduce_sum | solution.py:38
  9.2 0.8 reduce-window.4
  10.1 0.9 %reshape.180 = bf16[80,4,128]{2,1,0:T(4,128)(2,1)S(1)} reshape(bf16[80,512]{1,0:T(8,128)(2,1)} %param.5) | data formatting | bytes 163840 | tf_op jit(solution)/shard_map/reshape | solution.py:51
  11.7 0.1 add_add_fusion
  11.8 0.1 fusion.27
  11.9 0.2 multiply_cosine_fusion.1
  12.2 0.2 fusion.12
  12.3 0.1 maximum_bitcast_fusion
  12.5 0.1 eq.16
  12.6 0.1 le.48
  12.7 1.0 %fusion.26 = (bf16[80,64]{1,0:T(8,128)(2,1)S(1)}, bf16[80,64]{1,0:T(8,128)(2,1)S(1)}) fusion(f32[64]{0:T(128)S(1)} %negate_power_fusion, f32[80]{0:T(128)S(1)} %get-tuple-element.12, bf16[80,1,128]{2,0,1:T(8,128)(2,1)} %bitcast.31), kind=kLoop, calls=%fused_computation.41 | loop fusion | flops 56320 | bytes 41536 | tf_op jit(solution)/shard_map/concatenate | solution.py:27
  13.7 0.8 pad_maximum_fusion
  14.5 11.6 %all_gather.9 = bf16[640,256]{1,0:T(8,128)(2,1)S(1)} all-gather(bf16[80,256]{1,0:T(8,128)(2,1)S(1)} %pad_maximum_fusion), channel_id=1, replica_groups=mesh['kv'=4,'chip'=4,'core'=2] {'chip','core'}, dimensions={0}, use_global_device_ids=true | all-gather | bytes 368640 | tf_op jit(solution)/shard_map/all_gather | solution.py:59
  26.2 0.4 fusion.30
  26.6 0.4 fusion.3
  27.1 0.4 fusion.1
  27.5 1.9 %all_gather.10 = bf16[160,512]{1,0:T(8,128)(2,1)S(1)} all-gather(bf16[80,512]{1,0:T(8,128)(2,1)S(1)} %bitcast.26), channel_id=1, replica_groups=mesh['kv'=4,'chip'=4,'core'=2] {'core'}, dimensions={0}, use_global_device_ids=true | all-gather | bytes 245760 | tf_op jit(solution)/shard_map/all_gather | solution.py:82
  29.5 19.1 %all-gather.2.cloned.1.call-done = bf16[2048,512]{1,0:T(8,128)(2,1)} async-done(((bf16[512,512]{1,0:T(8,128)(2,1)}), bf16[2048,512]{1,0:T(8,128)(2,1)}) %all-gather.2.cloned.1.call-update) | async-done | bytes 2097168 | tf_op jit(solution)/shard_map/all_gather | solution.py:54
  48.5 3.3 %convolution_convert_fusion = bf16[160,2048]{1,0:T(8,128)(2,1)} fusion(bf16[160,512]{1,0:T(8,128)(2,1)S(1)} %all_gather.10, bf16[2048,512]{1,0:T(8,128)(2,1)} %all-gather.2.cloned.1.call-done), kind=kOutput, calls=%fused_computation | convolution fusion | flops 335872000 | bytes 2916352 | tf_op jit(solution)/shard_map/tk,nk->tn/dot_general | solution.py:83
  51.8 0.7 pad_maximum_fusion.1
  52.5 21.6 %reduce-scatter.2.cloned.1.call-done = bf16[160,512]{1,0:T(8,128)(2,1)} async-done(((bf16[160,2048]{1,0:T(8,128)(2,1)}), bf16[160,512]{1,0:T(8,128)(2,1)}) %reduce-scatter.2.cloned.1.call-update) | async-done | bytes 163856 | tf_op jit(solution)/shard_map/reduce_scatter | solution.py:86
  74.1 4.9 %all_to_all.19 = bf16[2,80,512]{2,1,0:T(8,128)(2,1)S(1)} all-to-all(bf16[2,80,512]{2,1,0:T(8,128)(2,1)} %bitcast.27), channel_id=1, replica_groups=mesh['kv'=4,'chip'=4,'core'=2] {'core'}, dimensions={0} | all-to-all | bytes 327680 | tf_op jit(solution)/shard_map/all_to_all | solution.py:87
  79.0 0.7 copy.16
  (15 shorter events, 0.3 us)
Async XLA Ops:
  7.2 41.4 %all-gather.2.cloned.1.call-start = ((), (), s32[]{:S(2)}) async-start(), calls=%async_computation.2 | async-start | bytes 2621440 | tf_op jit(solution)/shard_map/all_gather | solution.py:54
  7.9 66.2 %reduce-scatter.2.cloned.1.call-start = ((), (), s32[]{:S(2)}) async-start(), calls=%async_computation.3 | async-start | bytes 819200 | tf_op jit(solution)/shard_map/reduce_scatter | solution.py:86
Sparse Core Ops, SparseCore 0:
  9.8 38.6 all-gather.1
  51.9 22.1 reduce-scatter.1

commit v2 on v1

--- a/solution.py
+++ b/solution.py
@@ -51,7 +51,19 @@
     rot_queries = rotate(queries.reshape(tok_rows, groups, head_size), positions).astype(
         jnp.bfloat16
     )
-    w_share = lax.all_gather(out_weight, "chip", axis=0, tiled=True)
+    chips = lax.axis_size("chip")
+    if chips <= 8:
+        held = [out_weight] + [
+            lax.ppermute(out_weight, "chip", [(i, (i + s) % chips) for i in range(chips)])
+            for s in range(1, chips)
+        ]
+        back = jnp.stack(held[::-1] + held[::-1], axis=0)
+        here = lax.axis_index("chip")
+        w_share = lax.dynamic_slice_in_dim(back, chips - 1 - here, chips, 0).reshape(
+            chips * out_weight.shape[0], out_weight.shape[1]
+        )
+    else:
+        w_share = lax.all_gather(out_weight, "chip", axis=0, tiled=True)
     query_rows = jnp.transpose(rot_queries, (1, 0, 2)).reshape(groups * tok_rows, head_size)
     row_idx = jnp.tile(query_idx, groups)
     row_seg = jnp.tile(query_seg, groups)
@@ -83,8 +95,22 @@
     terms = jnp.einsum(
         "tk,nk->tn", chip_att, w_share, preferred_element_type=jnp.float32
     ).astype(jnp.bfloat16)
-    summed = lax.psum_scatter(terms, "kv", scatter_dimension=1, tiled=True)
-    hidden = lax.all_to_all(summed, "core", 0, 1, tiled=True)
+    kvs = lax.axis_size("kv")
+    per_c = terms.shape[1] // kvs
+    routed = (
+        terms.reshape(cores, tok_rows, kvs, per_c)
+        .transpose(2, 0, 1, 3)
+        .reshape(kvs * cores, tok_rows, per_c)
+    )
+    got = lax.all_to_all(routed, ("kv", "core"), 0, 0, tiled=True)
+    total = jnp.sum(got.reshape(kvs, cores, tok_rows, per_c).astype(jnp.float32), axis=0)
+    rows = out_weight.shape[0]
+    hidden = (
+        total.reshape(cores, tok_rows, per_c // rows, rows)
+        .transpose(1, 2, 0, 3)
+        .reshape(tok_rows, cores * per_c)
+        .astype(jnp.bfloat16)
+    )
     return (hidden, rot_keys)
 
 

time: 87 us -> 63.7 us (0.73)
  waiting for transfers between devices: 41.4 us -> 17.5 us
  between operations: 14.8 us -> 1.48 us
  starting transfers between devices: 0.08 us -> 9.94 us
  blocking collectives: 18.4 us -> 22.8 us
  matrix products: 4.12 us -> 1.69 us
  local copies, waits for them, and re-layouts: 1.83 us -> 3.88 us
    reduce_scatter x1 -> x0, waiting for transfers between devices: 21.6 us -> none  [body(): summed = lax.psum_scatter(terms, 'kv', scatter_dimension=1, tiled=True)]
    all_gather x1 -> x0, waiting for transfers between devices: 19.1 us -> none  [body(): w_share = lax.all_gather(out_weight, 'chip', axis=0, tiled=True)]
    all_to_all x0 -> x1, waiting for transfers between devices: none -> 17.5 us  [body(): got = lax.all_to_all(routed, ('kv', 'core'), 0, 0, tiled=True)]
    all_gather x1, blocking collectives: 11.6 us -> 20.9 us  [body(): lax.all_gather(jnp.concatenate([rot_keys, values], axis=1), BLK, axis=0,...]
    ppermute x0 -> x3, starting transfers between devices: none -> 5.06 us  [body(): lax.ppermute(out_weight, 'chip', [(i, (i + s) % chips) for i in range(chi...]
    all_to_all x1 -> x0, blocking collectives: 4.89 us -> none  [body(): hidden = lax.all_to_all(summed, 'core', 0, 1, tiled=True)]
    all_to_all x0 -> x1, starting transfers between devices: none -> 4.88 us  [body(): got = lax.all_to_all(routed, ('kv', 'core'), 0, 0, tiled=True)]
    dot_general x1, matrix products: 3.26 us -> 0.83 us  [body(): jnp.einsum('tk,nk->tn', chip_att, w_share, preferred_element_type=jnp.flo...]
  transfers between devices with their start and end apart: 2 -> 4, of which waited for: 2 -> 1; matrix products, arithmetic and copies ran while one was open for 9% -> 13% of each run, Pallas kernels for 0% -> 0%
where the time goes in v2:
time: 63.7 us; the launch traced here: 63.3 us
  blocking collectives  22.8 us (36%)
  waiting for transfers between devices  17.5 us (27%)
  starting transfers between devices  9.94 us (16%)
  other arithmetic  6.03 us (9%)
  local copies, waits for them, and re-layouts  3.88 us (6%)
  matrix products  1.69 us (3%)
  between operations  1.48 us (2%)
    all_gather x1, blocking collectives, body(): lax.all_gather(jnp.concatenate([rot_keys, values], axis=1), BLK, axis=0,...  20.9 us
    all_to_all x1, waiting for transfers between devices, body(): got = lax.all_to_all(routed, ('kv', 'core'), 0, 0, tiled=True)  17.5 us
    ppermute x3, starting transfers between devices, body(): lax.ppermute(out_weight, 'chip', [(i, (i + s) % chips) for i in range(chi...  5.06 us
    all_to_all x1, starting transfers between devices, body(): got = lax.all_to_all(routed, ('kv', 'core'), 0, 0, tiled=True)  4.88 us
    all_gather x1, blocking collectives, body(): chip_att = lax.all_gather(attended, 'core', axis=0, tiled=True)  1.92 us
    concatenate x2, other arithmetic, rotate(): jnp.concatenate([first * cosine - second * sine, second * cosine + first...  1.72 us
    reshape x2, local copies, waits for them, and re-layouts, body(): terms.reshape(cores, tok_rows, kvs, per_c).transpose(2, 0, 1, 3)  1.43 us
    reduce_sum x1, other arithmetic, body(): long_len = total_len - jnp.sum(lengths)  1.3 us
  transfers between devices with their start and end apart: 4, of which 1 were waited for; matrix products, arithmetic and copies ran while one was open for 13% of the time, Pallas kernels for 0%

profile of v2, /device:TPU:0, one launch (start us, length us, event | category | flops | bytes accessed | tf_op | source)
XLA Modules:
  0.0 63.3 jit_solution(3589366204013891725)
XLA Ops:
  0.6 3.0 %collective-permute-start.1 = (bf16[512,512]{1,0:T(8,128)(2,1)}, bf16[512,512]{1,0:T(8,128)(2,1)S(1)}, u32[]{:S(2)}, u32[]{:S(2)}) collective-permute-start(bf16[512,512]{1,0:T(8,128)(2,1)} %param.9), channel_id=1, source_target_pairs={{0,4},{2,6},{4,0},{6,2},{1,5},{3,7},{5,1},{7,3},{8,12},{10,14},{12... | collective-permute-start | bytes 1572872 | tf_op jit(solution)/shard_map/ppermute | solution.py:57
  3.7 1.4 %collective-permute-start = (bf16[512,512]{1,0:T(8,128)(2,1)}, bf16[512,512]{1,0:T(8,128)(2,1)S(1)}, u32[]{:S(2)}, u32[]{:S(2)}) collective-permute-start(bf16[512,512]{1,0:T(8,128)(2,1)} %param.9), channel_id=1, source_target_pairs={{0,6},{2,0},{4,2},{6,4},{1,7},{3,1},{5,3},{7,5},{8,14},{10,8},{12,... | collective-permute-start | bytes 1572872 | tf_op jit(solution)/shard_map/ppermute | solution.py:57
  5.1 0.6 collective-permute-start.2
  5.7 1.3 %reduce_sum.45 = s32[]{:T(128)} reduce(s32[4]{0:T(128)} %param.8, s32[]{:T(128)} %constant.19.clone.1), dimensions={0}, to_apply=%region_0.0 | reduce | flops 3 | bytes 24 | tf_op jit(solution)/shard_map/reduce_sum | solution.py:38
  7.0 0.8 %reduce-window.4 = s32[4,1]{0,1:T(1,128)S(1)} reduce-window(s32[4,1]{0,1:T(1,128)} %bitcast.54, s32[]{:T(128)} %constant.19.clone.1), window={size=4x1 pad=3_0x0_0}, to_apply=%region_1.0 | reduce-window | flops 12 | bytes 36 | tf_op jit(solution)/shard_map/reduce-window
  9.0 0.2 multiply_cosine_fusion.1
  9.2 1.0 %fusion.26 = (bf16[80,64]{1,0:T(8,128)(2,1)S(1)}, bf16[80,64]{1,0:T(8,128)(2,1)S(1)}) fusion(f32[64]{0:T(128)S(1)} %negate_power_fusion, f32[80]{0:T(128)S(1)} %get-tuple-element.12, bf16[80,1,128]{2,0,1:T(8,128)(2,1)} %bitcast.53), kind=kLoop, calls=%fused_computation.49 | loop fusion | flops 56320 | bytes 41536 | tf_op jit(solution)/shard_map/concatenate | solution.py:27
  10.3 0.9 %reshape.193 = bf16[80,4,128]{2,1,0:T(4,128)(2,1)S(1)} reshape(bf16[80,512]{1,0:T(8,128)(2,1)} %param.5) | data formatting | bytes 163840 | tf_op jit(solution)/shard_map/reshape | solution.py:51
  11.2 0.2 fusion.12
  11.5 0.8 %pad_maximum_fusion = bf16[80,256]{1,0:T(8,128)(2,1)S(1)} fusion(bf16[80,128]{1,0:T(8,128)(2,1)} %param.7, bf16[80,64]{1,0:T(8,128)(2,1)S(1)} %get-tuple-element.7, bf16[80,64]{1,0:T(8,128)(2,1)S(1)} %get-tuple-element.6), kind=kLoop, calls=%fused_computation.47 | loop fusion | flops 122880 | bytes 81920 | tf_op jit(solution)/shard_map/concatenate | solution.py:72
  12.3 20.9 %all_gather.6 = bf16[640,256]{1,0:T(8,128)(2,1)S(1)} all-gather(bf16[80,256]{1,0:T(8,128)(2,1)S(1)} %pad_maximum_fusion), channel_id=1, replica_groups=mesh['kv'=4,'chip'=4,'core'=2] {'chip','core'}, dimensions={0}, use_global_device_ids=true | all-gather | bytes 368640 | tf_op jit(solution)/shard_map/all_gather | solution.py:71
  33.2 0.5 fusion.30
  33.7 0.4 fusion.3
  34.1 0.4 fusion.1
  34.6 1.9 %all_gather.7 = bf16[160,512]{1,0:T(8,128)(2,1)S(1)} all-gather(bf16[80,512]{1,0:T(8,128)(2,1)S(1)} %bitcast.49), channel_id=1, replica_groups=mesh['kv'=4,'chip'=4,'core'=2] {'core'}, dimensions={0}, use_global_device_ids=true | all-gather | bytes 245760 | tf_op jit(solution)/shard_map/all_gather | solution.py:94
  36.9 0.1 constant_dynamic-slice_fusion
  37.0 0.8 %convolution_convert_fusion = bf16[160,2048]{1,0:T(8,128)(2,1)S(1)} fusion(bf16[160,512]{1,0:T(8,128)(2,1)S(1)} %all_gather.7, bf16[2048,512]{1,0:T(8,128)(2,1)S(1)} %bitcast.44), kind=kOutput, calls=%fused_computation | convolution fusion | flops 335872000 | bytes 2916352 | tf_op jit(solution)/shard_map/tk,nk->tn/dot_general | solution.py:95
  37.9 0.5 reshape.199
  38.4 1.0 %copy.21 = bf16[2,80,4,512]{3,1,0,2:T(8,128)(2,1)} copy(bf16[2,80,4,512]{3,2,1,0:T(4,128)(2,1)S(1)} %reshape.199) | data formatting | bytes 1310720 | tf_op jit(solution)/shard_map/reshape | solution.py:101
  39.3 4.9 %all-to-all-start = ((bf16[8,80,512]{2,1,0:T(8,128)(2,1)}), bf16[8,80,512]{2,1,0:T(8,128)(2,1)S(1)}, u32[]{:S(2)}, u32[]{:S(2)}) async-start(bf16[8,80,512]{2,1,0:T(8,128)(2,1)} %bitcast.15), calls=%async_computation | async-start | bytes 1310720 | tf_op jit(solution)/shard_map/all_to_all | solution.py:105
  44.2 0.7 %pad_maximum_fusion.1 = bf16[80,128]{1,0:T(8,128)(2,1)} fusion(bf16[80,64]{1,0:T(8,128)(2,1)S(1)} %get-tuple-element.7, bf16[80,64]{1,0:T(8,128)(2,1)S(1)} %get-tuple-element.6), kind=kLoop, calls=%fused_computation.50 | loop fusion | flops 40960 | bytes 40960 | tf_op jit(solution)/shard_map/concatenate | solution.py:27
  44.9 17.5 %all-to-all-done = bf16[8,80,512]{2,1,0:T(8,128)(2,1)S(1)} async-done(((bf16[8,80,512]{2,1,0:T(8,128)(2,1)}), bf16[8,80,512]{2,1,0:T(8,128)(2,1)S(1)}, u32[]{:S(2)}, u32[]{:S(2)}) %all-to-all-start) | async-done | bytes 655392 | tf_op jit(solution)/shard_map/all_to_all | solution.py:105
  62.5 0.2 copy.22
  62.7 0.7 %copy.24 = bf16[10,8,2,512]{3,1,2,0:T(8,128)(2,1)} copy(bf16[10,8,2,512]{3,2,1,0:T(2,128)(2,1)S(1)} %bitcast.46) | data formatting | bytes 327680
  (31 shorter events, 1.1 us)
Async XLA Ops:
  0.6 35.9 %collective-permute-start.1 = (bf16[512,512]{1,0:T(8,128)(2,1)}, bf16[512,512]{1,0:T(8,128)(2,1)S(1)}, u32[]{:S(2)}, u32[]{:S(2)}) collective-permute-start(bf16[512,512]{1,0:T(8,128)(2,1)} %param.9), channel_id=1, source_target_pairs={{0,4},{2,6},{4,0},{6,2},{1,5},{3,7},{5,1},{7,3},{8,12},{10,14},{12... | collective-permute-start | bytes 1572872 | tf_op jit(solution)/shard_map/ppermute | solution.py:57
  3.7 32.9 %collective-permute-start = (bf16[512,512]{1,0:T(8,128)(2,1)}, bf16[512,512]{1,0:T(8,128)(2,1)S(1)}, u32[]{:S(2)}, u32[]{:S(2)}) collective-permute-start(bf16[512,512]{1,0:T(8,128)(2,1)} %param.9), channel_id=1, source_target_pairs={{0,6},{2,0},{4,2},{6,4},{1,7},{3,1},{5,3},{7,5},{8,14},{10,8},{12,... | collective-permute-start | bytes 1572872 | tf_op jit(solution)/shard_map/ppermute | solution.py:57
  5.1 31.5 %collective-permute-start.2 = (bf16[512,512]{1,0:T(8,128)(2,1)}, bf16[512,512]{1,0:T(8,128)(2,1)S(1)}, u32[]{:S(2)}, u32[]{:S(2)}) collective-permute-start(bf16[512,512]{1,0:T(8,128)(2,1)} %param.9), channel_id=1, source_target_pairs={{0,2},{2,4},{4,6},{6,0},{1,3},{3,5},{5,7},{7,1},{8,10},{10,12},{12... | collective-permute-start | bytes 1572872 | tf_op jit(solution)/shard_map/ppermute | solution.py:57
  33.2 3.4 %copy-start = (bf16[512,512]{1,0:T(8,128)(2,1)S(1)}, bf16[512,512]{1,0:T(8,128)(2,1)}, u32[]{:S(2)}) copy-start(bf16[512,512]{1,0:T(8,128)(2,1)} %param.9) | copy-start | bytes 1572868
  39.3 23.1 %all-to-all-start = ((bf16[8,80,512]{2,1,0:T(8,128)(2,1)}), bf16[8,80,512]{2,1,0:T(8,128)(2,1)S(1)}, u32[]{:S(2)}, u32[]{:S(2)}) async-start(bf16[8,80,512]{2,1,0:T(8,128)(2,1)} %bitcast.15), calls=%async_computation | async-start | bytes 1310720 | tf_op jit(solution)/shard_map/all_to_all | solution.py:105

commit v3 on v2

v3 whole, which is shorter than its diff:
```python
import jax
import jax.numpy as jnp
import numpy as np
from jax import lax
from jax.sharding import Mesh
from jax.sharding import PartitionSpec as P

rope_base = 500000.0
BLK = ("chip", "core")


def locate(index, starts):
    hit = starts[None, :] <= index[:, None]
    segment = jnp.sum(hit.astype(jnp.int32), axis=1) - 1
    offset = jnp.max(jnp.where(hit, starts[None, :], 0), axis=1)
    return (segment, offset)


def half_swap(width, head_size):
    half = head_size // 2
    col = np.arange(width)
    within = col % head_size
    src = np.where(within < half, col + half, col - half)
    sign = np.where(within < half, -1.0, 1.0)
    swap = np.zeros((width, width), np.float32)
    swap[src, col] = sign
    return jnp.asarray(swap, jnp.bfloat16)


def rotate_flat(field, positions, head_size):
    half = head_size // 2
    steps = jnp.arange(half).astype(jnp.float32) * (2.0 / head_size)
    inverse = jnp.power(jnp.float32(rope_base), -steps)
    angle = positions.astype(jnp.float32)[:, None] * inverse[None, :]
    reps = field.shape[1] // head_size
    cosine = jnp.tile(jnp.cos(angle), (1, 2 * reps))
    sine = jnp.tile(jnp.sin(angle), (1, 2 * reps))
    swapped = jnp.dot(
        field, half_swap(field.shape[1], head_size), preferred_element_type=jnp.float32
    )
    return field.astype(jnp.float32) * cosine + swapped * sine


def body(queries, keys, values, lengths, out_weight):
    tok_rows = queries.shape[0]
    head_size = keys.shape[1]
    groups = queries.shape[1] // head_size
    cores = lax.axis_size("core")
    chips = lax.axis_size("chip")
    total_len = tok_rows * chips * cores
    seg_id = jnp.arange(lengths.shape[0] + 1)[:, None]
    short_id = jnp.arange(lengths.shape[0])[None, :]
    tail = jnp.sum(jnp.where(short_id >= seg_id - 1, lengths[None, :], 0), axis=1)
    starts = jnp.where(seg_id[:, 0] == 0, 0, total_len - tail)
    blk_idx = lax.axis_index("chip") * cores + lax.axis_index("core")
    first_tok = blk_idx * tok_rows
    query_idx = first_tok + jnp.arange(tok_rows)
    query_seg, query_off = locate(query_idx, starts)
    positions = query_idx - query_off
    if chips <= 8:
        held = [out_weight] + [
            lax.ppermute(out_weight, "chip", [(i, (i + s) % chips) for i in range(chips)])
            for s in range(1, chips)
        ]
        back = jnp.stack(held[::-1] + held[::-1], axis=0)
        here = lax.axis_index("chip")
        w_share = lax.dynamic_slice_in_dim(back, chips - 1 - here, chips, 0).reshape(
            chips * out_weight.shape[0], out_weight.shape[1]
        )
    else:
        w_share = lax.all_gather(out_weight, "chip", axis=0, tiled=True)
    rot_keys = rotate_flat(keys, positions, head_size).astype(jnp.bfloat16)
    rot_queries = rotate_flat(queries, positions, head_size).astype(jnp.bfloat16)
    query_rows = jnp.concatenate(
        [rot_queries[:, h * head_size:(h + 1) * head_size] for h in range(groups)], axis=0
    )
    row_idx = jnp.tile(query_idx, groups)
    row_seg = jnp.tile(query_seg, groups)
    scale = 1.0 / head_size**0.5
    kv_pair = lax.all_gather(
        jnp.concatenate([rot_keys, values], axis=1), BLK, axis=0, tiled=True
    )
    key_piece = kv_pair[:, :head_size]
    value_piece = kv_pair[:, head_size:]
    span = key_piece.shape[0]
    key_idx = jnp.arange(span)
    key_seg, key_off = locate(key_idx, starts)
    live = (key_seg[None, :] == row_seg[:, None]) & (key_idx[None, :] <= row_idx[:, None])
    scores = (
        jnp.einsum("rd,nd->rn", query_rows, key_piece, preferred_element_type=jnp.float32) * scale
    )
    scores = jnp.where(live, scores, -1e30)
    new_max = jnp.max(scores, axis=1)
    probs = jnp.where(live, jnp.exp(scores - new_max[:, None]), 0.0)
    new_sum = jnp.sum(probs, axis=1)
    new_weighted = jnp.dot(
        probs.astype(jnp.bfloat16), value_piece, preferred_element_type=jnp.float32
    )
    att_rows = (new_weighted / new_sum[:, None]).astype(jnp.bfloat16)
    attended = jnp.concatenate(
        [att_rows[h * tok_rows:(h + 1) * tok_rows] for h in range(groups)], axis=1
    )
    chip_att = lax.all_gather(attended, "core", axis=0, tiled=True)
    kvs = lax.axis_size("kv")
    per_c = w_share.shape[0] // kvs
    routed = jnp.stack(
        [
            jnp.dot(
                chip_att,
                w_share[c * per_c:(c + 1) * per_c].T,
                preferred_element_type=jnp.float32,
            ).astype(jnp.bfloat16)
            for c in range(kvs)
        ],
        axis=0,
    ).reshape(kvs * cores, tok_rows, per_c)
    got = lax.all_to_all(routed, ("kv", "core"), 0, 0, tiled=True)
    total = jnp.sum(got.reshape(kvs, cores, tok_rows, per_c).astype(jnp.float32), axis=0)
    rows = out_weight.shape[0]
    hidden = (
        total.reshape(cores, tok_rows, per_c // rows, rows)
        .transpose(1, 2, 0, 3)
        .reshape(tok_rows, cores * per_c)
        .astype(jnp.bfloat16)
    )
    return (hidden, rot_keys)


def solution(mesh):
    kv_size, blk_size = mesh.devices.shape
    sub = Mesh(mesh.devices.reshape(kv_size, blk_size // 2, 2), ("kv",) + BLK)
    return jax.shard_map(
        body,
        mesh=sub,
        in_specs=(P(BLK, "kv"), P(BLK, "kv"), P(BLK, "kv"), P(), P(BLK, "kv")),
        out_specs=(P(BLK, "kv"), P(BLK, "kv")),
        check_vma=False,
    )
```

time: 63.7 us -> 62.6 us (0.983)
  blocking collectives: 22.8 us -> 47.4 us
  waiting for transfers between devices: 17.5 us -> 0.01 us
  starting transfers between devices: 9.94 us -> 5.04 us
  other arithmetic: 6.03 us -> 2.49 us
  matrix products: 1.69 us -> 4.37 us
  local copies, waits for them, and re-layouts: 3.88 us -> 1.98 us
    all_to_all x0 -> x1, blocking collectives: none -> 22.9 us  [body(): got = lax.all_to_all(routed, ('kv', 'core'), 0, 0, tiled=True)]
    all_to_all x1 -> x0, waiting for transfers between devices: 17.5 us -> none  [body(): got = lax.all_to_all(routed, ('kv', 'core'), 0, 0, tiled=True)]
    all_to_all x1 -> x0, starting transfers between devices: 4.88 us -> none  [body(): got = lax.all_to_all(routed, ('kv', 'core'), 0, 0, tiled=True)]
    dot_general x1 -> x6, matrix products: 0.83 us -> 3.52 us  [the longest x2 2.23 us: rotate_flat(): jnp.dot(field, half_swap(field.shape[1], head_size), preferred_element_ty...]
    reshape x4 -> x0, local copies, waits for them, and re-layouts: 2.38 us -> none  [the longest x2 1.43 us: body(): terms.reshape(cores, tok_rows, kvs, per_c).transpose(2, 0, 1, 3)]
    concatenate x3 -> x1, other arithmetic: 1.79 us -> 0.01 us  [body(): jnp.concatenate([att_rows[h * tok_rows:(h + 1) * tok_rows] for h in range...]
    all_gather x1, blocking collectives: 20.9 us -> 22.6 us  [body(): lax.all_gather(jnp.concatenate([rot_keys, values], axis=1), BLK, axis=0,...]
    another operation x2 -> x1, other arithmetic: 1 us -> 0.09 us  [body(): jnp.stack([jnp.dot(chip_att, w_share[c * per_c:(c + 1) * per_c].T, prefer...]
  transfers between devices with their start and end apart: 4 -> 3, of which waited for: 1 -> 0; matrix products, arithmetic and copies ran while one was open for 13% -> 10% of each run, Pallas kernels for 0% -> 0%
where the time goes in v3:
time: 62.6 us; the launch traced here: 62.2 us
  blocking collectives  47.4 us (76%)
  starting transfers between devices  5.04 us (8%)
  matrix products  4.37 us (7%)
  other arithmetic  2.49 us (4%)
  local copies, waits for them, and re-layouts  1.98 us (3%)
  between operations  0.92 us (1%)
    all_to_all x1, blocking collectives, body(): got = lax.all_to_all(routed, ('kv', 'core'), 0, 0, tiled=True)  22.9 us
    all_gather x1, blocking collectives, body(): lax.all_gather(jnp.concatenate([rot_keys, values], axis=1), BLK, axis=0,...  22.6 us
    ppermute x3, starting transfers between devices, body(): lax.ppermute(out_weight, 'chip', [(i, (i + s) % chips) for i in range(chi...  5.04 us
    dot_general x2, matrix products, rotate_flat(): jnp.dot(field, half_swap(field.shape[1], head_size), preferred_element_ty...  2.23 us
    all_gather x1, blocking collectives, body(): chip_att = lax.all_gather(attended, 'core', axis=0, tiled=True)  1.92 us
    dot_general x4, matrix products, body(): jnp.dot(chip_att, w_share[c * per_c:(c + 1) * per_c].T, preferred_element...  1.29 us
  transfers between devices with their start and end apart: 3, of which 0 were waited for; matrix products, arithmetic and copies ran while one was open for 10% of the time, Pallas kernels for 0%

profile of v3, /device:TPU:0, one launch (start us, length us, event | category | flops | bytes accessed | tf_op | source)
XLA Modules:
  0.0 62.2 jit_solution(2226417976945646501)
XLA Ops:
  0.6 3.9 %collective-permute-start = (bf16[512,512]{1,0:T(8,128)(2,1)}, bf16[512,512]{1,0:T(8,128)(2,1)S(1)}, u32[]{:S(2)}, u32[]{:S(2)}) collective-permute-start(bf16[512,512]{1,0:T(8,128)(2,1)} %param.11), channel_id=1, source_target_pairs={{0,6},{2,0},{4,2},{6,4},{1,7},{3,1},{5,3},{7,5},{8,14},{10,8},{12,... | collective-permute-start | bytes 1572872 | tf_op jit(solution)/shard_map/ppermute | solution.py:62
  4.6 0.5 collective-permute-start.1
  5.1 0.6 collective-permute-start.2
  5.7 0.7 %select_reduce_fusion = s32[5]{0:T(128)S(1)} fusion(s32[4]{0:T(128)} %param.10, s32[5]{0:T(128)S(1)} %iota_add_fusion.1), kind=kLoop, calls=%fused_computation.63 | loop fusion | flops 55 | bytes 56 | tf_op jit(solution)/shard_map/reduce_sum | solution.py:53
  6.6 0.2 multiply_cosine_fusion
  6.9 0.1 tile.23
  7.2 0.1 tile.25
  7.3 1.3 %fusion.8 = bf16[80,512]{1,0:T(8,128)(2,1)S(1)} fusion(f32[80,512]{1,0:T(8,128)S(1)} %tile.25, bf16[80,512]{1,0:T(8,128)(2,1)} %param.7, bf16[512,512]{1,0:T(8,128)(2,1)} %constant.48.clone, f32[80,512]{1,0:T(8,128)S(1)} %tile.23), kind=kOutput, calls=%fused_computation.15 | convolution fusion | flops 42147840 | bytes 1015808 | tf_op jit(solution)/shard_map/dot_general | solution.py:38
  8.8 0.9 %fusion.11 = bf16[80,128]{1,0:T(8,128)(2,1)S(1)} fusion(f32[80,128]{1,0:T(8,128)S(1)} %copy.25, bf16[80,128]{1,0:T(8,128)(2,1)} %param.8, bf16[128,128]{1,0:T(8,128)(2,1)} %constant.47.clone, f32[80,128]{1,0:T(8,128)S(1)} %copy.24), kind=kOutput, calls=%fused_computation.19 | convolution fusion | flops 2672640 | bytes 155648 | tf_op jit(solution)/shard_map/dot_general | solution.py:38
  9.8 0.7 %pad_maximum_fusion.2 = bf16[80,256]{1,0:T(8,128)(2,1)S(1)} fusion(bf16[80,128]{1,0:T(8,128)(2,1)} %param.9, bf16[80,128]{1,0:T(8,128)(2,1)S(1)} %fusion.11), kind=kLoop, calls=%fused_computation.55 | loop fusion | flops 81920 | bytes 81920 | tf_op jit(solution)/shard_map/concatenate | solution.py:81
  10.5 22.6 %all_gather.6 = bf16[640,256]{1,0:T(8,128)(2,1)S(1)} all-gather(bf16[80,256]{1,0:T(8,128)(2,1)S(1)} %pad_maximum_fusion.2), channel_id=1, replica_groups=mesh['kv'=4,'chip'=4,'core'=2] {'chip','core'}, dimensions={0}, use_global_device_ids=true | all-gather | bytes 368640 | tf_op jit(solution)/shard_map/all_gather | solution.py:80
  33.2 0.1 eq.24
  33.4 0.4 fusion.40
  33.8 0.4 fusion.13
  34.2 0.4 fusion.7
  34.7 1.9 %all_gather.7 = bf16[160,512]{1,0:T(8,128)(2,1)S(1)} all-gather(bf16[80,512]{1,0:T(8,128)(2,1)S(1)} %pad_maximum_fusion.1), channel_id=1, replica_groups=mesh['kv'=4,'chip'=4,'core'=2] {'core'}, dimensions={0}, use_global_device_ids=true | all-gather | bytes 245760 | tf_op jit(solution)/shard_map/all_gather | solution.py:103
  37.0 0.3 fusion.1
  37.3 0.3 fusion.2
  37.7 0.3 fusion.3
  38.0 0.3 fusion.4
  38.4 22.9 %all_to_all.5 = bf16[8,80,512]{2,1,0:T(8,128)(2,1)S(1)} all-to-all(bf16[8,80,512]{2,1,0:T(8,128)(2,1)S(1)} %bitcast.67), channel_id=1, replica_groups=mesh['kv'=4,'chip'=4,'core'=2] {'kv','core'}, dimensions={0} | all-to-all | bytes 1310720 | tf_op jit(solution)/shard_map/all_to_all | solution.py:117
  61.3 0.1 reduce
  61.4 0.2 copy.26
  61.5 0.7 %copy.27 = bf16[10,8,2,512]{3,1,2,0:T(8,128)(2,1)} copy(bf16[10,8,2,512]{3,2,1,0:T(2,128)(2,1)S(1)} %bitcast.69) | data formatting | bytes 327680
  (38 shorter events, 1.1 us)
Async XLA Ops:
  0.6 36.0 %collective-permute-start = (bf16[512,512]{1,0:T(8,128)(2,1)}, bf16[512,512]{1,0:T(8,128)(2,1)S(1)}, u32[]{:S(2)}, u32[]{:S(2)}) collective-permute-start(bf16[512,512]{1,0:T(8,128)(2,1)} %param.11), channel_id=1, source_target_pairs={{0,6},{2,0},{4,2},{6,4},{1,7},{3,1},{5,3},{7,5},{8,14},{10,8},{12,... | collective-permute-start | bytes 1572872 | tf_op jit(solution)/shard_map/ppermute | solution.py:62
  4.6 32.1 %collective-permute-start.1 = (bf16[512,512]{1,0:T(8,128)(2,1)}, bf16[512,512]{1,0:T(8,128)(2,1)S(1)}, u32[]{:S(2)}, u32[]{:S(2)}) collective-permute-start(bf16[512,512]{1,0:T(8,128)(2,1)} %param.11), channel_id=1, source_target_pairs={{0,4},{2,6},{4,0},{6,2},{1,5},{3,7},{5,1},{7,3},{8,12},{10,14},{12... | collective-permute-start | bytes 1572872 | tf_op jit(solution)/shard_map/ppermute | solution.py:62
  5.1 31.6 %collective-permute-start.2 = (bf16[512,512]{1,0:T(8,128)(2,1)}, bf16[512,512]{1,0:T(8,128)(2,1)S(1)}, u32[]{:S(2)}, u32[]{:S(2)}) collective-permute-start(bf16[512,512]{1,0:T(8,128)(2,1)} %param.11), channel_id=1, source_target_pairs={{0,2},{2,4},{4,6},{6,0},{1,3},{3,5},{5,7},{7,1},{8,10},{10,12},{12... | collective-permute-start | bytes 1572872 | tf_op jit(solution)/shard_map/ppermute | solution.py:62
  9.8 27.0 %copy-start.1 = (bf16[80,128]{1,0:T(8,128)(2,1)}, bf16[80,128]{1,0:T(8,128)(2,1)S(1)}, u32[]{:S(2)}) copy-start(bf16[80,128]{1,0:T(8,128)(2,1)S(1)} %fusion.11) | copy-start | bytes 61444
  33.4 3.4 %copy-start = (bf16[512,512]{1,0:T(8,128)(2,1)S(1)}, bf16[512,512]{1,0:T(8,128)(2,1)}, u32[]{:S(2)}) copy-start(bf16[512,512]{1,0:T(8,128)(2,1)} %param.11) | copy-start | bytes 1572868

commit v4 on v3

--- a/solution.py
+++ b/solution.py
@@ -71,15 +71,21 @@
         w_share = lax.all_gather(out_weight, "chip", axis=0, tiled=True)
     rot_keys = rotate_flat(keys, positions, head_size).astype(jnp.bfloat16)
     rot_queries = rotate_flat(queries, positions, head_size).astype(jnp.bfloat16)
+    width = queries.shape[1]
+    chip_rows = lax.all_gather(
+        jnp.concatenate([rot_queries, rot_keys, values], axis=1), "core", axis=0, tiled=True
+    )
+    kv_pair = lax.all_gather(chip_rows[:, width:], "chip", axis=0, tiled=True)
+    chip_q = chip_rows[:, :width]
+    chip_tok = cores * tok_rows
+    chip_idx = lax.axis_index("chip") * chip_tok + jnp.arange(chip_tok)
+    chip_seg, _ = locate(chip_idx, starts)
     query_rows = jnp.concatenate(
-        [rot_queries[:, h * head_size:(h + 1) * head_size] for h in range(groups)], axis=0
+        [chip_q[:, h * head_size:(h + 1) * head_size] for h in range(groups)], axis=0
     )
-    row_idx = jnp.tile(query_idx, groups)
-    row_seg = jnp.tile(query_seg, groups)
+    row_idx = jnp.tile(chip_idx, groups)
+    row_seg = jnp.tile(chip_seg, groups)
     scale = 1.0 / head_size**0.5
-    kv_pair = lax.all_gather(
-        jnp.concatenate([rot_keys, values], axis=1), BLK, axis=0, tiled=True
-    )
     key_piece = kv_pair[:, :head_size]
     value_piece = kv_pair[:, head_size:]
     span = key_piece.shape[0]
@@ -97,10 +103,9 @@
         probs.astype(jnp.bfloat16), value_piece, preferred_element_type=jnp.float32
     )
     att_rows = (new_weighted / new_sum[:, None]).astype(jnp.bfloat16)
-    attended = jnp.concatenate(
-        [att_rows[h * tok_rows:(h + 1) * tok_rows] for h in range(groups)], axis=1
+    chip_att = jnp.concatenate(
+        [att_rows[h * chip_tok:(h + 1) * chip_tok] for h in range(groups)], axis=1
     )
-    chip_att = lax.all_gather(attended, "core", axis=0, tiled=True)
     kvs = lax.axis_size("kv")
     per_c = w_share.shape[0] // kvs
     routed = jnp.stack(

time: 62.6 us -> 61.5 us (0.982)
  blocking collectives: 47.4 us -> 45.5 us
    all_gather x2, blocking collectives: 24.6 us -> 22.6 us  [the longest x1 20.7 us: body(): kv_pair = lax.all_gather(chip_rows[:, width:], 'chip', axis=0, tiled=True)]
  transfers between devices with their start and end apart: 3 -> 3, of which waited for: 0 -> 0; matrix products, arithmetic and copies ran while one was open for 10% -> 11% of each run, Pallas kernels for 0% -> 0%
where the time goes in v4:
time: 61.5 us; the launch traced here: 61.1 us
  blocking collectives  45.5 us (74%)
  starting transfers between devices  5.04 us (8%)
  matrix products  4.86 us (8%)
  other arithmetic  2.64 us (4%)
  local copies, waits for them, and re-layouts  2.09 us (3%)
  between operations  0.93 us (2%)
    all_to_all x1, blocking collectives, body(): got = lax.all_to_all(routed, ('kv', 'core'), 0, 0, tiled=True)  22.8 us
    all_gather x1, blocking collectives, body(): kv_pair = lax.all_gather(chip_rows[:, width:], 'chip', axis=0, tiled=True)  20.7 us
    ppermute x3, starting transfers between devices, body(): lax.ppermute(out_weight, 'chip', [(i, (i + s) % chips) for i in range(chi...  5.04 us
    dot_general x2, matrix products, rotate_flat(): jnp.dot(field, half_swap(field.shape[1], head_size), preferred_element_ty...  2.23 us
    all_gather x1, blocking collectives, body(): lax.all_gather(jnp.concatenate([rot_queries, rot_keys, values], axis=1),...  1.98 us
    dot_general x4, matrix products, body(): jnp.dot(chip_att, w_share[c * per_c:(c + 1) * per_c].T, preferred_element...  1.31 us
  transfers between devices with their start and end apart: 3, of which 0 were waited for; matrix products, arithmetic and copies ran while one was open for 11% of the time, Pallas kernels for 0%

profile of v4, /device:TPU:0, one launch (start us, length us, event | category | flops | bytes accessed | tf_op | source)
XLA Modules:
  0.0 61.1 jit_solution(15061374193546664423)
XLA Ops:
  0.6 3.9 %collective-permute-start = (bf16[512,512]{1,0:T(8,128)(2,1)}, bf16[512,512]{1,0:T(8,128)(2,1)S(1)}, u32[]{:S(2)}, u32[]{:S(2)}) collective-permute-start(bf16[512,512]{1,0:T(8,128)(2,1)} %param.11), channel_id=1, source_target_pairs={{0,6},{2,0},{4,2},{6,4},{1,7},{3,1},{5,3},{7,5},{8,14},{10,8},{12,... | collective-permute-start | bytes 1572872 | tf_op jit(solution)/shard_map/ppermute | solution.py:62
  4.6 0.5 collective-permute-start.1
  5.1 0.6 collective-permute-start.2
  5.7 0.7 %select_reduce_fusion.1 = s32[5]{0:T(128)S(1)} fusion(s32[4]{0:T(128)} %param.10, s32[5]{0:T(128)S(1)} %iota_add_fusion.2), kind=kLoop, calls=%fused_computation.56 | loop fusion | flops 55 | bytes 56 | tf_op jit(solution)/shard_map/reduce_sum | solution.py:53
  6.5 0.2 multiply_cosine_fusion
  7.1 0.1 tile.25
  7.3 0.1 tile.23
  7.4 0.9 %fusion.11 = bf16[80,128]{1,0:T(8,128)(2,1)S(1)} fusion(f32[80,128]{1,0:T(8,128)S(1)} %copy.25, bf16[80,128]{1,0:T(8,128)(2,1)} %param.8, bf16[128,128]{1,0:T(8,128)(2,1)} %constant.49.clone, f32[80,128]{1,0:T(8,128)S(1)} %copy.24), kind=kOutput, calls=%fused_computation.21 | convolution fusion | flops 2672640 | bytes 155648 | tf_op jit(solution)/shard_map/dot_general | solution.py:38
  8.4 1.3 %fusion.8 = bf16[80,512]{1,0:T(8,128)(2,1)S(1)} fusion(f32[80,512]{1,0:T(8,128)S(1)} %tile.25, bf16[80,512]{1,0:T(8,128)(2,1)} %param.7, bf16[512,512]{1,0:T(8,128)(2,1)} %constant.50.clone, f32[80,512]{1,0:T(8,128)S(1)} %tile.23), kind=kOutput, calls=%fused_computation.17 | convolution fusion | flops 42147840 | bytes 1015808 | tf_op jit(solution)/shard_map/dot_general | solution.py:38
  9.7 0.7 %pad_maximum_fusion.2 = bf16[80,768]{1,0:T(8,128)(2,1)S(1)} fusion(bf16[80,128]{1,0:T(8,128)(2,1)} %param.9, bf16[80,128]{1,0:T(8,128)(2,1)S(1)} %fusion.11, bf16[80,512]{1,0:T(8,128)(2,1)S(1)} %fusion.8), kind=kLoop, calls=%fused_computation.48 | loop fusion | flops 368640 | bytes 245760 | tf_op jit(solution)/shard_map/concatenate | solution.py:76
  10.4 2.0 %all_gather.6 = bf16[160,768]{1,0:T(8,128)(2,1)S(1)} all-gather(bf16[80,768]{1,0:T(8,128)(2,1)S(1)} %pad_maximum_fusion.2), channel_id=1, replica_groups=mesh['kv'=4,'chip'=4,'core'=2] {'core'}, dimensions={0}, use_global_device_ids=true | all-gather | bytes 368640 | tf_op jit(solution)/shard_map/all_gather | solution.py:75
  12.6 20.7 %all_gather.7 = bf16[640,256]{1,0:T(8,128)(2,1)S(1)} all-gather(bf16[160,256]{1,0:T(8,128)(2,1)S(1)} %slice.85), channel_id=1, replica_groups=mesh['kv'=4,'chip'=4,'core'=2] {'chip'}, dimensions={0}, use_global_device_ids=true | all-gather | bytes 409600 | tf_op jit(solution)/shard_map/all_gather | solution.py:78
  33.5 0.6 fusion.33
  34.1 0.5 fusion.12
  34.6 0.7 %fusion.1 = bf16[640,128]{1,0:T(8,128)(2,1)S(1)} fusion(f32[640,640]{0,1:T(8,128)S(1)} %get-tuple-element.13, f32[640]{0:T(1024)S(1)} %get-tuple-element.12, s32[640]{0:T(1024)S(1)} %le.61, s32[640]{0:T(1024)S(1)} %eq.24, s32[640]{0:T(1024)S(1)} %broadcast_add_fusion, bf16[640,256]{1,0:T(8,128)(2,1)S(1)} %all_gather.7, f32[640]{0:T(1024)S(1)} %fusion.12), kind=kOutput, calls=%fused_computation.9 | convolution fusion | flops 107479040 | bytes 1986560 | tf_op jit(solution)/shard_map/dot_general | solution.py:102
  35.5 0.1 copy-done
  35.8 0.3 fusion.2
  36.2 0.3 fusion.5
  36.5 0.3 fusion.4
  36.8 0.3 fusion.3
  37.3 22.8 %all_to_all.5 = bf16[8,80,512]{2,1,0:T(8,128)(2,1)S(1)} all-to-all(bf16[8,80,512]{2,1,0:T(8,128)(2,1)S(1)} %bitcast.63), channel_id=1, replica_groups=mesh['kv'=4,'chip'=4,'core'=2] {'kv','core'}, dimensions={0} | all-to-all | bytes 1310720 | tf_op jit(solution)/shard_map/all_to_all | solution.py:122
  60.1 0.1 reduce
  60.2 0.2 copy.26
  60.4 0.7 %copy.27 = bf16[10,8,2,512]{3,1,2,0:T(8,128)(2,1)} copy(bf16[10,8,2,512]{3,2,1,0:T(2,128)(2,1)S(1)} %bitcast.65) | data formatting | bytes 327680
  (41 shorter events, 1.3 us)
Async XLA Ops:
  0.6 34.7 %collective-permute-start = (bf16[512,512]{1,0:T(8,128)(2,1)}, bf16[512,512]{1,0:T(8,128)(2,1)S(1)}, u32[]{:S(2)}, u32[]{:S(2)}) collective-permute-start(bf16[512,512]{1,0:T(8,128)(2,1)} %param.11), channel_id=1, source_target_pairs={{0,6},{2,0},{4,2},{6,4},{1,7},{3,1},{5,3},{7,5},{8,14},{10,8},{12,... | collective-permute-start | bytes 1572872 | tf_op jit(solution)/shard_map/ppermute | solution.py:62
  4.6 30.8 %collective-permute-start.1 = (bf16[512,512]{1,0:T(8,128)(2,1)}, bf16[512,512]{1,0:T(8,128)(2,1)S(1)}, u32[]{:S(2)}, u32[]{:S(2)}) collective-permute-start(bf16[512,512]{1,0:T(8,128)(2,1)} %param.11), channel_id=1, source_target_pairs={{0,4},{2,6},{4,0},{6,2},{1,5},{3,7},{5,1},{7,3},{8,12},{10,14},{12... | collective-permute-start | bytes 1572872 | tf_op jit(solution)/shard_map/ppermute | solution.py:62
  5.1 30.4 %collective-permute-start.2 = (bf16[512,512]{1,0:T(8,128)(2,1)}, bf16[512,512]{1,0:T(8,128)(2,1)S(1)}, u32[]{:S(2)}, u32[]{:S(2)}) collective-permute-start(bf16[512,512]{1,0:T(8,128)(2,1)} %param.11), channel_id=1, source_target_pairs={{0,2},{2,4},{4,6},{6,0},{1,3},{3,5},{5,7},{7,1},{8,10},{10,12},{12... | collective-permute-start | bytes 1572872 | tf_op jit(solution)/shard_map/ppermute | solution.py:62
  8.4 26.9 %copy-start.1 = (bf16[80,128]{1,0:T(8,128)(2,1)}, bf16[80,128]{1,0:T(8,128)(2,1)S(1)}, u32[]{:S(2)}) copy-start(bf16[80,128]{1,0:T(8,128)(2,1)S(1)} %fusion.11) | copy-start | bytes 61444
  34.6 1.0 %copy-start = (bf16[512,512]{1,0:T(8,128)(2,1)S(1)}, bf16[512,512]{1,0:T(8,128)(2,1)}, u32[]{:S(2)}) copy-start(bf16[512,512]{1,0:T(8,128)(2,1)} %param.11) | copy-start | bytes 1572868

commit v5 on v4

--- a/solution.py
+++ b/solution.py
@@ -57,7 +57,15 @@
     query_idx = first_tok + jnp.arange(tok_rows)
     query_seg, query_off = locate(query_idx, starts)
     positions = query_idx - query_off
+    rot_keys = rotate_flat(keys, positions, head_size).astype(jnp.bfloat16)
+    rot_queries = rotate_flat(queries, positions, head_size).astype(jnp.bfloat16)
+    width = queries.shape[1]
+    chip_rows = lax.all_gather(
+        jnp.concatenate([rot_queries, rot_keys, values], axis=1), "core", axis=0, tiled=True
+    )
+    kv_pair = lax.all_gather(chip_rows[:, width:], "chip", axis=0, tiled=True)
     if chips <= 8:
+        out_weight, kv_pair = lax.optimization_barrier((out_weight, kv_pair))
         held = [out_weight] + [
             lax.ppermute(out_weight, "chip", [(i, (i + s) % chips) for i in range(chips)])
             for s in range(1, chips)
@@ -69,13 +77,6 @@
         )
     else:
         w_share = lax.all_gather(out_weight, "chip", axis=0, tiled=True)
-    rot_keys = rotate_flat(keys, positions, head_size).astype(jnp.bfloat16)
-    rot_queries = rotate_flat(queries, positions, head_size).astype(jnp.bfloat16)
-    width = queries.shape[1]
-    chip_rows = lax.all_gather(
-        jnp.concatenate([rot_queries, rot_keys, values], axis=1), "core", axis=0, tiled=True
-    )
-    kv_pair = lax.all_gather(chip_rows[:, width:], "chip", axis=0, tiled=True)
     chip_q = chip_rows[:, :width]
     chip_tok = cores * tok_rows
     chip_idx = lax.axis_index("chip") * chip_tok + jnp.arange(chip_tok)

time: 61.5 us -> 68.5 us (1.11)
  waiting for transfers between devices: 0.01 us -> 18.6 us
  blocking collectives: 45.5 us -> 35.5 us
  starting transfers between devices: 5.04 us -> 3.57 us
    ppermute x3, waiting for transfers between devices: 0.01 us -> 18.6 us  [body(): lax.ppermute(out_weight, 'chip', [(i, (i + s) % chips) for i in range(chi...]
    all_gather x1, blocking collectives: 20.7 us -> 10.6 us  [body(): kv_pair = lax.all_gather(chip_rows[:, width:], 'chip', axis=0, tiled=True)]
    ppermute x3, starting transfers between devices: 5.04 us -> 3.57 us  [body(): lax.ppermute(out_weight, 'chip', [(i, (i + s) % chips) for i in range(chi...]
  transfers between devices with their start and end apart: 3 -> 3, of which waited for: 0 -> 2; matrix products, arithmetic and copies ran while one was open for 11% -> 3% of each run, Pallas kernels for 0% -> 0%
where the time goes in v5:
time: 68.5 us; the launch traced here: 68.2 us
  blocking collectives  35.5 us (52%)
  waiting for transfers between devices  18.6 us (27%)
  matrix products  4.84 us (7%)
  starting transfers between devices  3.57 us (5%)
  other arithmetic  2.69 us (4%)
  local copies, waits for them, and re-layouts  2 us (3%)
  between operations  0.96 us (1%)
    all_to_all x1, blocking collectives, body(): got = lax.all_to_all(routed, ('kv', 'core'), 0, 0, tiled=True)  22.8 us
    ppermute x3, waiting for transfers between devices, body(): lax.ppermute(out_weight, 'chip', [(i, (i + s) % chips) for i in range(chi...  18.6 us
    all_gather x1, blocking collectives, body(): kv_pair = lax.all_gather(chip_rows[:, width:], 'chip', axis=0, tiled=True)  10.6 us
    ppermute x3, starting transfers between devices, body(): lax.ppermute(out_weight, 'chip', [(i, (i + s) % chips) for i in range(chi...  3.57 us
    dot_general x2, matrix products, rotate_flat(): jnp.dot(field, half_swap(field.shape[1], head_size), preferred_element_ty...  2.23 us
    all_gather x1, blocking collectives, body(): lax.all_gather(jnp.concatenate([rot_queries, rot_keys, values], axis=1),...  2.07 us
  transfers between devices with their start and end apart: 3, of which 2 were waited for; matrix products, arithmetic and copies ran while one was open for 3% of the time, Pallas kernels for 0%

profile of v5, /device:TPU:0, one launch (start us, length us, event | category | flops | bytes accessed | tf_op | source)
XLA Modules:
  0.0 68.2 jit_solution(4482903291360272790)
XLA Ops:
  0.7 0.8 %select_reduce_fusion.1 = s32[5]{0:T(128)S(1)} fusion(s32[4]{0:T(128)} %param.10, s32[5]{0:T(128)S(1)} %iota_add_fusion.2), kind=kLoop, calls=%fused_computation.56 | loop fusion | flops 55 | bytes 56 | tf_op jit(solution)/shard_map/reduce_sum | solution.py:53
  1.6 0.2 multiply_cosine_fusion
  2.2 0.1 tile.23
  2.4 0.1 tile.25
  2.5 0.9 %fusion.11 = bf16[80,128]{1,0:T(8,128)(2,1)S(1)} fusion(f32[80,128]{1,0:T(8,128)S(1)} %copy.25, bf16[80,128]{1,0:T(8,128)(2,1)} %param.8, bf16[128,128]{1,0:T(8,128)(2,1)} %constant.49.clone, f32[80,128]{1,0:T(8,128)S(1)} %copy.24), kind=kOutput, calls=%fused_computation.21 | convolution fusion | flops 2672640 | bytes 155648 | tf_op jit(solution)/shard_map/dot_general | solution.py:38
  3.5 1.3 %fusion.8 = bf16[80,512]{1,0:T(8,128)(2,1)S(1)} fusion(f32[80,512]{1,0:T(8,128)S(1)} %tile.25, bf16[80,512]{1,0:T(8,128)(2,1)} %param.7, bf16[512,512]{1,0:T(8,128)(2,1)} %constant.50.clone, f32[80,512]{1,0:T(8,128)S(1)} %tile.23), kind=kOutput, calls=%fused_computation.17 | convolution fusion | flops 42147840 | bytes 1015808 | tf_op jit(solution)/shard_map/dot_general | solution.py:38
  4.7 0.7 %pad_maximum_fusion.2 = bf16[80,768]{1,0:T(8,128)(2,1)S(1)} fusion(bf16[80,128]{1,0:T(8,128)(2,1)} %param.9, bf16[80,128]{1,0:T(8,128)(2,1)S(1)} %fusion.11, bf16[80,512]{1,0:T(8,128)(2,1)S(1)} %fusion.8), kind=kLoop, calls=%fused_computation.48 | loop fusion | flops 368640 | bytes 245760 | tf_op jit(solution)/shard_map/concatenate | solution.py:64
  5.5 2.1 %all_gather.6 = bf16[160,768]{1,0:T(8,128)(2,1)S(1)} all-gather(bf16[80,768]{1,0:T(8,128)(2,1)S(1)} %pad_maximum_fusion.2), channel_id=1, replica_groups=mesh['kv'=4,'chip'=4,'core'=2] {'core'}, dimensions={0}, use_global_device_ids=true | all-gather | bytes 368640 | tf_op jit(solution)/shard_map/all_gather | solution.py:63
  7.6 10.6 %all_gather.7 = bf16[640,256]{1,0:T(8,128)(2,1)S(1)} all-gather(bf16[160,256]{1,0:T(8,128)(2,1)S(1)} %slice.85), channel_id=1, replica_groups=mesh['kv'=4,'chip'=4,'core'=2] {'chip'}, dimensions={0}, use_global_device_ids=true | all-gather | bytes 409600 | tf_op jit(solution)/shard_map/all_gather | solution.py:66
  18.2 1.5 %collective-permute-start = (bf16[512,512]{1,0:T(8,128)(2,1)S(1)}, bf16[512,512]{1,0:T(8,128)(2,1)S(1)}, u32[]{:S(2)}, u32[]{:S(2)}) collective-permute-start(bf16[512,512]{1,0:T(8,128)(2,1)S(1)} %copy-done), channel_id=1, source_target_pairs={{0,6},{2,0},{4,2},{6,4},{1,7},{3,1},{5,3},{7,5},{8,14},{10,8},{12,... | collective-permute-start | bytes 1572872 | tf_op jit(solution)/shard_map/ppermute | solution.py:70
  19.7 1.5 %collective-permute-start.1 = (bf16[512,512]{1,0:T(8,128)(2,1)S(1)}, bf16[512,512]{1,0:T(8,128)(2,1)S(1)}, u32[]{:S(2)}, u32[]{:S(2)}) collective-permute-start(bf16[512,512]{1,0:T(8,128)(2,1)S(1)} %copy-done), channel_id=1, source_target_pairs={{0,4},{2,6},{4,0},{6,2},{1,5},{3,7},{5,1},{7,3},{8,12},{10,14},{12... | collective-permute-start | bytes 1572872 | tf_op jit(solution)/shard_map/ppermute | solution.py:70
  21.2 0.6 collective-permute-start.2
  22.2 0.6 fusion.33
  22.7 0.5 fusion.12
  23.2 0.7 %fusion.1 = bf16[640,128]{1,0:T(8,128)(2,1)S(1)} fusion(f32[640,640]{0,1:T(8,128)S(1)} %get-tuple-element.17, f32[640]{0:T(1024)S(1)} %get-tuple-element.16, s32[640]{0:T(1024)S(1)} %le.61, s32[640]{0:T(1024)S(1)} %eq.24, s32[640]{0:T(1024)S(1)} %broadcast_add_fusion, f32[640]{0:T(1024)S(1)} %fusion.12, bf16[640,256]{1,0:T(8,128)(2,1)S(1)} %all_gather.7), kind=kOutput, calls=%fused_computation.9 | convolution fusion | flops 107479040 | bytes 1986560 | tf_op jit(solution)/shard_map/dot_general | solution.py:103
  24.0 9.1 %collective-permute-done = bf16[512,512]{1,0:T(8,128)(2,1)S(1)} collective-permute-done((bf16[512,512]{1,0:T(8,128)(2,1)S(1)}, bf16[512,512]{1,0:T(8,128)(2,1)S(1)}, u32[]{:S(2)}, u32[]{:S(2)}) %collective-permute-start) | collective-permute-done | bytes 524320 | tf_op jit(solution)/shard_map/ppermute | solution.py:70
  33.1 9.5 %collective-permute-done.1 = bf16[512,512]{1,0:T(8,128)(2,1)S(1)} collective-permute-done((bf16[512,512]{1,0:T(8,128)(2,1)S(1)}, bf16[512,512]{1,0:T(8,128)(2,1)S(1)}, u32[]{:S(2)}, u32[]{:S(2)}) %collective-permute-start.1) | collective-permute-done | bytes 524320 | tf_op jit(solution)/shard_map/ppermute | solution.py:70
  42.9 0.3 fusion.2
  43.3 0.3 fusion.3
  43.6 0.3 fusion.4
  43.9 0.3 fusion.5
  44.4 22.8 %all_to_all.5 = bf16[8,80,512]{2,1,0:T(8,128)(2,1)S(1)} all-to-all(bf16[8,80,512]{2,1,0:T(8,128)(2,1)S(1)} %bitcast.63), channel_id=1, replica_groups=mesh['kv'=4,'chip'=4,'core'=2] {'kv','core'}, dimensions={0} | all-to-all | bytes 1310720 | tf_op jit(solution)/shard_map/all_to_all | solution.py:123
  67.3 0.2 copy.26
  67.5 0.7 %copy.27 = bf16[10,8,2,512]{3,1,2,0:T(8,128)(2,1)} copy(bf16[10,8,2,512]{3,2,1,0:T(2,128)(2,1)S(1)} %bitcast.65) | data formatting | bytes 327680
  (41 shorter events, 1.4 us)
Async XLA Ops:
  0.6 17.6 %copy-start = (bf16[512,512]{1,0:T(8,128)(2,1)S(1)}, bf16[512,512]{1,0:T(8,128)(2,1)}, u32[]{:S(2)}) copy-start(bf16[512,512]{1,0:T(8,128)(2,1)} %param.11) | copy-start | bytes 1572868
  3.4 20.5 %copy-start.1 = (bf16[80,128]{1,0:T(8,128)(2,1)}, bf16[80,128]{1,0:T(8,128)(2,1)S(1)}, u32[]{:S(2)}) copy-start(bf16[80,128]{1,0:T(8,128)(2,1)S(1)} %fusion.11) | copy-start | bytes 61444
  18.2 14.9 %collective-permute-start = (bf16[512,512]{1,0:T(8,128)(2,1)S(1)}, bf16[512,512]{1,0:T(8,128)(2,1)S(1)}, u32[]{:S(2)}, u32[]{:S(2)}) collective-permute-start(bf16[512,512]{1,0:T(8,128)(2,1)S(1)} %copy-done), channel_id=1, source_target_pairs={{0,6},{2,0},{4,2},{6,4},{1,7},{3,1},{5,3},{7,5},{8,14},{10,8},{12,... | collective-permute-start | bytes 1572872 | tf_op jit(solution)/shard_map/ppermute | solution.py:70
  19.7 22.9 %collective-permute-start.1 = (bf16[512,512]{1,0:T(8,128)(2,1)S(1)}, bf16[512,512]{1,0:T(8,128)(2,1)S(1)}, u32[]{:S(2)}, u32[]{:S(2)}) collective-permute-start(bf16[512,512]{1,0:T(8,128)(2,1)S(1)} %copy-done), channel_id=1, source_target_pairs={{0,4},{2,6},{4,0},{6,2},{1,5},{3,7},{5,1},{7,3},{8,12},{10,14},{12... | collective-permute-start | bytes 1572872 | tf_op jit(solution)/shard_map/ppermute | solution.py:70
  21.2 21.5 %collective-permute-start.2 = (bf16[512,512]{1,0:T(8,128)(2,1)S(1)}, bf16[512,512]{1,0:T(8,128)(2,1)S(1)}, u32[]{:S(2)}, u32[]{:S(2)}) collective-permute-start(bf16[512,512]{1,0:T(8,128)(2,1)S(1)} %copy-done), channel_id=1, source_target_pairs={{0,2},{2,4},{4,6},{6,0},{1,3},{3,5},{5,7},{7,1},{8,10},{10,12},{12... | collective-permute-start | bytes 1572872 | tf_op jit(solution)/shard_map/ppermute | solution.py:70

commit v6 on v4

--- a/solution.py
+++ b/solution.py
@@ -41,6 +41,35 @@
     return field.astype(jnp.float32) * cosine + swapped * sine
 
 
+def gather_share(piece, chips):
+    if chips > 8:
+        return lax.all_gather(piece, "chip", axis=0, tiled=True)
+    held = [piece] + [
+        lax.ppermute(piece, "chip", [(i, (i + s) % chips) for i in range(chips)])
+        for s in range(1, chips)
+    ]
+    back = jnp.stack(held[::-1] + held[::-1], axis=0)
+    here = lax.axis_index("chip")
+    return lax.dynamic_slice_in_dim(back, chips - 1 - here, chips, 0).reshape(
+        chips * piece.shape[0], piece.shape[1]
+    )
+
+
+def project(chip_att, share, kvs, cores, tok_rows):
+    per_c = share.shape[0] // kvs
+    routed = jnp.stack(
+        [
+            jnp.dot(
+                chip_att, share[c * per_c:(c + 1) * per_c].T, preferred_element_type=jnp.float32
+            ).astype(jnp.bfloat16)
+            for c in range(kvs)
+        ],
+        axis=0,
+    ).reshape(kvs * cores, tok_rows, per_c)
+    got = lax.all_to_all(routed, ("kv", "core"), 0, 0, tiled=True)
+    return jnp.sum(got.reshape(kvs, cores, tok_rows, per_c).astype(jnp.float32), axis=0)
+
+
 def body(queries, keys, values, lengths, out_weight):
     tok_rows = queries.shape[0]
     head_size = keys.shape[1]
@@ -57,18 +86,9 @@
     query_idx = first_tok + jnp.arange(tok_rows)
     query_seg, query_off = locate(query_idx, starts)
     positions = query_idx - query_off
-    if chips <= 8:
-        held = [out_weight] + [
-            lax.ppermute(out_weight, "chip", [(i, (i + s) % chips) for i in range(chips)])
-            for s in range(1, chips)
-        ]
-        back = jnp.stack(held[::-1] + held[::-1], axis=0)
-        here = lax.axis_index("chip")
-        w_share = lax.dynamic_slice_in_dim(back, chips - 1 - here, chips, 0).reshape(
-            chips * out_weight.shape[0], out_weight.shape[1]
-        )
-    else:
-        w_share = lax.all_gather(out_weight, "chip", axis=0, tiled=True)
+    rows = out_weight.shape[0]
+    half_rows = rows // 2
+    share_lo = gather_share(out_weight[:half_rows], chips)
     rot_keys = rotate_flat(keys, positions, head_size).astype(jnp.bfloat16)
     rot_queries = rotate_flat(queries, positions, head_size).astype(jnp.bfloat16)
     width = queries.shape[1]
@@ -76,6 +96,8 @@
         jnp.concatenate([rot_queries, rot_keys, values], axis=1), "core", axis=0, tiled=True
     )
     kv_pair = lax.all_gather(chip_rows[:, width:], "chip", axis=0, tiled=True)
+    late_w, kv_pair = lax.optimization_barrier((out_weight[half_rows:], kv_pair))
+    share_hi = gather_share(late_w, chips)
     chip_q = chip_rows[:, :width]
     chip_tok = cores * tok_rows
     chip_idx = lax.axis_index("chip") * chip_tok + jnp.arange(chip_tok)
@@ -107,25 +129,14 @@
         [att_rows[h * chip_tok:(h + 1) * chip_tok] for h in range(groups)], axis=1
     )
     kvs = lax.axis_size("kv")
-    per_c = w_share.shape[0] // kvs
-    routed = jnp.stack(
-        [
-            jnp.dot(
-                chip_att,
-                w_share[c * per_c:(c + 1) * per_c].T,
-                preferred_element_type=jnp.float32,
-            ).astype(jnp.bfloat16)
-            for c in range(kvs)
-        ],
-        axis=0,
-    ).reshape(kvs * cores, tok_rows, per_c)
-    got = lax.all_to_all(routed, ("kv", "core"), 0, 0, tiled=True)
-    total = jnp.sum(got.reshape(kvs, cores, tok_rows, per_c).astype(jnp.float32), axis=0)
-    rows = out_weight.shape[0]
+    parts = jnp.stack(
+        [project(chip_att, share, kvs, cores, tok_rows) for share in (share_lo, share_hi)], 0
+    )
+    per_c = parts.shape[-1]
     hidden = (
-        total.reshape(cores, tok_rows, per_c // rows, rows)
-        .transpose(1, 2, 0, 3)
-        .reshape(tok_rows, cores * per_c)
+        parts.reshape(2, cores, tok_rows, per_c // half_rows, half_rows)
+        .transpose(2, 3, 1, 0, 4)
+        .reshape(tok_rows, 2 * cores * per_c)
         .astype(jnp.bfloat16)
     )
     return (hidden, rot_keys)

time: 61.5 us -> 62.7 us (1.020)
  blocking collectives: 45.5 us -> 13.9 us
  waiting for transfers between devices: 0.01 us -> 20.2 us
  starting transfers between devices: 5.04 us -> 17 us
  matrix products: 4.86 us -> 3.59 us
  local copies, waits for them, and re-layouts: 2.09 us -> 3.24 us
  other arithmetic: 2.64 us -> 3.38 us
    all_to_all x1 -> x0, blocking collectives: 22.8 us -> none  [body(): got = lax.all_to_all(routed, ('kv', 'core'), 0, 0, tiled=True)]
    all_to_all x0 -> x2, waiting for transfers between devices: none -> 19.5 us  [project(): got = lax.all_to_all(routed, ('kv', 'core'), 0, 0, tiled=True)]
    all_gather x1, blocking collectives: 20.7 us -> 11.9 us  [body(): kv_pair = lax.all_gather(chip_rows[:, width:], 'chip', axis=0, tiled=True)]
    all_to_all x0 -> x2, starting transfers between devices: none -> 8.31 us  [project(): got = lax.all_to_all(routed, ('kv', 'core'), 0, 0, tiled=True)]
    ppermute x3 -> x6, starting transfers between devices: 5.04 us -> 8.64 us  [gather_share(): lax.ppermute(piece, 'chip', [(i, (i + s) % chips) for i in range(chips)])]
    dot_general x2, matrix products: 2.23 us -> 0.35 us  [rotate_flat(): jnp.dot(field, half_swap(field.shape[1], head_size), preferred_element_ty...]
    another operation x1 -> x2, other arithmetic: 0.09 us -> 1.53 us  [project(): jnp.stack([jnp.dot(chip_att, share[c * per_c:(c + 1) * per_c].T, preferre...]
    slice x0 -> x1, local copies, waits for them, and re-layouts: none -> 1.12 us  [body(): share_lo = gather_share(out_weight[:half_rows], chips)]
  transfers between devices with their start and end apart: 3 -> 8, of which waited for: 0 -> 3; matrix products, arithmetic and copies ran while one was open for 11% -> 13% of each run, Pallas kernels for 0% -> 0%
where the time goes in v6:
time: 62.7 us; the launch traced here: 62.4 us
  waiting for transfers between devices  20.2 us (32%)
  starting transfers between devices  17 us (27%)
  blocking collectives  13.9 us (22%)
  matrix products  3.59 us (6%)
  other arithmetic  3.38 us (5%)
  local copies, waits for them, and re-layouts  3.24 us (5%)
  between operations  1.15 us (2%)
    all_to_all x2, waiting for transfers between devices, project(): got = lax.all_to_all(routed, ('kv', 'core'), 0, 0, tiled=True)  19.5 us
    all_gather x1, blocking collectives, body(): kv_pair = lax.all_gather(chip_rows[:, width:], 'chip', axis=0, tiled=True)  11.9 us
    ppermute x6, starting transfers between devices, gather_share(): lax.ppermute(piece, 'chip', [(i, (i + s) % chips) for i in range(chips)])  8.64 us
    all_to_all x2, starting transfers between devices, project(): got = lax.all_to_all(routed, ('kv', 'core'), 0, 0, tiled=True)  8.31 us
    all_gather x1, blocking collectives, body(): lax.all_gather(jnp.concatenate([rot_queries, rot_keys, values], axis=1),...  1.98 us
    dot_general x8, matrix products, project(): jnp.dot(chip_att, share[c * per_c:(c + 1) * per_c].T, preferred_element_t...  1.92 us
    another operation x2, other arithmetic, project(): jnp.stack([jnp.dot(chip_att, share[c * per_c:(c + 1) * per_c].T, preferre...  1.53 us
  transfers between devices with their start and end apart: 8, of which 3 were waited for; matrix products, arithmetic and copies ran while one was open for 13% of the time, Pallas kernels for 0%

profile of v6, /device:TPU:0, one launch (start us, length us, event | category | flops | bytes accessed | tf_op | source)
XLA Modules:
  0.0 62.4 jit_solution(16943738902835022534)
XLA Ops:
  0.7 1.1 %fusion.39 = (bf16[256,512]{1,0:T(8,128)(2,1)S(1)}, bf16[256,512]{1,0:T(8,128)(2,1)S(1)}) fusion(bf16[512,512]{1,0:T(8,128)(2,1)} %param.11), kind=kLoop, calls=%fused_computation.97 | loop fusion | bytes 1048576 | tf_op jit(solution)/shard_map/slice | solution.py:91
  1.8 3.9 %collective-permute-start = (bf16[256,512]{1,0:T(8,128)(2,1)S(1)}, bf16[256,512]{1,0:T(8,128)(2,1)S(1)}, u32[]{:S(2)}, u32[]{:S(2)}) collective-permute-start(bf16[256,512]{1,0:T(8,128)(2,1)S(1)} %get-tuple-element.6), channel_id=1, source_target_pairs={{0,6},{2,0},{4,2},{6,4},{1,7},{3,1},{5,3},{7,5},{8,14},{10,8},{12,... | collective-permute-start | bytes 786440 | tf_op jit(solution)/shard_map/ppermute | solution.py:48
  5.8 0.5 collective-permute-start.1
  6.3 0.6 collective-permute-start.2
  6.9 0.7 %select_reduce_fusion.1 = s32[5]{0:T(128)S(1)} fusion(s32[4]{0:T(128)} %param.10, s32[5]{0:T(128)S(1)} %iota_add_fusion.2), kind=kLoop, calls=%fused_computation.78 | loop fusion | flops 55 | bytes 56 | tf_op jit(solution)/shard_map/reduce_sum | solution.py:82
  9.1 2.0 %all_gather.6 = bf16[160,768]{1,0:T(8,128)(2,1)S(1)} all-gather(bf16[80,768]{1,0:T(8,128)(2,1)S(1)} %pad_maximum_fusion.3), channel_id=1, replica_groups=mesh['kv'=4,'chip'=4,'core'=2] {'core'}, dimensions={0}, use_global_device_ids=true | all-gather | bytes 368640 | tf_op jit(solution)/shard_map/all_gather | solution.py:95
  11.1 11.9 %all_gather.7 = bf16[640,256]{1,0:T(8,128)(2,1)S(1)} all-gather(bf16[160,256]{1,0:T(8,128)(2,1)S(1)} %slice.125), channel_id=1, replica_groups=mesh['kv'=4,'chip'=4,'core'=2] {'chip'}, dimensions={0}, use_global_device_ids=true | all-gather | bytes 409600 | tf_op jit(solution)/shard_map/all_gather | solution.py:98
  22.9 1.5 %collective-permute-start.3 = (bf16[256,512]{1,0:T(8,128)(2,1)S(1)}, bf16[256,512]{1,0:T(8,128)(2,1)S(1)}, u32[]{:S(2)}, u32[]{:S(2)}) collective-permute-start(bf16[256,512]{1,0:T(8,128)(2,1)S(1)} %get-tuple-element.5), channel_id=1, source_target_pairs={{0,6},{2,0},{4,2},{6,4},{1,7},{3,1},{5,3},{7,5},{8,14},{10,8},{12,... | collective-permute-start | bytes 786440 | tf_op jit(solution)/shard_map/ppermute | solution.py:48
  24.4 1.5 %collective-permute-start.4 = (bf16[256,512]{1,0:T(8,128)(2,1)S(1)}, bf16[256,512]{1,0:T(8,128)(2,1)S(1)}, u32[]{:S(2)}, u32[]{:S(2)}) collective-permute-start(bf16[256,512]{1,0:T(8,128)(2,1)S(1)} %get-tuple-element.5), channel_id=1, source_target_pairs={{0,4},{2,6},{4,0},{6,2},{1,5},{3,7},{5,1},{7,3},{8,12},{10,14},{12... | collective-permute-start | bytes 786440 | tf_op jit(solution)/shard_map/ppermute | solution.py:48
  26.3 0.6 fusion.42
  26.9 0.5 fusion.16
  27.4 0.7 %fusion.1 = bf16[640,128]{1,0:T(8,128)(2,1)S(1)} fusion(f32[640,640]{0,1:T(8,128)S(1)} %get-tuple-element.19, f32[640]{0:T(1024)S(1)} %get-tuple-element.18, s32[640]{0:T(1024)S(1)} %le.61, s32[640]{0:T(1024)S(1)} %eq.24, s32[640]{0:T(1024)S(1)} %broadcast_add_fusion, f32[640]{0:T(1024)S(1)} %fusion.16, bf16[640,256]{1,0:T(8,128)(2,1)S(1)} %all_gather.7), kind=kOutput, calls=%fused_computation.5 | convolution fusion | flops 107479040 | bytes 1986560 | tf_op jit(solution)/shard_map/dot_general | solution.py:124
  28.2 0.6 collective-permute-start.5
  29.1 0.2 fusion.5
  29.3 0.2 fusion.6
  29.6 0.2 fusion.7
  30.1 0.8 %pad_maximum_fusion = bf16[4,160,256]{2,1,0:T(8,128)(2,1)} fusion(bf16[1,160,256]{2,1,0:T(8,128)(2,1)S(1)} %fusion.8, bf16[1,160,256]{2,1,0:T(8,128)(2,1)S(1)} %fusion.7, bf16[1,160,256]{2,1,0:T(8,128)(2,1)S(1)} %fusion.6, bf16[1,160,256]{2,1,0:T(8,128)(2,1)S(1)} %fusion.5), kind=kLoop, calls=%fused_computation.33 | loop fusion | flops 491520 | bytes 655360 | tf_op jit(solution)/shard_map/stack | solution.py:60
  30.8 4.9 %all-to-all-start = ((bf16[8,80,256]{2,1,0:T(8,128)(2,1)}), bf16[8,80,256]{2,1,0:T(8,128)(2,1)S(1)}, u32[]{:S(2)}, u32[]{:S(2)}) async-start(bf16[8,80,256]{2,1,0:T(8,128)(2,1)} %bitcast.16), calls=%async_computation | async-start | bytes 655360 | tf_op jit(solution)/shard_map/all_to_all | solution.py:69
  35.7 0.7 %collective-permute-done.4 = bf16[256,512]{1,0:T(8,128)(2,1)S(1)} collective-permute-done((bf16[256,512]{1,0:T(8,128)(2,1)S(1)}, bf16[256,512]{1,0:T(8,128)(2,1)S(1)}, u32[]{:S(2)}, u32[]{:S(2)}) %collective-permute-start.4) | collective-permute-done | bytes 262176 | tf_op jit(solution)/shard_map/ppermute | solution.py:48
  37.6 0.8 %pad_maximum_fusion.1 = bf16[4,160,256]{2,1,0:T(8,128)(2,1)} fusion(bf16[1,160,256]{2,1,0:T(8,128)(2,1)S(1)} %fusion.12, bf16[1,160,256]{2,1,0:T(8,128)(2,1)S(1)} %fusion.11, bf16[1,160,256]{2,1,0:T(8,128)(2,1)S(1)} %fusion.10, bf16[1,160,256]{2,1,0:T(8,128)(2,1)S(1)} %fusion.9), kind=kLoop, calls=%fused_computation.34 | loop fusion | flops 491520 | bytes 655360 | tf_op jit(solution)/shard_map/stack | solution.py:60
  38.3 8.5 %all-to-all-done = bf16[8,80,256]{2,1,0:T(8,128)(2,1)S(1)} async-done(((bf16[8,80,256]{2,1,0:T(8,128)(2,1)}), bf16[8,80,256]{2,1,0:T(8,128)(2,1)S(1)}, u32[]{:S(2)}, u32[]{:S(2)}) %all-to-all-start) | async-done | bytes 327712 | tf_op jit(solution)/shard_map/all_to_all | solution.py:69
  46.9 3.4 %all-to-all-start.1 = ((bf16[8,80,256]{2,1,0:T(8,128)(2,1)}), bf16[8,80,256]{2,1,0:T(8,128)(2,1)S(1)}, u32[]{:S(2)}, u32[]{:S(2)}) async-start(bf16[8,80,256]{2,1,0:T(8,128)(2,1)} %bitcast.31), calls=%async_computation.1 | async-start | bytes 655360 | tf_op jit(solution)/shard_map/all_to_all | solution.py:69
  50.4 11.0 %all-to-all-done.1 = bf16[8,80,256]{2,1,0:T(8,128)(2,1)S(1)} async-done(((bf16[8,80,256]{2,1,0:T(8,128)(2,1)}), bf16[8,80,256]{2,1,0:T(8,128)(2,1)S(1)}, u32[]{:S(2)}, u32[]{:S(2)}) %all-to-all-start.1) | async-done | bytes 327712 | tf_op jit(solution)/shard_map/all_to_all | solution.py:69
  61.6 0.8 %convert_element_type.110 = bf16[80,1024]{1,0:T(8,128)(2,1)} reshape(bf16[80,1,2,2,256]{4,3,2,0,1:T(2,128)(2,1)S(1)} %copy.22) | data formatting | bytes 327680 | tf_op jit(solution)/shard_map/convert_element_type | solution.py:140
  (76 shorter events, 3.5 us)
Async XLA Ops:
  0.6 8.0 %copy-start.4 = (bf16[128,128]{1,0:T(8,128)(2,1)S(1)}, bf16[128,128]{1,0:T(8,128)(2,1)}, u32[]{:S(2)}) copy-start(bf16[128,128]{1,0:T(8,128)(2,1)} %constant.49.clone) | copy-start | bytes 98308
  0.6 8.2 %copy-start.1 = (bf16[512,512]{1,0:T(8,128)(2,1)S(1)}, bf16[512,512]{1,0:T(8,128)(2,1)}, u32[]{:S(2)}) copy-start(bf16[512,512]{1,0:T(8,128)(2,1)} %constant.50.clone) | copy-start | bytes 1572868
  0.7 8.0 %copy-start.5 = (bf16[80,128]{1,0:T(8,128)(2,1)S(1)}, bf16[80,128]{1,0:T(8,128)(2,1)}, u32[]{:S(2)}) copy-start(bf16[80,128]{1,0:T(8,128)(2,1)} %param.8) | copy-start | bytes 61444
  0.7 8.1 %copy-start.3 = (bf16[80,512]{1,0:T(8,128)(2,1)S(1)}, bf16[80,512]{1,0:T(8,128)(2,1)}, u32[]{:S(2)}) copy-start(bf16[80,512]{1,0:T(8,128)(2,1)} %param.7) | copy-start | bytes 245764
  0.7 8.4 %copy-start.6 = (bf16[80,128]{1,0:T(8,128)(2,1)S(1)}, bf16[80,128]{1,0:T(8,128)(2,1)}, u32[]{:S(2)}) copy-start(bf16[80,128]{1,0:T(8,128)(2,1)} %param.9) | copy-start | bytes 61444
  1.8 26.4 %collective-permute-start = (bf16[256,512]{1,0:T(8,128)(2,1)S(1)}, bf16[256,512]{1,0:T(8,128)(2,1)S(1)}, u32[]{:S(2)}, u32[]{:S(2)}) collective-permute-start(bf16[256,512]{1,0:T(8,128)(2,1)S(1)} %get-tuple-element.6), channel_id=1, source_target_pairs={{0,6},{2,0},{4,2},{6,4},{1,7},{3,1},{5,3},{7,5},{8,14},{10,8},{12,... | collective-permute-start | bytes 786440 | tf_op jit(solution)/shard_map/ppermute | solution.py:48
  5.8 23.1 %collective-permute-start.1 = (bf16[256,512]{1,0:T(8,128)(2,1)S(1)}, bf16[256,512]{1,0:T(8,128)(2,1)S(1)}, u32[]{:S(2)}, u32[]{:S(2)}) collective-permute-start(bf16[256,512]{1,0:T(8,128)(2,1)S(1)} %get-tuple-element.6), channel_id=1, source_target_pairs={{0,4},{2,6},{4,0},{6,2},{1,5},{3,7},{5,1},{7,3},{8,12},{10,14},{12... | collective-permute-start | bytes 786440 | tf_op jit(solution)/shard_map/ppermute | solution.py:48
  6.3 22.6 %collective-permute-start.2 = (bf16[256,512]{1,0:T(8,128)(2,1)S(1)}, bf16[256,512]{1,0:T(8,128)(2,1)S(1)}, u32[]{:S(2)}, u32[]{:S(2)}) collective-permute-start(bf16[256,512]{1,0:T(8,128)(2,1)S(1)} %get-tuple-element.6), channel_id=1, source_target_pairs={{0,2},{2,4},{4,6},{6,0},{1,3},{3,5},{5,7},{7,1},{8,10},{10,12},{12... | collective-permute-start | bytes 786440 | tf_op jit(solution)/shard_map/ppermute | solution.py:48
  8.8 18.1 %copy-start.2 = (bf16[80,128]{1,0:T(8,128)(2,1)}, bf16[80,128]{1,0:T(8,128)(2,1)S(1)}, u32[]{:S(2)}) copy-start(bf16[80,128]{1,0:T(8,128)(2,1)S(1)} %fusion.15) | copy-start | bytes 61444
  22.9 12.8 %collective-permute-start.3 = (bf16[256,512]{1,0:T(8,128)(2,1)S(1)}, bf16[256,512]{1,0:T(8,128)(2,1)S(1)}, u32[]{:S(2)}, u32[]{:S(2)}) collective-permute-start(bf16[256,512]{1,0:T(8,128)(2,1)S(1)} %get-tuple-element.5), channel_id=1, source_target_pairs={{0,6},{2,0},{4,2},{6,4},{1,7},{3,1},{5,3},{7,5},{8,14},{10,8},{12,... | collective-permute-start | bytes 786440 | tf_op jit(solution)/shard_map/ppermute | solution.py:48
  24.4 12.0 %collective-permute-start.4 = (bf16[256,512]{1,0:T(8,128)(2,1)S(1)}, bf16[256,512]{1,0:T(8,128)(2,1)S(1)}, u32[]{:S(2)}, u32[]{:S(2)}) collective-permute-start(bf16[256,512]{1,0:T(8,128)(2,1)S(1)} %get-tuple-element.5), channel_id=1, source_target_pairs={{0,4},{2,6},{4,0},{6,2},{1,5},{3,7},{5,1},{7,3},{8,12},{10,14},{12... | collective-permute-start | bytes 786440 | tf_op jit(solution)/shard_map/ppermute | solution.py:48
  27.4 1.5 %copy-start = (bf16[512,512]{1,0:T(8,128)(2,1)S(1)}, bf16[512,512]{1,0:T(8,128)(2,1)}, u32[]{:S(2)}) copy-start(bf16[512,512]{1,0:T(8,128)(2,1)} %param.11) | copy-start | bytes 1572868
  28.2 8.2 %collective-permute-start.5 = (bf16[256,512]{1,0:T(8,128)(2,1)S(1)}, bf16[256,512]{1,0:T(8,128)(2,1)S(1)}, u32[]{:S(2)}, u32[]{:S(2)}) collective-permute-start(bf16[256,512]{1,0:T(8,128)(2,1)S(1)} %get-tuple-element.5), channel_id=1, source_target_pairs={{0,2},{2,4},{4,6},{6,0},{1,3},{3,5},{5,7},{7,1},{8,10},{10,12},{12... | collective-permute-start | bytes 786440 | tf_op jit(solution)/shard_map/ppermute | solution.py:48
  30.8 16.0 %all-to-all-start = ((bf16[8,80,256]{2,1,0:T(8,128)(2,1)}), bf16[8,80,256]{2,1,0:T(8,128)(2,1)S(1)}, u32[]{:S(2)}, u32[]{:S(2)}) async-start(bf16[8,80,256]{2,1,0:T(8,128)(2,1)} %bitcast.16), calls=%async_computation | async-start | bytes 655360 | tf_op jit(solution)/shard_map/all_to_all | solution.py:69
  46.9 14.5 %all-to-all-start.1 = ((bf16[8,80,256]{2,1,0:T(8,128)(2,1)}), bf16[8,80,256]{2,1,0:T(8,128)(2,1)S(1)}, u32[]{:S(2)}, u32[]{:S(2)}) async-start(bf16[8,80,256]{2,1,0:T(8,128)(2,1)} %bitcast.31), calls=%async_computation.1 | async-start | bytes 655360 | tf_op jit(solution)/shard_map/all_to_all | solution.py:69

commit v7 on v4

--- a/solution.py
+++ b/solution.py
@@ -75,7 +75,20 @@
     chip_rows = lax.all_gather(
         jnp.concatenate([rot_queries, rot_keys, values], axis=1), "core", axis=0, tiled=True
     )
-    kv_pair = lax.all_gather(chip_rows[:, width:], "chip", axis=0, tiled=True)
+    chip_kv = chip_rows[:, width:]
+    if chips <= 8:
+        kv_pair = jnp.concatenate(
+            [chip_kv]
+            + [
+                lax.ppermute(chip_kv, "chip", [(i, (i + s) % chips) for i in range(chips)])
+                for s in range(1, chips)
+            ],
+            axis=0,
+        )
+        src_chip = (lax.axis_index("chip") - jnp.arange(chips)) % chips
+    else:
+        kv_pair = lax.all_gather(chip_kv, "chip", axis=0, tiled=True)
+        src_chip = jnp.arange(chips)
     chip_q = chip_rows[:, :width]
     chip_tok = cores * tok_rows
     chip_idx = lax.axis_index("chip") * chip_tok + jnp.arange(chip_tok)
@@ -89,7 +102,8 @@
     key_piece = kv_pair[:, :head_size]
     value_piece = kv_pair[:, head_size:]
     span = key_piece.shape[0]
-    key_idx = jnp.arange(span)
+    chip_tok_kv = chip_kv.shape[0]
+    key_idx = (src_chip[:, None] * chip_tok_kv + jnp.arange(chip_tok_kv)[None, :]).reshape(span)
     key_seg, key_off = locate(key_idx, starts)
     live = (key_seg[None, :] == row_seg[:, None]) & (key_idx[None, :] <= row_idx[:, None])
     scores = (

time: 61.5 us -> 60.7 us (0.987)
  blocking collectives: 45.5 us -> 24.8 us
  waiting for transfers between devices: 0.01 us -> 14.5 us
  starting transfers between devices: 5.04 us -> 10.5 us
    all_gather x1 -> x0, blocking collectives: 20.7 us -> none  [body(): kv_pair = lax.all_gather(chip_rows[:, width:], 'chip', axis=0, tiled=True)]
    ppermute x0 -> x3, waiting for transfers between devices: none -> 14.4 us  [body(): lax.ppermute(chip_kv, 'chip', [(i, (i + s) % chips) for i in range(chips)])]
    ppermute x0 -> x3, starting transfers between devices: none -> 3.59 us  [body(): lax.ppermute(chip_kv, 'chip', [(i, (i + s) % chips) for i in range(chips)])]
    ppermute x3, starting transfers between devices: 5.04 us -> 6.9 us  [body(): lax.ppermute(out_weight, 'chip', [(i, (i + s) % chips) for i in range(chi...]
  transfers between devices with their start and end apart: 3 -> 6, of which waited for: 0 -> 2; matrix products, arithmetic and copies ran while one was open for 11% -> 12% of each run, Pallas kernels for 0% -> 0%
where the time goes in v7:
time: 60.7 us; the launch traced here: 60.3 us
  blocking collectives  24.8 us (41%)
  waiting for transfers between devices  14.5 us (24%)
  starting transfers between devices  10.5 us (17%)
  matrix products  4.79 us (8%)
  other arithmetic  2.72 us (4%)
  local copies, waits for them, and re-layouts  2.08 us (3%)
  between operations  0.97 us (2%)
    all_to_all x1, blocking collectives, body(): got = lax.all_to_all(routed, ('kv', 'core'), 0, 0, tiled=True)  22.8 us
    ppermute x3, waiting for transfers between devices, body(): lax.ppermute(chip_kv, 'chip', [(i, (i + s) % chips) for i in range(chips)])  14.4 us
    ppermute x3, starting transfers between devices, body(): lax.ppermute(out_weight, 'chip', [(i, (i + s) % chips) for i in range(chi...  6.9 us
    ppermute x3, starting transfers between devices, body(): lax.ppermute(chip_kv, 'chip', [(i, (i + s) % chips) for i in range(chips)])  3.59 us
    dot_general x2, matrix products, rotate_flat(): jnp.dot(field, half_swap(field.shape[1], head_size), preferred_element_ty...  2.23 us
    all_gather x1, blocking collectives, body(): lax.all_gather(jnp.concatenate([rot_queries, rot_keys, values], axis=1),...  1.98 us
    dot_general x4, matrix products, body(): jnp.dot(chip_att, w_share[c * per_c:(c + 1) * per_c].T, preferred_element...  1.32 us
  transfers between devices with their start and end apart: 6, of which 2 were waited for; matrix products, arithmetic and copies ran while one was open for 12% of the time, Pallas kernels for 0%

profile of v7, /device:TPU:0, one launch (start us, length us, event | category | flops | bytes accessed | tf_op | source)
XLA Modules:
  0.0 60.3 jit_solution(17252683101599315602)
XLA Ops:
  0.6 3.9 %collective-permute-start.3 = (bf16[512,512]{1,0:T(8,128)(2,1)}, bf16[512,512]{1,0:T(8,128)(2,1)S(1)}, u32[]{:S(2)}, u32[]{:S(2)}) collective-permute-start(bf16[512,512]{1,0:T(8,128)(2,1)} %param.11), channel_id=1, source_target_pairs={{0,6},{2,0},{4,2},{6,4},{1,7},{3,1},{5,3},{7,5},{8,14},{10,8},{12,... | collective-permute-start | bytes 1572872 | tf_op jit(solution)/shard_map/ppermute | solution.py:62
  4.6 0.5 collective-permute-start.4
  5.1 0.7 %select_reduce_fusion.1 = s32[5]{0:T(128)S(1)} fusion(s32[4]{0:T(128)} %param.10, s32[5]{0:T(128)S(1)} %iota_add_fusion.3), kind=kLoop, calls=%fused_computation.59 | loop fusion | flops 55 | bytes 56 | tf_op jit(solution)/shard_map/reduce_sum | solution.py:53
  6.0 0.2 multiply_cosine_fusion
  6.6 0.1 tile.25
  6.9 0.9 %fusion.10 = bf16[80,128]{1,0:T(8,128)(2,1)S(1)} fusion(f32[80,128]{1,0:T(8,128)S(1)} %copy.25, bf16[80,128]{1,0:T(8,128)(2,1)} %param.8, bf16[128,128]{1,0:T(8,128)(2,1)} %constant.63.clone, f32[80,128]{1,0:T(8,128)S(1)} %copy.24), kind=kOutput, calls=%fused_computation.20 | convolution fusion | flops 2672640 | bytes 155648 | tf_op jit(solution)/shard_map/dot_general | solution.py:38
  7.8 1.3 %fusion.7 = bf16[80,512]{1,0:T(8,128)(2,1)S(1)} fusion(f32[80,512]{1,0:T(8,128)S(1)} %tile.25, bf16[80,512]{1,0:T(8,128)(2,1)} %param.7, bf16[512,512]{1,0:T(8,128)(2,1)} %constant.64.clone, f32[80,512]{1,0:T(8,128)S(1)} %tile.23), kind=kOutput, calls=%fused_computation.16 | convolution fusion | flops 42147840 | bytes 1015808 | tf_op jit(solution)/shard_map/dot_general | solution.py:38
  9.1 0.7 %pad_maximum_fusion.3 = bf16[80,768]{1,0:T(8,128)(2,1)S(1)} fusion(bf16[80,128]{1,0:T(8,128)(2,1)} %param.9, bf16[80,128]{1,0:T(8,128)(2,1)S(1)} %fusion.10, bf16[80,512]{1,0:T(8,128)(2,1)S(1)} %fusion.7), kind=kLoop, calls=%fused_computation.49 | loop fusion | flops 368640 | bytes 245760 | tf_op jit(solution)/shard_map/concatenate | solution.py:76
  9.9 2.0 %all_gather.3 = bf16[160,768]{1,0:T(8,128)(2,1)S(1)} all-gather(bf16[80,768]{1,0:T(8,128)(2,1)S(1)} %pad_maximum_fusion.3), channel_id=1, replica_groups=mesh['kv'=4,'chip'=4,'core'=2] {'core'}, dimensions={0}, use_global_device_ids=true | all-gather | bytes 368640 | tf_op jit(solution)/shard_map/all_gather | solution.py:75
  12.0 2.0 %collective-permute-start.1 = (bf16[160,256]{1,0:T(8,128)(2,1)S(1)}, bf16[160,256]{1,0:T(8,128)(2,1)S(1)}, u32[]{:S(2)}, u32[]{:S(2)}) collective-permute-start(bf16[160,256]{1,0:T(8,128)(2,1)S(1)} %slice.85), channel_id=1, source_target_pairs={{0,4},{2,6},{4,0},{6,2},{1,5},{3,7},{5,1},{7,3},{8,12},{10,14},{12... | collective-permute-start | bytes 245768 | tf_op jit(solution)/shard_map/ppermute | solution.py:83
  14.0 1.5 %collective-permute-start = (bf16[160,256]{1,0:T(8,128)(2,1)S(1)}, bf16[160,256]{1,0:T(8,128)(2,1)S(1)}, u32[]{:S(2)}, u32[]{:S(2)}) collective-permute-start(bf16[160,256]{1,0:T(8,128)(2,1)S(1)} %slice.85), channel_id=1, source_target_pairs={{0,2},{2,4},{4,6},{6,0},{1,3},{3,5},{5,7},{7,1},{8,10},{10,12},{12... | collective-permute-start | bytes 245768 | tf_op jit(solution)/shard_map/ppermute | solution.py:83
  16.0 2.6 %collective-permute-done.2 = bf16[160,256]{1,0:T(8,128)(2,1)S(1)} collective-permute-done((bf16[160,256]{1,0:T(8,128)(2,1)S(1)}, bf16[160,256]{1,0:T(8,128)(2,1)S(1)}, u32[]{:S(2)}, u32[]{:S(2)}) %collective-permute-start.2) | collective-permute-done | bytes 81952 | tf_op jit(solution)/shard_map/ppermute | solution.py:83
  18.7 2.4 %collective-permute-start.5 = (bf16[512,512]{1,0:T(8,128)(2,1)S(1)}, bf16[512,512]{1,0:T(8,128)(2,1)S(1)}, u32[]{:S(2)}, u32[]{:S(2)}) collective-permute-start(bf16[512,512]{1,0:T(8,128)(2,1)S(1)} %copy-done), channel_id=1, source_target_pairs={{0,2},{2,4},{4,6},{6,0},{1,3},{3,5},{5,7},{7,1},{8,10},{10,12},{12... | collective-permute-start | bytes 1572872 | tf_op jit(solution)/shard_map/ppermute | solution.py:62
  21.1 11.8 %collective-permute-done.1 = bf16[160,256]{1,0:T(8,128)(2,1)S(1)} collective-permute-done((bf16[160,256]{1,0:T(8,128)(2,1)S(1)}, bf16[160,256]{1,0:T(8,128)(2,1)S(1)}, u32[]{:S(2)}, u32[]{:S(2)}) %collective-permute-start.1) | collective-permute-done | bytes 81952 | tf_op jit(solution)/shard_map/ppermute | solution.py:83
  33.0 0.6 fusion.35
  33.5 0.5 fusion.11
  34.0 0.7 %fusion = bf16[640,128]{1,0:T(8,128)(2,1)S(1)} fusion(f32[640,640]{0,1:T(8,128)S(1)} %get-tuple-element.13, f32[640]{0:T(1024)S(1)} %get-tuple-element.12, s32[640]{0:T(1024)S(1)} %le.61, s32[640]{0:T(1024)S(1)} %eq.26, s32[640]{0:T(1024)S(1)} %add.94, s32[640]{0:T(1024)S(1)} %broadcast_add_fusion, bf16[640,256]{1,0:T(8,128)(2,1)S(1)} %pad_maximum_fusion.1, ...), kind=kOutput, calls=%fused_computation.8 | convolution fusion | flops 107479040 | bytes 1990656 | tf_op jit(solution)/shard_map/dot_general | solution.py:116
  35.1 0.3 fusion.1
  35.4 0.3 fusion.4
  35.8 0.3 fusion.3
  36.1 0.3 fusion.2
  36.5 22.8 %all_to_all.5 = bf16[8,80,512]{2,1,0:T(8,128)(2,1)S(1)} all-to-all(bf16[8,80,512]{2,1,0:T(8,128)(2,1)S(1)} %bitcast.63), channel_id=1, replica_groups=mesh['kv'=4,'chip'=4,'core'=2] {'kv','core'}, dimensions={0} | all-to-all | bytes 1310720 | tf_op jit(solution)/shard_map/all_to_all | solution.py:136
  59.5 0.2 copy.26
  59.7 0.7 %copy.27 = bf16[10,8,2,512]{3,1,2,0:T(8,128)(2,1)} copy(bf16[10,8,2,512]{3,2,1,0:T(2,128)(2,1)S(1)} %bitcast.65) | data formatting | bytes 327680
  (50 shorter events, 1.8 us)
Async XLA Ops:
  0.6 18.0 %copy-start = (bf16[512,512]{1,0:T(8,128)(2,1)S(1)}, bf16[512,512]{1,0:T(8,128)(2,1)}, u32[]{:S(2)}) copy-start(bf16[512,512]{1,0:T(8,128)(2,1)} %param.11) | copy-start | bytes 1572868
  0.6 34.1 %collective-permute-start.3 = (bf16[512,512]{1,0:T(8,128)(2,1)}, bf16[512,512]{1,0:T(8,128)(2,1)S(1)}, u32[]{:S(2)}, u32[]{:S(2)}) collective-permute-start(bf16[512,512]{1,0:T(8,128)(2,1)} %param.11), channel_id=1, source_target_pairs={{0,6},{2,0},{4,2},{6,4},{1,7},{3,1},{5,3},{7,5},{8,14},{10,8},{12,... | collective-permute-start | bytes 1572872 | tf_op jit(solution)/shard_map/ppermute | solution.py:62
  4.6 30.2 %collective-permute-start.4 = (bf16[512,512]{1,0:T(8,128)(2,1)}, bf16[512,512]{1,0:T(8,128)(2,1)S(1)}, u32[]{:S(2)}, u32[]{:S(2)}) collective-permute-start(bf16[512,512]{1,0:T(8,128)(2,1)} %param.11), channel_id=1, source_target_pairs={{0,4},{2,6},{4,0},{6,2},{1,5},{3,7},{5,1},{7,3},{8,12},{10,14},{12... | collective-permute-start | bytes 1572872 | tf_op jit(solution)/shard_map/ppermute | solution.py:62
  7.8 26.9 %copy-start.1 = (bf16[80,128]{1,0:T(8,128)(2,1)}, bf16[80,128]{1,0:T(8,128)(2,1)S(1)}, u32[]{:S(2)}) copy-start(bf16[80,128]{1,0:T(8,128)(2,1)S(1)} %fusion.10) | copy-start | bytes 61444
  11.9 6.8 %collective-permute-start.2 = (bf16[160,256]{1,0:T(8,128)(2,1)S(1)}, bf16[160,256]{1,0:T(8,128)(2,1)S(1)}, u32[]{:S(2)}, u32[]{:S(2)}) collective-permute-start(bf16[160,256]{1,0:T(8,128)(2,1)S(1)} %slice.85), channel_id=1, source_target_pairs={{0,6},{2,0},{4,2},{6,4},{1,7},{3,1},{5,3},{7,5},{8,14},{10,8},{12,... | collective-permute-start | bytes 245768 | tf_op jit(solution)/shard_map/ppermute | solution.py:83
  12.0 21.0 %collective-permute-start.1 = (bf16[160,256]{1,0:T(8,128)(2,1)S(1)}, bf16[160,256]{1,0:T(8,128)(2,1)S(1)}, u32[]{:S(2)}, u32[]{:S(2)}) collective-permute-start(bf16[160,256]{1,0:T(8,128)(2,1)S(1)} %slice.85), channel_id=1, source_target_pairs={{0,4},{2,6},{4,0},{6,2},{1,5},{3,7},{5,1},{7,3},{8,12},{10,14},{12... | collective-permute-start | bytes 245768 | tf_op jit(solution)/shard_map/ppermute | solution.py:83
  14.0 19.0 %collective-permute-start = (bf16[160,256]{1,0:T(8,128)(2,1)S(1)}, bf16[160,256]{1,0:T(8,128)(2,1)S(1)}, u32[]{:S(2)}, u32[]{:S(2)}) collective-permute-start(bf16[160,256]{1,0:T(8,128)(2,1)S(1)} %slice.85), channel_id=1, source_target_pairs={{0,2},{2,4},{4,6},{6,0},{1,3},{3,5},{5,7},{7,1},{8,10},{10,12},{12... | collective-permute-start | bytes 245768 | tf_op jit(solution)/shard_map/ppermute | solution.py:83
  18.7 16.2 %collective-permute-start.5 = (bf16[512,512]{1,0:T(8,128)(2,1)S(1)}, bf16[512,512]{1,0:T(8,128)(2,1)S(1)}, u32[]{:S(2)}, u32[]{:S(2)}) collective-permute-start(bf16[512,512]{1,0:T(8,128)(2,1)S(1)} %copy-done), channel_id=1, source_target_pairs={{0,2},{2,4},{4,6},{6,0},{1,3},{3,5},{5,7},{7,1},{8,10},{10,12},{12... | collective-permute-start | bytes 1572872 | tf_op jit(solution)/shard_map/ppermute | solution.py:62

commit v8 on v5

--- a/solution.py
+++ b/solution.py
@@ -58,14 +58,26 @@
     query_seg, query_off = locate(query_idx, starts)
     positions = query_idx - query_off
     rot_keys = rotate_flat(keys, positions, head_size).astype(jnp.bfloat16)
-    rot_queries = rotate_flat(queries, positions, head_size).astype(jnp.bfloat16)
     width = queries.shape[1]
     chip_rows = lax.all_gather(
-        jnp.concatenate([rot_queries, rot_keys, values], axis=1), "core", axis=0, tiled=True
+        jnp.concatenate([queries, keys, values], axis=1), "core", axis=0, tiled=True
     )
-    kv_pair = lax.all_gather(chip_rows[:, width:], "chip", axis=0, tiled=True)
+    chip_kv = chip_rows[:, width:]
+    out_weight, chip_kv = lax.optimization_barrier((out_weight, chip_kv))
     if chips <= 8:
-        out_weight, kv_pair = lax.optimization_barrier((out_weight, kv_pair))
+        kv_pair = jnp.concatenate(
+            [chip_kv]
+            + [
+                lax.ppermute(chip_kv, "chip", [(i, (i + s) % chips) for i in range(chips)])
+                for s in range(1, chips)
+            ],
+            axis=0,
+        )
+        src_chip = (lax.axis_index("chip") - jnp.arange(chips)) % chips
+    else:
+        kv_pair = lax.all_gather(chip_kv, "chip", axis=0, tiled=True)
+        src_chip = jnp.arange(chips)
+    if chips <= 8:
         held = [out_weight] + [
             lax.ppermute(out_weight, "chip", [(i, (i + s) % chips) for i in range(chips)])
             for s in range(1, chips)
@@ -80,18 +92,22 @@
     chip_q = chip_rows[:, :width]
     chip_tok = cores * tok_rows
     chip_idx = lax.axis_index("chip") * chip_tok + jnp.arange(chip_tok)
-    chip_seg, _ = locate(chip_idx, starts)
+    chip_seg, chip_off = locate(chip_idx, starts)
+    chip_q = rotate_flat(chip_q, chip_idx - chip_off, head_size).astype(jnp.bfloat16)
     query_rows = jnp.concatenate(
         [chip_q[:, h * head_size:(h + 1) * head_size] for h in range(groups)], axis=0
     )
     row_idx = jnp.tile(chip_idx, groups)
     row_seg = jnp.tile(chip_seg, groups)
     scale = 1.0 / head_size**0.5
-    key_piece = kv_pair[:, :head_size]
     value_piece = kv_pair[:, head_size:]
-    span = key_piece.shape[0]
-    key_idx = jnp.arange(span)
+    span = kv_pair.shape[0]
+    chip_tok_kv = chip_kv.shape[0]
+    key_idx = (src_chip[:, None] * chip_tok_kv + jnp.arange(chip_tok_kv)[None, :]).reshape(span)
     key_seg, key_off = locate(key_idx, starts)
+    key_piece = rotate_flat(kv_pair[:, :head_size], key_idx - key_off, head_size).astype(
+        jnp.bfloat16
+    )
     live = (key_seg[None, :] == row_seg[:, None]) & (key_idx[None, :] <= row_idx[:, None])
     scores = (
         jnp.einsum("rd,nd->rn", query_rows, key_piece, preferred_element_type=jnp.float32) * scale

time: 68.5 us -> 61.8 us (0.902)
  blocking collectives: 35.5 us -> 2.07 us
  starting transfers between devices: 3.57 us -> 13 us
  waiting for transfers between devices: 18.6 us -> 26 us
  other arithmetic: 2.69 us -> 6.18 us
  matrix products: 4.84 us -> 8.3 us
  local copies, waits for them, and re-layouts: 2 us -> 5 us
    all_to_all x1 -> x0, blocking collectives: 22.8 us -> none  [body(): got = lax.all_to_all(routed, ('kv', 'core'), 0, 0, tiled=True)]
    all_to_all x0 -> x1, waiting for transfers between devices: none -> 16.9 us  [body(): got = lax.all_to_all(routed, ('kv', 'core'), 0, 0, tiled=True)]
    all_gather x2 -> x1, blocking collectives: 12.7 us -> 2.07 us  [body(): lax.all_gather(jnp.concatenate([queries, keys, values], axis=1), 'core',...]
    ppermute x3, waiting for transfers between devices: 18.6 us -> 9.04 us  [body(): lax.ppermute(out_weight, 'chip', [(i, (i + s) % chips) for i in range(chi...]
    ppermute x0 -> x3, starting transfers between devices: none -> 5.85 us  [body(): lax.ppermute(chip_kv, 'chip', [(i, (i + s) % chips) for i in range(chips)])]
    all_to_all x0 -> x1, starting transfers between devices: none -> 4.99 us  [body(): got = lax.all_to_all(routed, ('kv', 'core'), 0, 0, tiled=True)]
    dot_general x1, matrix products: 0.57 us -> 2.81 us  [body(): jnp.einsum('rd,nd->rn', query_rows, key_piece, preferred_element_type=jnp...]
    unnamed x12 -> x17, local copies, waits for them, and re-layouts: 0.95 us -> 2.87 us
  transfers between devices with their start and end apart: 3 -> 7, of which waited for: 2 -> 2; matrix products, arithmetic and copies ran while one was open for 3% -> 25% of each run, Pallas kernels for 0% -> 0%
where the time goes in v8:
time: 61.8 us; the launch traced here: 61.4 us
  waiting for transfers between devices  26 us (42%)
  starting transfers between devices  13 us (21%)
  matrix products  8.3 us (13%)
  other arithmetic  6.18 us (10%)
  local copies, waits for them, and re-layouts  5 us (8%)
  blocking collectives  2.07 us (3%)
  between operations  0.96 us (2%)
    all_to_all x1, waiting for transfers between devices, body(): got = lax.all_to_all(routed, ('kv', 'core'), 0, 0, tiled=True)  16.9 us
    ppermute x3, waiting for transfers between devices, body(): lax.ppermute(out_weight, 'chip', [(i, (i + s) % chips) for i in range(chi...  9.04 us
    ppermute x3, starting transfers between devices, body(): lax.ppermute(chip_kv, 'chip', [(i, (i + s) % chips) for i in range(chips)])  5.85 us
    all_to_all x1, starting transfers between devices, body(): got = lax.all_to_all(routed, ('kv', 'core'), 0, 0, tiled=True)  4.99 us
    unnamed x17, local copies, waits for them, and re-layouts  2.87 us
    dot_general x1, matrix products, body(): jnp.einsum('rd,nd->rn', query_rows, key_piece, preferred_element_type=jnp...  2.81 us
    ppermute x3, starting transfers between devices, body(): lax.ppermute(out_weight, 'chip', [(i, (i + s) % chips) for i in range(chi...  2.13 us
    dot_general x1, matrix products, body(): jnp.dot(probs.astype(jnp.bfloat16), value_piece, preferred_element_type=j...  2.12 us
  transfers between devices with their start and end apart: 7, of which 2 were waited for; matrix products, arithmetic and copies ran while one was open for 25% of the time, Pallas kernels for 0%

profile of v8, /device:TPU:0, one launch (start us, length us, event | category | flops | bytes accessed | tf_op | source)
XLA Modules:
  0.0 61.4 jit_solution(13160813018386088003)
XLA Ops:
  0.6 0.9 %pad_maximum_fusion.2 = bf16[80,768]{1,0:T(8,128)(2,1)S(1)} fusion(bf16[80,128]{1,0:T(8,128)(2,1)} %param.10, bf16[80,128]{1,0:T(8,128)(2,1)} %param.9, bf16[80,512]{1,0:T(8,128)(2,1)} %param.8), kind=kLoop, calls=%fused_computation.52 | loop fusion | flops 368640 | bytes 245760 | tf_op jit(solution)/shard_map/concatenate | solution.py:63
  1.6 2.1 %all_gather.3 = bf16[160,768]{1,0:T(8,128)(2,1)S(1)} all-gather(bf16[80,768]{1,0:T(8,128)(2,1)S(1)} %pad_maximum_fusion.2), channel_id=1, replica_groups=mesh['kv'=4,'chip'=4,'core'=2] {'core'}, dimensions={0}, use_global_device_ids=true | all-gather | bytes 368640 | tf_op jit(solution)/shard_map/all_gather | solution.py:62
  3.7 2.9 %collective-permute-start = (bf16[160,256]{1,0:T(8,128)(2,1)S(1)}, bf16[160,256]{1,0:T(8,128)(2,1)S(1)}, u32[]{:S(2)}, u32[]{:S(2)}) collective-permute-start(bf16[160,256]{1,0:T(8,128)(2,1)S(1)} %slice.85), channel_id=1, source_target_pairs={{0,2},{2,4},{4,6},{6,0},{1,3},{3,5},{5,7},{7,1},{8,10},{10,12},{12... | collective-permute-start | bytes 245768 | tf_op jit(solution)/shard_map/ppermute | solution.py:71
  6.6 1.5 %collective-permute-start.1 = (bf16[160,256]{1,0:T(8,128)(2,1)S(1)}, bf16[160,256]{1,0:T(8,128)(2,1)S(1)}, u32[]{:S(2)}, u32[]{:S(2)}) collective-permute-start(bf16[160,256]{1,0:T(8,128)(2,1)S(1)} %slice.85), channel_id=1, source_target_pairs={{0,4},{2,6},{4,0},{6,2},{1,5},{3,7},{5,1},{7,3},{8,12},{10,14},{12... | collective-permute-start | bytes 245768 | tf_op jit(solution)/shard_map/ppermute | solution.py:71
  8.1 1.4 %collective-permute-start.2 = (bf16[160,256]{1,0:T(8,128)(2,1)S(1)}, bf16[160,256]{1,0:T(8,128)(2,1)S(1)}, u32[]{:S(2)}, u32[]{:S(2)}) collective-permute-start(bf16[160,256]{1,0:T(8,128)(2,1)S(1)} %slice.85), channel_id=1, source_target_pairs={{0,6},{2,0},{4,2},{6,4},{1,7},{3,1},{5,3},{7,5},{8,14},{10,8},{12,... | collective-permute-start | bytes 245768 | tf_op jit(solution)/shard_map/ppermute | solution.py:71
  9.5 0.5 collective-permute-start.3
  10.0 1.5 %collective-permute-start.4 = (bf16[512,512]{1,0:T(8,128)(2,1)}, bf16[512,512]{1,0:T(8,128)(2,1)S(1)}, u32[]{:S(2)}, u32[]{:S(2)}) collective-permute-start(bf16[512,512]{1,0:T(8,128)(2,1)} %param.12), channel_id=1, source_target_pairs={{0,4},{2,6},{4,0},{6,2},{1,5},{3,7},{5,1},{7,3},{8,12},{10,14},{12... | collective-permute-start | bytes 1572872 | tf_op jit(solution)/shard_map/ppermute | solution.py:82
  11.6 0.7 %select_reduce_fusion.1 = s32[5]{0:T(128)S(1)} fusion(s32[4]{0:T(128)} %param.11, s32[5]{0:T(128)S(1)} %iota_add_fusion.3), kind=kLoop, calls=%fused_computation.75 | loop fusion | flops 55 | bytes 56 | tf_op jit(solution)/shard_map/reduce_sum | solution.py:53
  12.5 0.4 multiply_cosine_fusion.1
  13.3 1.3 %fusion.2 = bf16[160,512]{1,0:T(8,128)(2,1)S(1)} fusion(f32[160,512]{1,0:T(8,128)S(1)} %tile.33, bf16[512,512]{1,0:T(8,128)(2,1)} %constant.64.clone, f32[160,512]{1,0:T(8,128)S(1)} %tile.31, bf16[160,768]{1,0:T(8,128)(2,1)S(1)} %all_gather.3), kind=kOutput, calls=%fused_computation.12 | convolution fusion | flops 84295680 | bytes 1671168 | tf_op jit(solution)/shard_map/dot_general | solution.py:38
  15.0 0.6 %multiply_sine_fusion = (f32[640,64]{0,1:T(8,128)S(1)}, f32[640,64]{0,1:T(8,128)S(1)}) fusion(f32[64]{0:T(128)S(1)} %negate_power_fusion, f32[640]{0:T(1024)S(1)} %subtract_convert_fusion), kind=kLoop, calls=%fused_computation.39 | loop fusion | flops 40960 | bytes 330496 | tf_op jit(solution)/shard_map/sin | solution.py:37
  16.2 0.6 %constant_dynamic-update-slice_fusion.3 = bf16[640,256]{1,0:T(8,128)(2,1)} fusion(bf16[160,256]{1,0:T(8,128)(2,1)S(1)} %slice.85), kind=kLoop, calls=%fused_computation.60 | loop fusion | bytes 163840
  16.9 0.6 %constant_dynamic-update-slice_fusion.2 = bf16[640,256]{1,0:T(8,128)(2,1)} fusion(bf16[640,256]{1,0:T(8,128)(2,1)} %constant_dynamic-update-slice_fusion.3, bf16[160,256]{1,0:T(8,128)(2,1)S(1)} %collective-permute-done), kind=kLoop, calls=%fused_computation.59 | loop fusion | bytes 163840
  17.5 0.6 %constant_dynamic-update-slice_fusion.1 = bf16[640,256]{1,0:T(8,128)(2,1)} fusion(bf16[640,256]{1,0:T(8,128)(2,1)} %constant_dynamic-update-slice_fusion.2, bf16[160,256]{1,0:T(8,128)(2,1)S(1)} %collective-permute-done.1), kind=kLoop, calls=%fused_computation.58 | loop fusion | bytes 163840
  18.2 0.6 %constant_dynamic-update-slice_fusion = bf16[640,256]{1,0:T(8,128)(2,1)} fusion(bf16[640,256]{1,0:T(8,128)(2,1)} %constant_dynamic-update-slice_fusion.1, bf16[160,256]{1,0:T(8,128)(2,1)S(1)} %collective-permute-done.2), kind=kLoop, calls=%fused_computation.57 | loop fusion | bytes 163840 | tf_op jit(solution)/shard_map/concatenate | solution.py:68
  18.8 2.8 %fusion.40 = (f32[640]{0:T(1024)S(1)}, f32[640,640]{0,1:T(8,128)}) fusion(f32[640,128]{1,0:T(8,128)S(1)} %copy.23, f32[640,128]{1,0:T(8,128)S(1)} %copy.24, bf16[128,128]{1,0:T(8,128)(2,1)S(1)} %copy-done.2, bf16[640,256]{1,0:T(8,128)(2,1)} %constant_dynamic-update-slice_fusion, bf16[160,128]{1,0:T(8,128)(2,1)S(1)} %get-tuple-element.15, ...), kind=kOutput, calls=%fused_computation.96 | convolution fusion | flops 129351040 | bytes 2830848 | tf_op jit(solution)/shard_map/rd,nd->rn/dot_general | solution.py:113
  21.6 1.9 %fusion.10 = f32[640]{0:T(1024)S(1)} fusion(f32[640,640]{0,1:T(8,128)} %get-tuple-element.25, f32[640]{0:T(1024)S(1)} %get-tuple-element.24, s32[640]{0:T(1024)S(1)} %le.61, s32[640]{0:T(1024)S(1)} %eq.26, s32[640]{0:T(1024)S(1)} %add.104, s32[640]{0:T(1024)S(1)} %broadcast_add_fusion), kind=kLoop, calls=%fused_computation.21 | loop fusion | flops 2456960 | bytes 1653760 | tf_op jit(solution)/shard_map/reduce_sum | solution.py:118
  23.5 2.1 %fusion.1 = bf16[640,128]{1,0:T(8,128)(2,1)S(1)} fusion(f32[640,640]{0,1:T(8,128)} %get-tuple-element.25, f32[640]{0:T(1024)S(1)} %get-tuple-element.24, s32[640]{0:T(1024)S(1)} %le.61, s32[640]{0:T(1024)S(1)} %eq.26, s32[640]{0:T(1024)S(1)} %add.104, s32[640]{0:T(1024)S(1)} %broadcast_add_fusion, bf16[640,256]{1,0:T(8,128)(2,1)} %constant_dynamic-update-slice_fusion, ...), kind=kOutput, calls=%fused_computation.11 | convolution fusion | flops 107479040 | bytes 1981440 | tf_op jit(solution)/shard_map/dot_general | solution.py:119
  25.8 9.0 %collective-permute-done.5 = bf16[512,512]{1,0:T(8,128)(2,1)S(1)} collective-permute-done((bf16[512,512]{1,0:T(8,128)(2,1)S(1)}, bf16[512,512]{1,0:T(8,128)(2,1)S(1)}, u32[]{:S(2)}, u32[]{:S(2)}) %collective-permute-start.5) | collective-permute-done | bytes 524320 | tf_op jit(solution)/shard_map/ppermute | solution.py:82
  36.4 0.9 %pad_maximum_fusion = bf16[4,160,512]{2,1,0:T(8,128)(2,1)} fusion(bf16[1,160,512]{2,1,0:T(8,128)(2,1)S(1)} %fusion.6, bf16[1,160,512]{2,1,0:T(8,128)(2,1)S(1)} %fusion.5, bf16[1,160,512]{2,1,0:T(8,128)(2,1)S(1)} %fusion.4, bf16[1,160,512]{2,1,0:T(8,128)(2,1)S(1)} %fusion.3), kind=kLoop, calls=%fused_computation.25 | loop fusion | flops 983040 | bytes 1310720 | tf_op jit(solution)/shard_map/stack | solution.py:128
  37.3 5.0 %all-to-all-start = ((bf16[8,80,512]{2,1,0:T(8,128)(2,1)}), bf16[8,80,512]{2,1,0:T(8,128)(2,1)S(1)}, u32[]{:S(2)}, u32[]{:S(2)}) async-start(bf16[8,80,512]{2,1,0:T(8,128)(2,1)} %bitcast.14), calls=%async_computation | async-start | bytes 1310720 | tf_op jit(solution)/shard_map/all_to_all | solution.py:139
  42.8 0.8 %fusion.9 = bf16[80,128]{1,0:T(8,128)(2,1)} fusion(f32[80,128]{1,0:T(8,128)S(1)} %copy.27, bf16[80,128]{1,0:T(8,128)(2,1)S(1)} %copy-done.1, bf16[128,128]{1,0:T(8,128)(2,1)S(1)} %copy-done.2, f32[80,128]{1,0:T(8,128)S(1)} %copy.26), kind=kOutput, calls=%fused_computation.20 | convolution fusion | flops 2672640 | bytes 155648 | tf_op jit(solution)/shard_map/dot_general | solution.py:38
  43.6 16.9 %all-to-all-done = bf16[8,80,512]{2,1,0:T(8,128)(2,1)S(1)} async-done(((bf16[8,80,512]{2,1,0:T(8,128)(2,1)}), bf16[8,80,512]{2,1,0:T(8,128)(2,1)S(1)}, u32[]{:S(2)}, u32[]{:S(2)}) %all-to-all-start) | async-done | bytes 655392 | tf_op jit(solution)/shard_map/all_to_all | solution.py:139
  60.8 0.7 %copy.28 = bf16[10,8,2,512]{3,1,2,0:T(8,128)(2,1)} copy(bf16[10,8,2,512]{3,2,1,0:T(2,128)(2,1)S(1)} %bitcast.60) | data formatting | bytes 327680
  (61 shorter events, 3.9 us)
Async XLA Ops:
  3.6 13.1 %copy-start = (bf16[512,512]{1,0:T(8,128)(2,1)S(1)}, bf16[512,512]{1,0:T(8,128)(2,1)}, u32[]{:S(2)}) copy-start(bf16[512,512]{1,0:T(8,128)(2,1)} %param.12) | copy-start | bytes 1572868
  3.7 13.1 %collective-permute-start = (bf16[160,256]{1,0:T(8,128)(2,1)S(1)}, bf16[160,256]{1,0:T(8,128)(2,1)S(1)}, u32[]{:S(2)}, u32[]{:S(2)}) collective-permute-start(bf16[160,256]{1,0:T(8,128)(2,1)S(1)} %slice.85), channel_id=1, source_target_pairs={{0,2},{2,4},{4,6},{6,0},{1,3},{3,5},{5,7},{7,1},{8,10},{10,12},{12... | collective-permute-start | bytes 245768 | tf_op jit(solution)/shard_map/ppermute | solution.py:71
  6.6 11.0 %collective-permute-start.1 = (bf16[160,256]{1,0:T(8,128)(2,1)S(1)}, bf16[160,256]{1,0:T(8,128)(2,1)S(1)}, u32[]{:S(2)}, u32[]{:S(2)}) collective-permute-start(bf16[160,256]{1,0:T(8,128)(2,1)S(1)} %slice.85), channel_id=1, source_target_pairs={{0,4},{2,6},{4,0},{6,2},{1,5},{3,7},{5,1},{7,3},{8,12},{10,14},{12... | collective-permute-start | bytes 245768 | tf_op jit(solution)/shard_map/ppermute | solution.py:71
  8.1 10.1 %collective-permute-start.2 = (bf16[160,256]{1,0:T(8,128)(2,1)S(1)}, bf16[160,256]{1,0:T(8,128)(2,1)S(1)}, u32[]{:S(2)}, u32[]{:S(2)}) collective-permute-start(bf16[160,256]{1,0:T(8,128)(2,1)S(1)} %slice.85), channel_id=1, source_target_pairs={{0,6},{2,0},{4,2},{6,4},{1,7},{3,1},{5,3},{7,5},{8,14},{10,8},{12,... | collective-permute-start | bytes 245768 | tf_op jit(solution)/shard_map/ppermute | solution.py:71
  9.5 16.1 %collective-permute-start.3 = (bf16[512,512]{1,0:T(8,128)(2,1)}, bf16[512,512]{1,0:T(8,128)(2,1)S(1)}, u32[]{:S(2)}, u32[]{:S(2)}) collective-permute-start(bf16[512,512]{1,0:T(8,128)(2,1)} %param.12), channel_id=1, source_target_pairs={{0,6},{2,0},{4,2},{6,4},{1,7},{3,1},{5,3},{7,5},{8,14},{10,8},{12,... | collective-permute-start | bytes 1572872 | tf_op jit(solution)/shard_map/ppermute | solution.py:82
  10.0 15.7 %collective-permute-start.4 = (bf16[512,512]{1,0:T(8,128)(2,1)}, bf16[512,512]{1,0:T(8,128)(2,1)S(1)}, u32[]{:S(2)}, u32[]{:S(2)}) collective-permute-start(bf16[512,512]{1,0:T(8,128)(2,1)} %param.12), channel_id=1, source_target_pairs={{0,4},{2,6},{4,0},{6,2},{1,5},{3,7},{5,1},{7,3},{8,12},{10,14},{12... | collective-permute-start | bytes 1572872 | tf_op jit(solution)/shard_map/ppermute | solution.py:82
  12.8 6.0 %copy-start.2 = (bf16[128,128]{1,0:T(8,128)(2,1)S(1)}, bf16[128,128]{1,0:T(8,128)(2,1)}, u32[]{:S(2)}) copy-start(bf16[128,128]{1,0:T(8,128)(2,1)} %constant.63.clone) | copy-start | bytes 98308
  16.8 18.0 %collective-permute-start.5 = (bf16[512,512]{1,0:T(8,128)(2,1)S(1)}, bf16[512,512]{1,0:T(8,128)(2,1)S(1)}, u32[]{:S(2)}, u32[]{:S(2)}) collective-permute-start(bf16[512,512]{1,0:T(8,128)(2,1)S(1)} %copy-done), channel_id=1, source_target_pairs={{0,2},{2,4},{4,6},{6,0},{1,3},{3,5},{5,7},{7,1},{8,10},{10,12},{12... | collective-permute-start | bytes 1572872 | tf_op jit(solution)/shard_map/ppermute | solution.py:82
  35.0 7.8 %copy-start.1 = (bf16[80,128]{1,0:T(8,128)(2,1)S(1)}, bf16[80,128]{1,0:T(8,128)(2,1)}, u32[]{:S(2)}) copy-start(bf16[80,128]{1,0:T(8,128)(2,1)} %param.9) | copy-start | bytes 61444
  37.3 23.2 %all-to-all-start = ((bf16[8,80,512]{2,1,0:T(8,128)(2,1)}), bf16[8,80,512]{2,1,0:T(8,128)(2,1)S(1)}, u32[]{:S(2)}, u32[]{:S(2)}) async-start(bf16[8,80,512]{2,1,0:T(8,128)(2,1)} %bitcast.14), calls=%async_computation | async-start | bytes 1310720 | tf_op jit(solution)/shard_map/all_to_all | solution.py:139

commit v9 on v8

--- a/solution.py
+++ b/solution.py
@@ -65,29 +65,32 @@
     chip_kv = chip_rows[:, width:]
     out_weight, chip_kv = lax.optimization_barrier((out_weight, chip_kv))
     if chips <= 8:
-        kv_pair = jnp.concatenate(
-            [chip_kv]
-            + [
-                lax.ppermute(chip_kv, "chip", [(i, (i + s) % chips) for i in range(chips)])
-                for s in range(1, chips)
-            ],
-            axis=0,
-        )
+        ring = lambda s: [(i, (i + s) % chips) for i in range(chips)]
+        kv_own = sorted({1, chips - 1} - {0})
+        kv_held = {0: chip_kv}
+        for s in kv_own:
+            kv_held[s] = lax.ppermute(chip_kv, "chip", ring(s))
+        kv_size = chip_kv.size
+        held = [out_weight]
+        for s in range(1, chips):
+            if s in kv_held:
+                held.append(lax.ppermute(out_weight, "chip", ring(s)))
+            else:
+                both = lax.ppermute(
+                    jnp.concatenate([chip_kv.reshape(-1), out_weight.reshape(-1)]), "chip", ring(s)
+                )
+                kv_held[s] = both[:kv_size].reshape(chip_kv.shape)
+                held.append(both[kv_size:].reshape(out_weight.shape))
+        kv_pair = jnp.concatenate([kv_held[s] for s in range(chips)], axis=0)
         src_chip = (lax.axis_index("chip") - jnp.arange(chips)) % chips
-    else:
-        kv_pair = lax.all_gather(chip_kv, "chip", axis=0, tiled=True)
-        src_chip = jnp.arange(chips)
-    if chips <= 8:
-        held = [out_weight] + [
-            lax.ppermute(out_weight, "chip", [(i, (i + s) % chips) for i in range(chips)])
-            for s in range(1, chips)
-        ]
         back = jnp.stack(held[::-1] + held[::-1], axis=0)
         here = lax.axis_index("chip")
         w_share = lax.dynamic_slice_in_dim(back, chips - 1 - here, chips, 0).reshape(
             chips * out_weight.shape[0], out_weight.shape[1]
         )
     else:
+        kv_pair = lax.all_gather(chip_kv, "chip", axis=0, tiled=True)
+        src_chip = jnp.arange(chips)
         w_share = lax.all_gather(out_weight, "chip", axis=0, tiled=True)
     chip_q = chip_rows[:, :width]
     chip_tok = cores * tok_rows
@@ -108,6 +111,7 @@
     key_piece = rotate_flat(kv_pair[:, :head_size], key_idx - key_off, head_size).astype(
         jnp.bfloat16
     )
+    key_piece, value_piece = lax.optimization_barrier((key_piece, value_piece))
     live = (key_seg[None, :] == row_seg[:, None]) & (key_idx[None, :] <= row_idx[:, None])
     scores = (
         jnp.einsum("rd,nd->rn", query_rows, key_piece, preferred_element_type=jnp.float32) * scale

time: 61.8 us -> 70.8 us (1.15)
  waiting for transfers between devices: 26 us -> 33.5 us
  local copies, waits for them, and re-layouts: 5 us -> 9.81 us
  matrix products: 8.3 us -> 4.79 us
    ppermute x6 -> x5, waiting for transfers between devices: 9.05 us -> 16.6 us  [the longest x1 13 us: body(): lax.ppermute(jnp.concatenate([chip_kv.reshape(-1), out_weight.reshape(-1)...]
    unnamed x17 -> x33, local copies, waits for them, and re-layouts: 2.87 us -> 6.13 us
    dot_general x1, matrix products: 2.81 us -> 0.55 us  [body(): jnp.einsum('rd,nd->rn', query_rows, key_piece, preferred_element_type=jnp...]
    dot_general x1, matrix products: 2.12 us -> 0.69 us  [body(): jnp.dot(probs.astype(jnp.bfloat16), value_piece, preferred_element_type=j...]
    reduce_sum x1, other arithmetic: 1.89 us -> 0.47 us  [body(): new_sum = jnp.sum(probs, axis=1)]
    another operation x6, local copies, waits for them, and re-layouts: 0.5 us -> 1.39 us  [rotate_flat(): sine = jnp.tile(jnp.sin(angle), (1, 2 * reps))]
    concatenate x0 -> x1, other arithmetic: none -> 0.88 us  [body(): jnp.concatenate([chip_kv.reshape(-1), out_weight.reshape(-1)])]
    dot_general x2 -> x3, matrix products: 2.05 us -> 2.24 us  [rotate_flat(): jnp.dot(field, half_swap(field.shape[1], head_size), preferred_element_ty...]
  transfers between devices with their start and end apart: 7 -> 6, of which waited for: 2 -> 3; matrix products, arithmetic and copies ran while one was open for 25% -> 20% of each run, Pallas kernels for 0% -> 0%
where the time goes in v9:
time: 70.8 us; the launch traced here: 70.3 us
  waiting for transfers between devices  33.5 us (47%)
  starting transfers between devices  12.9 us (18%)
  local copies, waits for them, and re-layouts  9.81 us (14%)
  other arithmetic  6.19 us (9%)
  matrix products  4.79 us (7%)
  blocking collectives  2.07 us (3%)
  between operations  1.06 us (1%)
    all_to_all x1, waiting for transfers between devices, body(): got = lax.all_to_all(routed, ('kv', 'core'), 0, 0, tiled=True)  16.9 us
    ppermute x1, waiting for transfers between devices, body(): lax.ppermute(jnp.concatenate([chip_kv.reshape(-1), out_weight.reshape(-1)...  13 us
    unnamed x33, local copies, waits for them, and re-layouts  6.13 us
    all_to_all x1, starting transfers between devices, body(): got = lax.all_to_all(routed, ('kv', 'core'), 0, 0, tiled=True)  5 us
    ppermute x2, starting transfers between devices, body(): kv_held[s] = lax.ppermute(chip_kv, 'chip', ring(s))  3.91 us
    ppermute x2, waiting for transfers between devices, body(): held.append(lax.ppermute(out_weight, 'chip', ring(s)))  3.58 us
    dot_general x3, matrix products, rotate_flat(): jnp.dot(field, half_swap(field.shape[1], head_size), preferred_element_ty...  2.24 us
    all_gather x1, blocking collectives, body(): lax.all_gather(jnp.concatenate([queries, keys, values], axis=1), 'core',...  2.07 us
  transfers between devices with their start and end apart: 6, of which 3 were waited for; matrix products, arithmetic and copies ran while one was open for 20% of the time, Pallas kernels for 0%

profile of v9, /device:TPU:0, one launch (start us, length us, event | category | flops | bytes accessed | tf_op | source)
XLA Modules:
  0.0 70.3 jit_solution(3060028580258963442)
XLA Ops:
  0.6 0.9 %pad_maximum_fusion.3 = bf16[80,768]{1,0:T(8,128)(2,1)S(1)} fusion(bf16[80,128]{1,0:T(8,128)(2,1)} %param.10, bf16[80,128]{1,0:T(8,128)(2,1)} %param.9, bf16[80,512]{1,0:T(8,128)(2,1)} %param.8), kind=kLoop, calls=%fused_computation.50 | loop fusion | flops 368640 | bytes 245760 | tf_op jit(solution)/shard_map/concatenate | solution.py:63
  1.6 2.1 %all_gather.3 = bf16[160,768]{1,0:T(8,128)(2,1)S(1)} all-gather(bf16[80,768]{1,0:T(8,128)(2,1)S(1)} %pad_maximum_fusion.3), channel_id=1, replica_groups=mesh['kv'=4,'chip'=4,'core'=2] {'core'}, dimensions={0}, use_global_device_ids=true | all-gather | bytes 368640 | tf_op jit(solution)/shard_map/all_gather | solution.py:62
  3.7 2.9 %collective-permute-start = (bf16[160,256]{1,0:T(8,128)(2,1)S(1)}, bf16[160,256]{1,0:T(8,128)(2,1)}, u32[]{:S(2)}, u32[]{:S(2)}) collective-permute-start(bf16[160,256]{1,0:T(8,128)(2,1)S(1)} %slice.104), channel_id=1, source_target_pairs={{0,2},{2,4},{4,6},{6,0},{1,3},{3,5},{5,7},{7,1},{8,10},{10,12},{12... | collective-permute-start | bytes 245768 | tf_op jit(solution)/shard_map/ppermute | solution.py:72
  6.6 1.0 %collective-permute-start.2 = (bf16[160,256]{1,0:T(8,128)(2,1)S(1)}, bf16[160,256]{1,0:T(8,128)(2,1)}, u32[]{:S(2)}, u32[]{:S(2)}) collective-permute-start(bf16[160,256]{1,0:T(8,128)(2,1)S(1)} %slice.104), channel_id=1, source_target_pairs={{0,6},{2,0},{4,2},{6,4},{1,7},{3,1},{5,3},{7,5},{8,14},{10,8},{12,... | collective-permute-start | bytes 245768 | tf_op jit(solution)/shard_map/ppermute | solution.py:72
  7.6 2.0 %collective-permute-start.3 = (bf16[512,512]{1,0:T(8,128)(2,1)}, bf16[512,512]{1,0:T(8,128)(2,1)S(1)}, u32[]{:S(2)}, u32[]{:S(2)}) collective-permute-start(bf16[512,512]{1,0:T(8,128)(2,1)} %param.12), channel_id=1, source_target_pairs={{0,6},{2,0},{4,2},{6,4},{1,7},{3,1},{5,3},{7,5},{8,14},{10,8},{12,... | collective-permute-start | bytes 1572872 | tf_op jit(solution)/shard_map/ppermute | solution.py:77
  9.6 1.3 %copy.29 = bf16[64,4,8,128]{3,1,2,0:T(4,128)(2,1)S(1)} copy(bf16[64,4,8,128]{3,2,1,0:T(8,128)(2,1)} %bitcast.60) | data formatting | bytes 1048576
  11.0 0.9 %pad_maximum_fusion.1 = bf16[303104]{0:T(1024)(128)(2,1)} fusion(bf16[262144]{0:T(1024)(128)(2,1)S(1)} %bitcast.62, bf16[40960]{0:T(1024)(128)(2,1)S(1)} %bitcast.68), kind=kLoop, calls=%fused_computation.26 | loop fusion | flops 1212416 | bytes 1212416 | tf_op jit(solution)/shard_map/concatenate | solution.py:80
  11.8 1.9 %collective-permute-start.1 = (bf16[303104]{0:T(1024)(128)(2,1)}, bf16[303104]{0:T(1024)(128)(2,1)S(1)}, u32[]{:S(2)}, u32[]{:S(2)}) collective-permute-start(bf16[303104]{0:T(1024)(128)(2,1)} %pad_maximum_fusion.1), channel_id=1, source_target_pairs={{0,4},{2,6},{4,0},{6,2},{1,5},{3,7},{5,1},{7,3},{8,12},{10,14},{12... | collective-permute-start | bytes 1818632 | tf_op jit(solution)/shard_map/ppermute | solution.py:79
  14.8 1.0 %multiply_cosine_fusion.1 = (f32[160,64]{1,0:T(8,128)S(1)}, f32[160,64]{1,0:T(8,128)}) fusion(f32[64]{0:T(128)S(1)} %negate_power_fusion, f32[160]{0:T(256)S(1)} %get-tuple-element.32), kind=kLoop, calls=%fused_computation.52 | loop fusion | flops 10240 | bytes 82816 | tf_op jit(solution)/shard_map/cos | solution.py:36
  16.1 0.9 %tile.32 = f32[160,8,64]{2,1,0:T(8,128)S(1)} broadcast(f32[160,64]{1,0:T(8,128)} %get-tuple-element.25), dimensions={0,2} | broadcast | bytes 368640 | tf_op jit(solution)/shard_map/tile | solution.py:37
  17.2 1.3 %fusion.2 = bf16[160,512]{1,0:T(8,128)(2,1)S(1)} fusion(f32[160,512]{1,0:T(8,128)S(1)} %tile.33, bf16[512,512]{1,0:T(8,128)(2,1)} %constant.64.clone, f32[160,512]{1,0:T(8,128)S(1)} %tile.31, bf16[160,768]{1,0:T(8,128)(2,1)S(1)} %all_gather.3), kind=kOutput, calls=%fused_computation.12 | convolution fusion | flops 84295680 | bytes 1671168 | tf_op jit(solution)/shard_map/dot_general | solution.py:38
  19.8 0.9 %constant_dynamic-update-slice_fusion.2 = bf16[640,256]{1,0:T(8,128)(2,1)S(1)} fusion(bf16[640,256]{1,0:T(8,128)(2,1)S(1)} %constant_dynamic-update-slice_fusion.3, bf16[160,256]{1,0:T(8,128)(2,1)} %collective-permute-done), kind=kLoop, calls=%fused_computation.57 | loop fusion | bytes 163840
  20.7 3.6 %collective-permute-done.3 = bf16[512,512]{1,0:T(8,128)(2,1)S(1)} collective-permute-done((bf16[512,512]{1,0:T(8,128)(2,1)}, bf16[512,512]{1,0:T(8,128)(2,1)S(1)}, u32[]{:S(2)}, u32[]{:S(2)}) %collective-permute-start.3) | collective-permute-done | bytes 524320 | tf_op jit(solution)/shard_map/ppermute | solution.py:77
  24.3 0.8 %bitcast_dynamic-update-slice_fusion.4 = bf16[8,512,512]{2,1,0:T(8,128)(2,1)} fusion(bf16[512,512]{1,0:T(8,128)(2,1)S(1)} %collective-permute-done.3), kind=kLoop, calls=%fused_computation.35 | loop fusion | bytes 1048576
  25.1 13.0 %collective-permute-done.1 = bf16[303104]{0:T(1024)(128)(2,1)S(1)} collective-permute-done((bf16[303104]{0:T(1024)(128)(2,1)}, bf16[303104]{0:T(1024)(128)(2,1)S(1)}, u32[]{:S(2)}, u32[]{:S(2)}) %collective-permute-start.1) | collective-permute-done | bytes 606240 | tf_op jit(solution)/shard_map/ppermute | solution.py:79
  38.2 0.9 %constant_dynamic-update-slice_fusion = bf16[640,256]{1,0:T(8,128)(2,1)S(1)} fusion(bf16[640,256]{1,0:T(8,128)(2,1)S(1)} %constant_dynamic-update-slice_fusion.1, bf16[160,256]{1,0:T(8,128)(2,1)} %collective-permute-done.2), kind=kLoop, calls=%fused_computation.55 | loop fusion | bytes 163840 | tf_op jit(solution)/shard_map/concatenate | solution.py:84
  40.7 1.1 %copy-done.3 = bf16[8,512,512]{2,1,0:T(8,128)(2,1)S(1)} copy-done((bf16[8,512,512]{2,1,0:T(8,128)(2,1)S(1)}, bf16[8,512,512]{2,1,0:T(8,128)(2,1)}, u32[]{:S(2)}) %copy-start.3) | copy-done | bytes 4194328
  41.9 0.7 fusion.1
  42.7 1.0 %copy-done = bf16[512,512]{1,0:T(8,128)(2,1)S(1)} copy-done((bf16[512,512]{1,0:T(8,128)(2,1)S(1)}, bf16[512,512]{1,0:T(8,128)(2,1)}, u32[]{:S(2)}) %copy-start) | copy-done | bytes 524312
  45.2 0.9 %pad_maximum_fusion = bf16[4,160,512]{2,1,0:T(8,128)(2,1)} fusion(bf16[1,160,512]{2,1,0:T(8,128)(2,1)S(1)} %fusion.6, bf16[1,160,512]{2,1,0:T(8,128)(2,1)S(1)} %fusion.5, bf16[1,160,512]{2,1,0:T(8,128)(2,1)S(1)} %fusion.4, bf16[1,160,512]{2,1,0:T(8,128)(2,1)S(1)} %fusion.3), kind=kLoop, calls=%fused_computation.25 | loop fusion | flops 983040 | bytes 1310720 | tf_op jit(solution)/shard_map/stack | solution.py:132
  46.2 5.0 %all-to-all-start = ((bf16[8,80,512]{2,1,0:T(8,128)(2,1)}), bf16[8,80,512]{2,1,0:T(8,128)(2,1)S(1)}, u32[]{:S(2)}, u32[]{:S(2)}) async-start(bf16[8,80,512]{2,1,0:T(8,128)(2,1)} %bitcast.13), calls=%async_computation | async-start | bytes 1310720 | tf_op jit(solution)/shard_map/all_to_all | solution.py:143
  51.7 0.8 %fusion.9 = bf16[80,128]{1,0:T(8,128)(2,1)} fusion(f32[80,128]{1,0:T(8,128)S(1)} %copy.27, bf16[80,128]{1,0:T(8,128)(2,1)S(1)} %copy-done.2, bf16[128,128]{1,0:T(8,128)(2,1)S(1)} %copy-done.1, f32[80,128]{1,0:T(8,128)S(1)} %copy.26), kind=kOutput, calls=%fused_computation.20 | convolution fusion | flops 2672640 | bytes 155648 | tf_op jit(solution)/shard_map/dot_general | solution.py:38
  52.4 16.9 %all-to-all-done = bf16[8,80,512]{2,1,0:T(8,128)(2,1)S(1)} async-done(((bf16[8,80,512]{2,1,0:T(8,128)(2,1)}), bf16[8,80,512]{2,1,0:T(8,128)(2,1)S(1)}, u32[]{:S(2)}, u32[]{:S(2)}) %all-to-all-start) | async-done | bytes 655392 | tf_op jit(solution)/shard_map/all_to_all | solution.py:143
  69.6 0.7 copy.30
  (81 shorter events, 6.8 us)
Async XLA Ops:
  0.6 13.3 %copy-start.9 = (s32[4]{0:T(128)S(1)}, s32[4]{0:T(128)}, u32[]{:S(2)}) copy-start(s32[4]{0:T(128)} %param.11) | copy-start | bytes 52
  3.7 16.2 %collective-permute-start = (bf16[160,256]{1,0:T(8,128)(2,1)S(1)}, bf16[160,256]{1,0:T(8,128)(2,1)}, u32[]{:S(2)}, u32[]{:S(2)}) collective-permute-start(bf16[160,256]{1,0:T(8,128)(2,1)S(1)} %slice.104), channel_id=1, source_target_pairs={{0,2},{2,4},{4,6},{6,0},{1,3},{3,5},{5,7},{7,1},{8,10},{10,12},{12... | collective-permute-start | bytes 245768 | tf_op jit(solution)/shard_map/ppermute | solution.py:72
  6.6 31.6 %collective-permute-start.2 = (bf16[160,256]{1,0:T(8,128)(2,1)S(1)}, bf16[160,256]{1,0:T(8,128)(2,1)}, u32[]{:S(2)}, u32[]{:S(2)}) collective-permute-start(bf16[160,256]{1,0:T(8,128)(2,1)S(1)} %slice.104), channel_id=1, source_target_pairs={{0,6},{2,0},{4,2},{6,4},{1,7},{3,1},{5,3},{7,5},{8,14},{10,8},{12,... | collective-permute-start | bytes 245768 | tf_op jit(solution)/shard_map/ppermute | solution.py:72
  7.6 16.7 %collective-permute-start.3 = (bf16[512,512]{1,0:T(8,128)(2,1)}, bf16[512,512]{1,0:T(8,128)(2,1)S(1)}, u32[]{:S(2)}, u32[]{:S(2)}) collective-permute-start(bf16[512,512]{1,0:T(8,128)(2,1)} %param.12), channel_id=1, source_target_pairs={{0,6},{2,0},{4,2},{6,4},{1,7},{3,1},{5,3},{7,5},{8,14},{10,8},{12,... | collective-permute-start | bytes 1572872 | tf_op jit(solution)/shard_map/ppermute | solution.py:77
  9.5 33.1 %collective-permute-start.4 = (bf16[512,512]{1,0:T(8,128)(2,1)}, bf16[512,512]{1,0:T(8,128)(2,1)S(1)}, u32[]{:S(2)}, u32[]{:S(2)}) collective-permute-start(bf16[512,512]{1,0:T(8,128)(2,1)} %param.12), channel_id=1, source_target_pairs={{0,2},{2,4},{4,6},{6,0},{1,3},{3,5},{5,7},{7,1},{8,10},{10,12},{12... | collective-permute-start | bytes 1572872 | tf_op jit(solution)/shard_map/ppermute | solution.py:77
  11.8 26.3 %collective-permute-start.1 = (bf16[303104]{0:T(1024)(128)(2,1)}, bf16[303104]{0:T(1024)(128)(2,1)S(1)}, u32[]{:S(2)}, u32[]{:S(2)}) collective-permute-start(bf16[303104]{0:T(1024)(128)(2,1)} %pad_maximum_fusion.1), channel_id=1, source_target_pairs={{0,4},{2,6},{4,0},{6,2},{1,5},{3,7},{5,1},{7,3},{8,12},{10,14},{12... | collective-permute-start | bytes 1818632 | tf_op jit(solution)/shard_map/ppermute | solution.py:79
  14.0 0.8 %copy-start.7 = (s32[5]{0:T(128)}, s32[5]{0:T(128)S(1)}, u32[]{:S(2)}) copy-start(s32[5]{0:T(128)S(1)} %compare_select_fusion.4) | copy-start | bytes 64
  14.1 0.8 %copy-start.4 = (s32[160]{0:T(256)}, s32[160]{0:T(256)S(1)}, u32[]{:S(2)}) copy-start(s32[160]{0:T(256)S(1)} %iota_add_fusion.1) | copy-start | bytes 1924
  18.5 1.1 %copy-start.6 = (s32[160]{0:T(256)S(1)}, s32[160]{0:T(256)}, u32[]{:S(2)}) copy-start(s32[160]{0:T(256)} %get-tuple-element.33) | copy-start | bytes 1924
  18.5 1.2 %copy-start.5 = (s32[160]{0:T(256)S(1)}, s32[160]{0:T(256)}, u32[]{:S(2)}) copy-start(s32[160]{0:T(256)} %copy-done.4) | copy-start | bytes 1924
  19.4 19.7 %copy-start.1 = (bf16[128,128]{1,0:T(8,128)(2,1)S(1)}, bf16[128,128]{1,0:T(8,128)(2,1)}, u32[]{:S(2)}) copy-start(bf16[128,128]{1,0:T(8,128)(2,1)} %constant.63.clone) | copy-start | bytes 98308
  39.7 2.2 %copy-start.3 = (bf16[8,512,512]{2,1,0:T(8,128)(2,1)S(1)}, bf16[8,512,512]{2,1,0:T(8,128)(2,1)}, u32[]{:S(2)}) copy-start(bf16[8,512,512]{2,1,0:T(8,128)(2,1)} %bitcast_dynamic-update-slice_fusion.4) | copy-start | bytes 12582916
  42.6 1.0 %copy-start = (bf16[512,512]{1,0:T(8,128)(2,1)S(1)}, bf16[512,512]{1,0:T(8,128)(2,1)}, u32[]{:S(2)}) copy-start(bf16[512,512]{1,0:T(8,128)(2,1)} %param.12) | copy-start | bytes 1572868
  44.9 6.3 %copy-start.8 = (s32[5]{0:T(128)S(1)}, s32[5]{0:T(128)}, u32[]{:S(2)}) copy-start(s32[5]{0:T(128)} %copy-done.7) | copy-start | bytes 64
  45.2 6.5 %copy-start.2 = (bf16[80,128]{1,0:T(8,128)(2,1)S(1)}, bf16[80,128]{1,0:T(8,128)(2,1)}, u32[]{:S(2)}) copy-start(bf16[80,128]{1,0:T(8,128)(2,1)} %param.9) | copy-start | bytes 61444
  46.2 23.2 %all-to-all-start = ((bf16[8,80,512]{2,1,0:T(8,128)(2,1)}), bf16[8,80,512]{2,1,0:T(8,128)(2,1)S(1)}, u32[]{:S(2)}, u32[]{:S(2)}) async-start(bf16[8,80,512]{2,1,0:T(8,128)(2,1)} %bitcast.13), calls=%async_computation | async-start | bytes 1310720 | tf_op jit(solution)/shard_map/all_to_all | solution.py:143

commit v10 on v7

--- a/solution.py
+++ b/solution.py
@@ -57,14 +57,13 @@
     query_idx = first_tok + jnp.arange(tok_rows)
     query_seg, query_off = locate(query_idx, starts)
     positions = query_idx - query_off
-    if chips <= 8:
+    if chips <= 8 and chips & (chips - 1) == 0:
         held = [out_weight] + [
-            lax.ppermute(out_weight, "chip", [(i, (i + s) % chips) for i in range(chips)])
-            for s in range(1, chips)
+            lax.ppermute(out_weight, "chip", [(i, i ^ d) for i in range(chips)])
+            for d in range(1, chips)
         ]
-        back = jnp.stack(held[::-1] + held[::-1], axis=0)
-        here = lax.axis_index("chip")
-        w_share = lax.dynamic_slice_in_dim(back, chips - 1 - here, chips, 0).reshape(
+        order = lax.axis_index("chip") ^ jnp.arange(chips)
+        w_share = jnp.stack(held, axis=0)[order].reshape(
             chips * out_weight.shape[0], out_weight.shape[1]
         )
     else:
@@ -76,16 +75,16 @@
         jnp.concatenate([rot_queries, rot_keys, values], axis=1), "core", axis=0, tiled=True
     )
     chip_kv = chip_rows[:, width:]
-    if chips <= 8:
+    if chips <= 8 and chips & (chips - 1) == 0:
         kv_pair = jnp.concatenate(
             [chip_kv]
             + [
-                lax.ppermute(chip_kv, "chip", [(i, (i + s) % chips) for i in range(chips)])
-                for s in range(1, chips)
+                lax.ppermute(chip_kv, "chip", [(i, i ^ d) for i in range(chips)])
+                for d in range(1, chips)
             ],
             axis=0,
         )
-        src_chip = (lax.axis_index("chip") - jnp.arange(chips)) % chips
+        src_chip = lax.axis_index("chip") ^ jnp.arange(chips)
     else:
         kv_pair = lax.all_gather(chip_kv, "chip", axis=0, tiled=True)
         src_chip = jnp.arange(chips)

time: 60.7 us -> 65.4 us (1.077)
  local copies, waits for them, and re-layouts: 2.08 us -> 4.63 us
  waiting for transfers between devices: 14.5 us -> 16.2 us
  starting transfers between devices: 10.5 us -> 9.77 us
    dot_general x4, matrix products: 1.32 us -> 3.52 us  [body(): jnp.dot(chip_att, w_share[c * per_c:(c + 1) * per_c].T, preferred_element...]
    gather x0 -> x1, local copies, waits for them, and re-layouts: none -> 2.03 us  [body(): jnp.stack(held, axis=0)[order]]
    dot_general x2, matrix products: 2.23 us -> 0.35 us  [rotate_flat(): jnp.dot(field, half_swap(field.shape[1], head_size), preferred_element_ty...]
    ppermute x6, waiting for transfers between devices: 14.5 us -> 16.2 us  [the longest x3 16.2 us: body(): lax.ppermute(chip_kv, 'chip', [(i, i ^ d) for i in range(chips)])]
    another operation x0 -> x1, other arithmetic: none -> 1.3 us  [body(): jnp.stack(held, axis=0)[order]]
    concatenate x1, other arithmetic: 0.74 us -> 0.01 us  [body(): jnp.concatenate([rot_queries, rot_keys, values], axis=1)]
    ppermute x6, starting transfers between devices: 10.5 us -> 9.77 us  [the longest x3 6.22 us: body(): lax.ppermute(out_weight, 'chip', [(i, i ^ d) for i in range(chips)])]
    unnamed x12 -> x19, local copies, waits for them, and re-layouts: 0.95 us -> 1.5 us
  transfers between devices with their start and end apart: 6 -> 6, of which waited for: 2 -> 2; matrix products, arithmetic and copies ran while one was open for 12% -> 7% of each run, Pallas kernels for 0% -> 0%
where the time goes in v10:
time: 65.4 us; the launch traced here: 65.1 us
  blocking collectives  25 us (38%)
  waiting for transfers between devices  16.2 us (25%)
  starting transfers between devices  9.77 us (15%)
  matrix products  5.11 us (8%)
  local copies, waits for them, and re-layouts  4.63 us (7%)
  other arithmetic  3.3 us (5%)
  between operations  1.02 us (2%)
    all_to_all x1, blocking collectives, body(): got = lax.all_to_all(routed, ('kv', 'core'), 0, 0, tiled=True)  23 us
    ppermute x3, waiting for transfers between devices, body(): lax.ppermute(chip_kv, 'chip', [(i, i ^ d) for i in range(chips)])  16.2 us
    ppermute x3, starting transfers between devices, body(): lax.ppermute(out_weight, 'chip', [(i, i ^ d) for i in range(chips)])  6.22 us
    ppermute x3, starting transfers between devices, body(): lax.ppermute(chip_kv, 'chip', [(i, i ^ d) for i in range(chips)])  3.54 us
    dot_general x4, matrix products, body(): jnp.dot(chip_att, w_share[c * per_c:(c + 1) * per_c].T, preferred_element...  3.52 us
    gather x1, local copies, waits for them, and re-layouts, body(): jnp.stack(held, axis=0)[order]  2.03 us
    all_gather x1, blocking collectives, body(): lax.all_gather(jnp.concatenate([rot_queries, rot_keys, values], axis=1),...  1.98 us
    unnamed x19, local copies, waits for them, and re-layouts  1.5 us
  transfers between devices with their start and end apart: 6, of which 2 were waited for; matrix products, arithmetic and copies ran while one was open for 7% of the time, Pallas kernels for 0%

profile of v10, /device:TPU:0, one launch (start us, length us, event | category | flops | bytes accessed | tf_op | source)
XLA Modules:
  0.0 65.1 jit_solution(18408756783599655760)
XLA Ops:
  0.7 4.0 %collective-permute-start.5 = (bf16[512,512]{1,0:T(8,128)(2,1)}, bf16[512,512]{1,0:T(8,128)(2,1)S(1)}, u32[]{:S(2)}, u32[]{:S(2)}) collective-permute-start(bf16[512,512]{1,0:T(8,128)(2,1)} %param.11), channel_id=1, source_target_pairs={{0,6},{2,4},{4,2},{6,0},{1,7},{3,5},{5,3},{7,1},{8,14},{10,12},{12... | collective-permute-start | bytes 1572872 | tf_op jit(solution)/shard_map/ppermute | solution.py:62
  4.6 0.5 collective-permute-start.4
  5.2 0.7 %select_reduce_fusion.1 = s32[5]{0:T(128)S(1)} fusion(s32[4]{0:T(128)} %param.10, s32[5]{0:T(128)S(1)} %iota_add_fusion.3), kind=kLoop, calls=%fused_computation.53 | loop fusion | flops 55 | bytes 56 | tf_op jit(solution)/shard_map/reduce_sum | solution.py:53
  6.0 0.2 multiply_cosine_fusion
  7.1 0.2 fusion.7
  7.4 2.0 %all_gather.3 = bf16[160,768]{1,0:T(8,128)(2,1)S(1)} all-gather(bf16[80,768]{1,0:T(8,128)(2,1)S(1)} %pad_maximum_fusion.4), channel_id=1, replica_groups=mesh['kv'=4,'chip'=4,'core'=2] {'core'}, dimensions={0}, use_global_device_ids=true | all-gather | bytes 368640 | tf_op jit(solution)/shard_map/all_gather | solution.py:74
  9.4 1.5 %collective-permute-start.2 = (bf16[160,256]{1,0:T(8,128)(2,1)S(1)}, bf16[160,256]{1,0:T(8,128)(2,1)S(1)}, u32[]{:S(2)}, u32[]{:S(2)}) collective-permute-start(bf16[160,256]{1,0:T(8,128)(2,1)S(1)} %slice.87), channel_id=1, source_target_pairs={{0,6},{2,4},{4,2},{6,0},{1,7},{3,5},{5,3},{7,1},{8,14},{10,12},{12... | collective-permute-start | bytes 245768 | tf_op jit(solution)/shard_map/ppermute | solution.py:82
  11.0 1.9 %collective-permute-start = (bf16[160,256]{1,0:T(8,128)(2,1)S(1)}, bf16[160,256]{1,0:T(8,128)(2,1)S(1)}, u32[]{:S(2)}, u32[]{:S(2)}) collective-permute-start(bf16[160,256]{1,0:T(8,128)(2,1)S(1)} %slice.87), channel_id=1, source_target_pairs={{0,2},{2,0},{4,6},{6,4},{1,3},{3,1},{5,7},{7,5},{8,10},{10,8},{12,... | collective-permute-start | bytes 245768 | tf_op jit(solution)/shard_map/ppermute | solution.py:82
  13.5 5.9 %collective-permute-done.2 = bf16[160,256]{1,0:T(8,128)(2,1)S(1)} collective-permute-done((bf16[160,256]{1,0:T(8,128)(2,1)S(1)}, bf16[160,256]{1,0:T(8,128)(2,1)S(1)}, u32[]{:S(2)}, u32[]{:S(2)}) %collective-permute-start.2) | collective-permute-done | bytes 81952 | tf_op jit(solution)/shard_map/ppermute | solution.py:82
  19.4 1.8 %collective-permute-start.3 = (bf16[512,512]{1,0:T(8,128)(2,1)S(1)}, bf16[512,512]{1,0:T(8,128)(2,1)S(1)}, u32[]{:S(2)}, u32[]{:S(2)}) collective-permute-start(bf16[512,512]{1,0:T(8,128)(2,1)S(1)} %copy-done.2), channel_id=1, source_target_pairs={{0,2},{2,0},{4,6},{6,4},{1,3},{3,1},{5,7},{7,5},{8,10},{10,8},{12,... | collective-permute-start | bytes 1572872 | tf_op jit(solution)/shard_map/ppermute | solution.py:62
  21.2 10.4 %collective-permute-done.1 = bf16[160,256]{1,0:T(8,128)(2,1)S(1)} collective-permute-done((bf16[160,256]{1,0:T(8,128)(2,1)S(1)}, bf16[160,256]{1,0:T(8,128)(2,1)S(1)}, u32[]{:S(2)}, u32[]{:S(2)}) %collective-permute-start.1) | collective-permute-done | bytes 81952 | tf_op jit(solution)/shard_map/ppermute | solution.py:82
  31.5 0.6 fusion.30
  32.1 0.5 fusion.11
  32.6 0.7 %fusion = bf16[640,128]{1,0:T(8,128)(2,1)S(1)} fusion(f32[640,640]{0,1:T(8,128)S(1)} %get-tuple-element.13, f32[640]{0:T(1024)S(1)} %get-tuple-element.12, s32[640]{0:T(1024)S(1)} %le.61, s32[640]{0:T(1024)S(1)} %eq.24, s32[640]{0:T(1024)S(1)} %add.89, s32[640]{0:T(1024)S(1)} %broadcast_add_fusion, bf16[640,256]{1,0:T(8,128)(2,1)S(1)} %pad_maximum_fusion.2, ...), kind=kOutput, calls=%fused_computation.10 | convolution fusion | flops 107479040 | bytes 1990656 | tf_op jit(solution)/shard_map/dot_general | solution.py:115
  33.3 0.8 %copy-done.3 = bf16[512,512]{1,0:T(8,128)(2,1)} copy-done((bf16[512,512]{1,0:T(8,128)(2,1)}, bf16[512,512]{1,0:T(8,128)(2,1)S(1)}, u32[]{:S(2)}) %copy-start.3) | copy-done | bytes 524312
  34.1 1.3 %pad_maximum_fusion = bf16[4,512,512]{2,1,0:T(8,128)(2,1)S(1)} fusion(bf16[1,512,512]{2,1,0:T(8,128)(2,1)S(1)} %bitcast.62, bf16[1,512,512]{2,1,0:T(8,128)(2,1)} %bitcast.63, bf16[1,512,512]{2,1,0:T(8,128)(2,1)S(1)} %bitcast.64, bf16[1,512,512]{2,1,0:T(8,128)(2,1)S(1)} %bitcast.61), kind=kLoop, calls=%fused_computation.1 | loop fusion | flops 3145728 | bytes 4194304 | tf_op jit(solution)/shard_map/stack | solution.py:66
  35.4 2.0 %gather_fusion = bf16[4,512,512]{2,1,0:T(8,128)(2,1)} fusion(bf16[4,512,512]{2,1,0:T(8,128)(2,1)S(1)} %pad_maximum_fusion, s32[1024]{0:T(1024)S(1)} %pad_clamp_fusion), kind=kCustom, calls=%fused_computation | custom fusion | bytes 4194320 | tf_op jit(solution)/shard_map/gather | solution.py:66
  37.5 1.5 %fusion.4 = bf16[1,160,512]{2,1,0:T(8,128)(2,1)S(1)} fusion(bf16[4,512,512]{2,1,0:T(8,128)(2,1)} %gather_fusion, bf16[160,128]{1,0:T(8,128)(2,1)S(1)} %get-tuple-element.7, bf16[160,128]{1,0:T(8,128)(2,1)S(1)} %get-tuple-element.8, bf16[160,128]{1,0:T(8,128)(2,1)S(1)} %get-tuple-element.9, bf16[160,128]{1,0:T(8,128)(2,1)S(1)} %get-tuple-element.6), kind=kOutput, calls=%fused_computation.14 | convolution fusion | flops 84623360 | bytes 851968 | tf_op jit(solution)/shard_map/dot_general | solution.py:126
  39.0 1.4 %fusion.3 = bf16[1,160,512]{2,1,0:T(8,128)(2,1)S(1)} fusion(bf16[4,512,512]{2,1,0:T(8,128)(2,1)} %gather_fusion, bf16[160,128]{1,0:T(8,128)(2,1)S(1)} %get-tuple-element.7, bf16[160,128]{1,0:T(8,128)(2,1)S(1)} %get-tuple-element.8, bf16[160,128]{1,0:T(8,128)(2,1)S(1)} %get-tuple-element.9, bf16[160,128]{1,0:T(8,128)(2,1)S(1)} %get-tuple-element.6), kind=kOutput, calls=%fused_computation.13 | convolution fusion | flops 84623360 | bytes 851968 | tf_op jit(solution)/shard_map/dot_general | solution.py:126
  40.3 0.3 fusion.2
  40.7 0.3 fusion.1
  41.1 23.0 %all_to_all.5 = bf16[8,80,512]{2,1,0:T(8,128)(2,1)S(1)} all-to-all(bf16[8,80,512]{2,1,0:T(8,128)(2,1)S(1)} %bitcast.57), channel_id=1, replica_groups=mesh['kv'=4,'chip'=4,'core'=2] {'kv','core'}, dimensions={0} | all-to-all | bytes 1310720 | tf_op jit(solution)/shard_map/all_to_all | solution.py:135
  64.2 0.2 copy.26
  64.4 0.7 %copy.27 = bf16[10,8,2,512]{3,1,2,0:T(8,128)(2,1)} copy(bf16[10,8,2,512]{3,2,1,0:T(2,128)(2,1)S(1)} %bitcast.59) | data formatting | bytes 327680
  (60 shorter events, 1.8 us)
Async XLA Ops:
  0.6 6.3 %copy-start.6 = (bf16[128,128]{1,0:T(8,128)(2,1)S(1)}, bf16[128,128]{1,0:T(8,128)(2,1)}, u32[]{:S(2)}) copy-start(bf16[128,128]{1,0:T(8,128)(2,1)} %constant.48.clone) | copy-start | bytes 98308
  0.6 6.5 %copy-start.1 = (bf16[512,512]{1,0:T(8,128)(2,1)S(1)}, bf16[512,512]{1,0:T(8,128)(2,1)}, u32[]{:S(2)}) copy-start(bf16[512,512]{1,0:T(8,128)(2,1)} %constant.49.clone) | copy-start | bytes 1572868
  0.7 6.3 %copy-start.7 = (bf16[80,128]{1,0:T(8,128)(2,1)S(1)}, bf16[80,128]{1,0:T(8,128)(2,1)}, u32[]{:S(2)}) copy-start(bf16[80,128]{1,0:T(8,128)(2,1)} %param.8) | copy-start | bytes 61444
  0.7 6.4 %copy-start.5 = (bf16[80,512]{1,0:T(8,128)(2,1)S(1)}, bf16[80,512]{1,0:T(8,128)(2,1)}, u32[]{:S(2)}) copy-start(bf16[80,512]{1,0:T(8,128)(2,1)} %param.7) | copy-start | bytes 245764
  0.7 32.6 %collective-permute-start.5 = (bf16[512,512]{1,0:T(8,128)(2,1)}, bf16[512,512]{1,0:T(8,128)(2,1)S(1)}, u32[]{:S(2)}, u32[]{:S(2)}) collective-permute-start(bf16[512,512]{1,0:T(8,128)(2,1)} %param.11), channel_id=1, source_target_pairs={{0,6},{2,4},{4,2},{6,0},{1,7},{3,5},{5,3},{7,1},{8,14},{10,12},{12... | collective-permute-start | bytes 1572872 | tf_op jit(solution)/shard_map/ppermute | solution.py:62
  4.6 28.7 %collective-permute-start.4 = (bf16[512,512]{1,0:T(8,128)(2,1)}, bf16[512,512]{1,0:T(8,128)(2,1)S(1)}, u32[]{:S(2)}, u32[]{:S(2)}) collective-permute-start(bf16[512,512]{1,0:T(8,128)(2,1)} %param.11), channel_id=1, source_target_pairs={{0,4},{2,6},{4,0},{6,2},{1,5},{3,7},{5,1},{7,3},{8,12},{10,14},{12... | collective-permute-start | bytes 1572872 | tf_op jit(solution)/shard_map/ppermute | solution.py:62
  6.3 1.0 %copy-start.8 = (bf16[80,128]{1,0:T(8,128)(2,1)S(1)}, bf16[80,128]{1,0:T(8,128)(2,1)}, u32[]{:S(2)}) copy-start(bf16[80,128]{1,0:T(8,128)(2,1)} %param.9) | copy-start | bytes 61444
  6.8 12.6 %copy-start.2 = (bf16[512,512]{1,0:T(8,128)(2,1)S(1)}, bf16[512,512]{1,0:T(8,128)(2,1)}, u32[]{:S(2)}) copy-start(bf16[512,512]{1,0:T(8,128)(2,1)} %param.11) | copy-start | bytes 1572868
  7.1 25.0 %copy-start.4 = (bf16[80,128]{1,0:T(8,128)(2,1)}, bf16[80,128]{1,0:T(8,128)(2,1)S(1)}, u32[]{:S(2)}) copy-start(bf16[80,128]{1,0:T(8,128)(2,1)S(1)} %fusion.10) | copy-start | bytes 61444
  9.4 10.0 %collective-permute-start.2 = (bf16[160,256]{1,0:T(8,128)(2,1)S(1)}, bf16[160,256]{1,0:T(8,128)(2,1)S(1)}, u32[]{:S(2)}, u32[]{:S(2)}) collective-permute-start(bf16[160,256]{1,0:T(8,128)(2,1)S(1)} %slice.87), channel_id=1, source_target_pairs={{0,6},{2,4},{4,2},{6,0},{1,7},{3,5},{5,3},{7,1},{8,14},{10,12},{12... | collective-permute-start | bytes 245768 | tf_op jit(solution)/shard_map/ppermute | solution.py:82
  10.9 20.6 %collective-permute-start.1 = (bf16[160,256]{1,0:T(8,128)(2,1)S(1)}, bf16[160,256]{1,0:T(8,128)(2,1)S(1)}, u32[]{:S(2)}, u32[]{:S(2)}) collective-permute-start(bf16[160,256]{1,0:T(8,128)(2,1)S(1)} %slice.87), channel_id=1, source_target_pairs={{0,4},{2,6},{4,0},{6,2},{1,5},{3,7},{5,1},{7,3},{8,12},{10,14},{12... | collective-permute-start | bytes 245768 | tf_op jit(solution)/shard_map/ppermute | solution.py:82
  11.0 20.5 %collective-permute-start = (bf16[160,256]{1,0:T(8,128)(2,1)S(1)}, bf16[160,256]{1,0:T(8,128)(2,1)S(1)}, u32[]{:S(2)}, u32[]{:S(2)}) collective-permute-start(bf16[160,256]{1,0:T(8,128)(2,1)S(1)} %slice.87), channel_id=1, source_target_pairs={{0,2},{2,0},{4,6},{6,4},{1,3},{3,1},{5,7},{7,5},{8,10},{10,8},{12,... | collective-permute-start | bytes 245768 | tf_op jit(solution)/shard_map/ppermute | solution.py:82
  19.4 13.9 %collective-permute-start.3 = (bf16[512,512]{1,0:T(8,128)(2,1)S(1)}, bf16[512,512]{1,0:T(8,128)(2,1)S(1)}, u32[]{:S(2)}, u32[]{:S(2)}) collective-permute-start(bf16[512,512]{1,0:T(8,128)(2,1)S(1)} %copy-done.2), channel_id=1, source_target_pairs={{0,2},{2,0},{4,6},{6,4},{1,3},{3,1},{5,7},{7,5},{8,10},{10,8},{12,... | collective-permute-start | bytes 1572872 | tf_op jit(solution)/shard_map/ppermute | solution.py:62
  33.3 0.8 %copy-start.3 = (bf16[512,512]{1,0:T(8,128)(2,1)}, bf16[512,512]{1,0:T(8,128)(2,1)S(1)}, u32[]{:S(2)}) copy-start(bf16[512,512]{1,0:T(8,128)(2,1)S(1)} %collective-permute-done.4) | copy-start | bytes 1572868
  37.5 2.9 %copy-start = (bf16[4,512,512]{2,1,0:T(8,128)(2,1)S(1)}, bf16[4,512,512]{2,1,0:T(8,128)(2,1)}, u32[]{:S(2)}) copy-start(bf16[4,512,512]{2,1,0:T(8,128)(2,1)} %gather_fusion) | copy-start | bytes 6291460

commit v11 on v8

--- a/solution.py
+++ b/solution.py
@@ -89,7 +89,7 @@
         )
     else:
         w_share = lax.all_gather(out_weight, "chip", axis=0, tiled=True)
-    chip_q = chip_rows[:, :width]
+    kv_pair, chip_q = lax.optimization_barrier((kv_pair, chip_rows[:, :width]))
     chip_tok = cores * tok_rows
     chip_idx = lax.axis_index("chip") * chip_tok + jnp.arange(chip_tok)
     chip_seg, chip_off = locate(chip_idx, starts)
@@ -108,6 +108,7 @@
     key_piece = rotate_flat(kv_pair[:, :head_size], key_idx - key_off, head_size).astype(
         jnp.bfloat16
     )
+    key_piece, value_piece = lax.optimization_barrier((key_piece, value_piece))
     live = (key_seg[None, :] == row_seg[:, None]) & (key_idx[None, :] <= row_idx[:, None])
     scores = (
         jnp.einsum("rd,nd->rn", query_rows, key_piece, preferred_element_type=jnp.float32) * scale

time: 61.8 us -> 62.5 us (1.011)
  matrix products: 8.3 us -> 5.64 us
  waiting for transfers between devices: 26 us -> 27.7 us
  other arithmetic: 6.18 us -> 7.03 us
  local copies, waits for them, and re-layouts: 5 us -> 5.67 us
    dot_general x1, matrix products: 2.81 us -> 0.55 us  [body(): jnp.einsum('rd,nd->rn', query_rows, key_piece, preferred_element_type=jnp...]
    ppermute x3, waiting for transfers between devices: 9.04 us -> 10.8 us  [body(): lax.ppermute(out_weight, 'chip', [(i, (i + s) % chips) for i in range(chi...]
    unnamed x17 -> x18, local copies, waits for them, and re-layouts: 2.87 us -> 1.29 us
    dot_general x1, matrix products: 2.12 us -> 0.69 us  [body(): jnp.dot(probs.astype(jnp.bfloat16), value_piece, preferred_element_type=j...]
    reduce_sum x1, other arithmetic: 1.89 us -> 0.47 us  [body(): new_sum = jnp.sum(probs, axis=1)]
    cos x2 -> x3, other arithmetic: 0.55 us -> 1.83 us  [rotate_flat(): cosine = jnp.tile(jnp.cos(angle), (1, 2 * reps))]
    dot_general x2 -> x3, matrix products: 2.05 us -> 3.08 us  [rotate_flat(): jnp.dot(field, half_swap(field.shape[1], head_size), preferred_element_ty...]
    concatenate x0 -> x1, other arithmetic: none -> 1.03 us  [body(): jnp.concatenate([chip_kv] + [lax.ppermute(chip_kv, 'chip', [(i, (i + s) %...]
  transfers between devices with their start and end apart: 7 -> 7, of which waited for: 2 -> 3; matrix products, arithmetic and copies ran while one was open for 25% -> 21% of each run, Pallas kernels for 0% -> 0%
where the time goes in v11:
time: 62.5 us; the launch traced here: 62.1 us
  waiting for transfers between devices  27.7 us (44%)
  starting transfers between devices  13 us (21%)
  other arithmetic  7.03 us (11%)
  local copies, waits for them, and re-layouts  5.67 us (9%)
  matrix products  5.64 us (9%)
  blocking collectives  2.07 us (3%)
  between operations  0.98 us (2%)
    all_to_all x1, waiting for transfers between devices, body(): got = lax.all_to_all(routed, ('kv', 'core'), 0, 0, tiled=True)  16.9 us
    ppermute x3, waiting for transfers between devices, body(): lax.ppermute(out_weight, 'chip', [(i, (i + s) % chips) for i in range(chi...  10.8 us
    ppermute x3, starting transfers between devices, body(): lax.ppermute(chip_kv, 'chip', [(i, (i + s) % chips) for i in range(chips)])  5.8 us
    all_to_all x1, starting transfers between devices, body(): got = lax.all_to_all(routed, ('kv', 'core'), 0, 0, tiled=True)  5.07 us
    dot_general x3, matrix products, rotate_flat(): jnp.dot(field, half_swap(field.shape[1], head_size), preferred_element_ty...  3.08 us
    ppermute x3, starting transfers between devices, body(): lax.ppermute(out_weight, 'chip', [(i, (i + s) % chips) for i in range(chi...  2.11 us
    all_gather x1, blocking collectives, body(): lax.all_gather(jnp.concatenate([queries, keys, values], axis=1), 'core',...  2.07 us
    cos x3, other arithmetic, rotate_flat(): cosine = jnp.tile(jnp.cos(angle), (1, 2 * reps))  1.83 us
  transfers between devices with their start and end apart: 7, of which 3 were waited for; matrix products, arithmetic and copies ran while one was open for 21% of the time, Pallas kernels for 0%

profile of v11, /device:TPU:0, one launch (start us, length us, event | category | flops | bytes accessed | tf_op | source)
XLA Modules:
  0.0 62.1 jit_solution(17108166213172293909)
XLA Ops:
  0.6 1.0 %pad_maximum_fusion.3 = bf16[80,768]{1,0:T(8,128)(2,1)S(1)} fusion(bf16[80,128]{1,0:T(8,128)(2,1)} %param.10, bf16[80,128]{1,0:T(8,128)(2,1)} %param.9, bf16[80,512]{1,0:T(8,128)(2,1)} %param.8), kind=kLoop, calls=%fused_computation.52 | loop fusion | flops 368640 | bytes 245760 | tf_op jit(solution)/shard_map/concatenate | solution.py:63
  1.6 2.1 %all_gather.3 = bf16[160,768]{1,0:T(8,128)(2,1)S(1)} all-gather(bf16[80,768]{1,0:T(8,128)(2,1)S(1)} %pad_maximum_fusion.3), channel_id=1, replica_groups=mesh['kv'=4,'chip'=4,'core'=2] {'core'}, dimensions={0}, use_global_device_ids=true | all-gather | bytes 368640 | tf_op jit(solution)/shard_map/all_gather | solution.py:62
  3.7 0.6 %slice.80 = bf16[160,256]{1,0:T(8,128)(2,1)} slice(bf16[160,768]{1,0:T(8,128)(2,1)S(1)} %all_gather.3), slice={[0:160], [512:768]} | slice | bytes 163840 | tf_op jit(solution)/shard_map/slice | solution.py:65
  4.3 2.8 %collective-permute-start = (bf16[160,256]{1,0:T(8,128)(2,1)}, bf16[160,256]{1,0:T(8,128)(2,1)}, u32[]{:S(2)}, u32[]{:S(2)}) collective-permute-start(bf16[160,256]{1,0:T(8,128)(2,1)} %slice.80), channel_id=1, source_target_pairs={{0,2},{2,4},{4,6},{6,0},{1,3},{3,5},{5,7},{7,1},{8,10},{10,12},{12... | collective-permute-start | bytes 245768 | tf_op jit(solution)/shard_map/ppermute | solution.py:71
  7.2 1.5 %collective-permute-start.1 = (bf16[160,256]{1,0:T(8,128)(2,1)}, bf16[160,256]{1,0:T(8,128)(2,1)}, u32[]{:S(2)}, u32[]{:S(2)}) collective-permute-start(bf16[160,256]{1,0:T(8,128)(2,1)} %slice.80), channel_id=1, source_target_pairs={{0,4},{2,6},{4,0},{6,2},{1,5},{3,7},{5,1},{7,3},{8,12},{10,14},{12... | collective-permute-start | bytes 245768 | tf_op jit(solution)/shard_map/ppermute | solution.py:71
  8.7 1.4 %collective-permute-start.2 = (bf16[160,256]{1,0:T(8,128)(2,1)}, bf16[160,256]{1,0:T(8,128)(2,1)}, u32[]{:S(2)}, u32[]{:S(2)}) collective-permute-start(bf16[160,256]{1,0:T(8,128)(2,1)} %slice.80), channel_id=1, source_target_pairs={{0,6},{2,0},{4,2},{6,4},{1,7},{3,1},{5,3},{7,5},{8,14},{10,8},{12,... | collective-permute-start | bytes 245768 | tf_op jit(solution)/shard_map/ppermute | solution.py:71
  10.7 1.5 %collective-permute-start.4 = (bf16[512,512]{1,0:T(8,128)(2,1)}, bf16[512,512]{1,0:T(8,128)(2,1)S(1)}, u32[]{:S(2)}, u32[]{:S(2)}) collective-permute-start(bf16[512,512]{1,0:T(8,128)(2,1)} %param.12), channel_id=1, source_target_pairs={{0,4},{2,6},{4,0},{6,2},{1,5},{3,7},{5,1},{7,3},{8,12},{10,14},{12... | collective-permute-start | bytes 1572872 | tf_op jit(solution)/shard_map/ppermute | solution.py:82
  12.4 0.7 %select_reduce_fusion.1 = s32[5]{0:T(128)S(1)} fusion(s32[4]{0:T(128)} %param.11, s32[5]{0:T(128)S(1)} %iota_add_fusion.3), kind=kLoop, calls=%fused_computation.71 | loop fusion | flops 55 | bytes 56 | tf_op jit(solution)/shard_map/reduce_sum | solution.py:53
  13.7 0.6 %multiply_cosine_fusion = (f32[640,64]{0,1:T(8,128)S(1)}, f32[640,64]{0,1:T(8,128)S(1)}) fusion(f32[64]{0:T(128)S(1)} %negate_power_fusion, f32[640]{0:T(1024)S(1)} %get-tuple-element.34), kind=kLoop, calls=%fused_computation.42 | loop fusion | flops 40960 | bytes 330496 | tf_op jit(solution)/shard_map/cos | solution.py:36
  14.9 1.0 %multiply_cosine_fusion.1 = (f32[160,64]{1,0:T(8,128)S(1)}, f32[160,64]{1,0:T(8,128)}) fusion(f32[64]{0:T(128)S(1)} %negate_power_fusion, f32[160]{0:T(256)S(1)} %get-tuple-element.36), kind=kLoop, calls=%fused_computation.54 | loop fusion | flops 10240 | bytes 82816 | tf_op jit(solution)/shard_map/cos | solution.py:36
  15.9 0.7 %slice.81 = bf16[160,512]{1,0:T(8,128)(2,1)} slice(bf16[160,768]{1,0:T(8,128)(2,1)S(1)} %all_gather.3), slice={[0:160], [0:512]} | slice | bytes 327680 | tf_op jit(solution)/shard_map/slice | solution.py:92
  17.2 0.9 %tile.32 = f32[160,8,64]{2,1,0:T(8,128)S(1)} broadcast(f32[160,64]{1,0:T(8,128)} %get-tuple-element.29), dimensions={0,2} | broadcast | bytes 368640 | tf_op jit(solution)/shard_map/tile | solution.py:37
  18.3 0.7 %tile.28 = s32[4,160]{1,0:T(4,128)S(1)} broadcast(s32[160]{0:T(256)} %get-tuple-element.37), dimensions={1} | broadcast | bytes 3200 | tf_op jit(solution)/shard_map/tile | solution.py:101
  19.2 1.0 %pad_maximum_fusion.1 = bf16[640,256]{1,0:T(8,128)(2,1)S(1)} fusion(bf16[160,256]{1,0:T(8,128)(2,1)} %collective-permute-done.2, bf16[160,256]{1,0:T(8,128)(2,1)} %collective-permute-done.1, bf16[160,256]{1,0:T(8,128)(2,1)} %collective-permute-done, bf16[160,256]{1,0:T(8,128)(2,1)} %slice.80), kind=kLoop, calls=%fused_computation.40 | loop fusion | flops 1310720 | bytes 655360 | tf_op jit(solution)/shard_map/concatenate | solution.py:68
  20.3 1.0 %fusion.2 = bf16[640,128]{1,0:T(8,128)(2,1)S(1)} fusion(f32[640,128]{1,0:T(8,128)S(1)} %copy.24, bf16[128,128]{1,0:T(8,128)(2,1)} %constant.63.clone, f32[640,128]{1,0:T(8,128)S(1)} %copy.23, bf16[640,256]{1,0:T(8,128)(2,1)S(1)} %pad_maximum_fusion.1), kind=kOutput, calls=%fused_computation.8 | convolution fusion | flops 21381120 | bytes 1179648 | tf_op jit(solution)/shard_map/dot_general | solution.py:38
  21.3 1.4 %fusion.4 = bf16[160,512]{1,0:T(8,128)(2,1)S(1)} fusion(f32[160,512]{1,0:T(8,128)S(1)} %tile.33, bf16[160,512]{1,0:T(8,128)(2,1)} %slice.81, bf16[512,512]{1,0:T(8,128)(2,1)} %constant.64.clone, f32[160,512]{1,0:T(8,128)S(1)} %tile.31), kind=kOutput, calls=%fused_computation.14 | convolution fusion | flops 84295680 | bytes 1507328 | tf_op jit(solution)/shard_map/dot_general | solution.py:38
  23.7 0.7 %fusion.3 = bf16[640,128]{1,0:T(8,128)(2,1)S(1)} fusion(bf16[640,128]{1,0:T(8,128)(2,1)S(1)} %slice.67, f32[640,640]{0,1:T(8,128)S(1)} %get-tuple-element.33, f32[640]{0:T(1024)S(1)} %get-tuple-element.32, s32[640]{0:T(1024)S(1)} %le.61, s32[640]{0:T(1024)S(1)} %eq.26, s32[640]{0:T(1024)S(1)} %add.104, s32[640]{0:T(1024)S(1)} %get-tuple-element.35, ...), kind=kOutput, calls=%fused_computation.13 | convolution fusion | flops 107479040 | bytes 1981440 | tf_op jit(solution)/shard_map/dot_general | solution.py:120
  24.4 1.0 %collective-permute-done.3 = bf16[512,512]{1,0:T(8,128)(2,1)S(1)} collective-permute-done((bf16[512,512]{1,0:T(8,128)(2,1)}, bf16[512,512]{1,0:T(8,128)(2,1)S(1)}, u32[]{:S(2)}, u32[]{:S(2)}) %collective-permute-start.3) | collective-permute-done | bytes 524320 | tf_op jit(solution)/shard_map/ppermute | solution.py:82
  25.6 9.8 %collective-permute-done.5 = bf16[512,512]{1,0:T(8,128)(2,1)S(1)} collective-permute-done((bf16[512,512]{1,0:T(8,128)(2,1)S(1)}, bf16[512,512]{1,0:T(8,128)(2,1)S(1)}, u32[]{:S(2)}, u32[]{:S(2)}) %collective-permute-start.5) | collective-permute-done | bytes 524320 | tf_op jit(solution)/shard_map/ppermute | solution.py:82
  37.0 0.9 %pad_maximum_fusion = bf16[4,160,512]{2,1,0:T(8,128)(2,1)} fusion(bf16[1,160,512]{2,1,0:T(8,128)(2,1)S(1)} %fusion.8, bf16[1,160,512]{2,1,0:T(8,128)(2,1)S(1)} %fusion.7, bf16[1,160,512]{2,1,0:T(8,128)(2,1)S(1)} %fusion.6, bf16[1,160,512]{2,1,0:T(8,128)(2,1)S(1)} %fusion.5), kind=kLoop, calls=%fused_computation.27 | loop fusion | flops 983040 | bytes 1310720 | tf_op jit(solution)/shard_map/stack | solution.py:129
  37.9 5.1 %all-to-all-start = ((bf16[8,80,512]{2,1,0:T(8,128)(2,1)}), bf16[8,80,512]{2,1,0:T(8,128)(2,1)S(1)}, u32[]{:S(2)}, u32[]{:S(2)}) async-start(bf16[8,80,512]{2,1,0:T(8,128)(2,1)} %bitcast.14), calls=%async_computation | async-start | bytes 1310720 | tf_op jit(solution)/shard_map/all_to_all | solution.py:140
  43.5 0.8 %fusion.11 = bf16[80,128]{1,0:T(8,128)(2,1)} fusion(f32[80,128]{1,0:T(8,128)S(1)} %copy.27, bf16[80,128]{1,0:T(8,128)(2,1)S(1)} %copy-done.2, bf16[128,128]{1,0:T(8,128)(2,1)S(1)} %copy-done.1, f32[80,128]{1,0:T(8,128)S(1)} %copy.26), kind=kOutput, calls=%fused_computation.22 | convolution fusion | flops 2672640 | bytes 155648 | tf_op jit(solution)/shard_map/dot_general | solution.py:38
  44.2 16.9 %all-to-all-done = bf16[8,80,512]{2,1,0:T(8,128)(2,1)S(1)} async-done(((bf16[8,80,512]{2,1,0:T(8,128)(2,1)}), bf16[8,80,512]{2,1,0:T(8,128)(2,1)S(1)}, u32[]{:S(2)}, u32[]{:S(2)}) %all-to-all-start) | async-done | bytes 655392 | tf_op jit(solution)/shard_map/all_to_all | solution.py:140
  61.4 0.7 %copy.28 = bf16[10,8,2,512]{3,1,2,0:T(8,128)(2,1)} copy(bf16[10,8,2,512]{3,2,1,0:T(2,128)(2,1)S(1)} %bitcast.63) | data formatting | bytes 327680
  (64 shorter events, 6.2 us)
Async XLA Ops:
  0.6 18.5 %copy-start = (bf16[512,512]{1,0:T(8,128)(2,1)S(1)}, bf16[512,512]{1,0:T(8,128)(2,1)}, u32[]{:S(2)}) copy-start(bf16[512,512]{1,0:T(8,128)(2,1)} %param.12) | copy-start | bytes 1572868
  4.3 14.8 %collective-permute-start = (bf16[160,256]{1,0:T(8,128)(2,1)}, bf16[160,256]{1,0:T(8,128)(2,1)}, u32[]{:S(2)}, u32[]{:S(2)}) collective-permute-start(bf16[160,256]{1,0:T(8,128)(2,1)} %slice.80), channel_id=1, source_target_pairs={{0,2},{2,4},{4,6},{6,0},{1,3},{3,5},{5,7},{7,1},{8,10},{10,12},{12... | collective-permute-start | bytes 245768 | tf_op jit(solution)/shard_map/ppermute | solution.py:71
  7.2 12.0 %collective-permute-start.1 = (bf16[160,256]{1,0:T(8,128)(2,1)}, bf16[160,256]{1,0:T(8,128)(2,1)}, u32[]{:S(2)}, u32[]{:S(2)}) collective-permute-start(bf16[160,256]{1,0:T(8,128)(2,1)} %slice.80), channel_id=1, source_target_pairs={{0,4},{2,6},{4,0},{6,2},{1,5},{3,7},{5,1},{7,3},{8,12},{10,14},{12... | collective-permute-start | bytes 245768 | tf_op jit(solution)/shard_map/ppermute | solution.py:71
  8.7 10.5 %collective-permute-start.2 = (bf16[160,256]{1,0:T(8,128)(2,1)}, bf16[160,256]{1,0:T(8,128)(2,1)}, u32[]{:S(2)}, u32[]{:S(2)}) collective-permute-start(bf16[160,256]{1,0:T(8,128)(2,1)} %slice.80), channel_id=1, source_target_pairs={{0,6},{2,0},{4,2},{6,4},{1,7},{3,1},{5,3},{7,5},{8,14},{10,8},{12,... | collective-permute-start | bytes 245768 | tf_op jit(solution)/shard_map/ppermute | solution.py:71
  10.1 15.3 %collective-permute-start.3 = (bf16[512,512]{1,0:T(8,128)(2,1)}, bf16[512,512]{1,0:T(8,128)(2,1)S(1)}, u32[]{:S(2)}, u32[]{:S(2)}) collective-permute-start(bf16[512,512]{1,0:T(8,128)(2,1)} %param.12), channel_id=1, source_target_pairs={{0,6},{2,0},{4,2},{6,4},{1,7},{3,1},{5,3},{7,5},{8,14},{10,8},{12,... | collective-permute-start | bytes 1572872 | tf_op jit(solution)/shard_map/ppermute | solution.py:82
  10.7 14.8 %collective-permute-start.4 = (bf16[512,512]{1,0:T(8,128)(2,1)}, bf16[512,512]{1,0:T(8,128)(2,1)S(1)}, u32[]{:S(2)}, u32[]{:S(2)}) collective-permute-start(bf16[512,512]{1,0:T(8,128)(2,1)} %param.12), channel_id=1, source_target_pairs={{0,4},{2,6},{4,0},{6,2},{1,5},{3,7},{5,1},{7,3},{8,12},{10,14},{12... | collective-permute-start | bytes 1572872 | tf_op jit(solution)/shard_map/ppermute | solution.py:82
  13.1 0.5 copy-start.3
  19.2 16.2 %collective-permute-start.5 = (bf16[512,512]{1,0:T(8,128)(2,1)S(1)}, bf16[512,512]{1,0:T(8,128)(2,1)S(1)}, u32[]{:S(2)}, u32[]{:S(2)}) collective-permute-start(bf16[512,512]{1,0:T(8,128)(2,1)S(1)} %copy-done), channel_id=1, source_target_pairs={{0,2},{2,4},{4,6},{6,0},{1,3},{3,5},{5,7},{7,1},{8,10},{10,12},{12... | collective-permute-start | bytes 1572872 | tf_op jit(solution)/shard_map/ppermute | solution.py:82
  35.6 7.4 %copy-start.4 = (s32[5]{0:T(128)S(1)}, s32[5]{0:T(128)}, u32[]{:S(2)}) copy-start(s32[5]{0:T(128)} %copy-done.3) | copy-start | bytes 64
  35.6 7.9 %copy-start.1 = (bf16[128,128]{1,0:T(8,128)(2,1)S(1)}, bf16[128,128]{1,0:T(8,128)(2,1)}, u32[]{:S(2)}) copy-start(bf16[128,128]{1,0:T(8,128)(2,1)} %constant.63.clone) | copy-start | bytes 98308
  35.6 7.9 %copy-start.2 = (bf16[80,128]{1,0:T(8,128)(2,1)S(1)}, bf16[80,128]{1,0:T(8,128)(2,1)}, u32[]{:S(2)}) copy-start(bf16[80,128]{1,0:T(8,128)(2,1)} %param.9) | copy-start | bytes 61444
  37.9 23.2 %all-to-all-start = ((bf16[8,80,512]{2,1,0:T(8,128)(2,1)}), bf16[8,80,512]{2,1,0:T(8,128)(2,1)S(1)}, u32[]{:S(2)}, u32[]{:S(2)}) async-start(bf16[8,80,512]{2,1,0:T(8,128)(2,1)} %bitcast.14), calls=%async_computation | async-start | bytes 1310720 | tf_op jit(solution)/shard_map/all_to_all | solution.py:140

commit v12 on v8

--- a/solution.py
+++ b/solution.py
@@ -65,14 +65,21 @@
     chip_kv = chip_rows[:, width:]
     out_weight, chip_kv = lax.optimization_barrier((out_weight, chip_kv))
     if chips <= 8:
-        kv_pair = jnp.concatenate(
-            [chip_kv]
-            + [
-                lax.ppermute(chip_kv, "chip", [(i, (i + s) % chips) for i in range(chips)])
-                for s in range(1, chips)
-            ],
-            axis=0,
-        )
+        reach = chips // 2
+        mine = [list(range(1, reach + 1)), [chips - p for p in range(1, reach + 1)]]
+        got = []
+        for p in range(reach):
+            pairs = []
+            for i in range(chips):
+                for k in range(cores):
+                    pairs.append((i * cores + k, ((i + mine[k][p]) % chips) * cores + k))
+            got.append(lax.ppermute(chip_kv, BLK, pairs))
+        both = lax.all_gather(jnp.stack(got, 0), "core", axis=0, tiled=False)
+        pieces = {0: chip_kv}
+        for k in range(cores):
+            for p in range(reach):
+                pieces.setdefault(mine[k][p], both[k, p])
+        kv_pair = jnp.concatenate([pieces[s] for s in range(chips)], axis=0)
         src_chip = (lax.axis_index("chip") - jnp.arange(chips)) % chips
     else:
         kv_pair = lax.all_gather(chip_kv, "chip", axis=0, tiled=True)
@@ -108,6 +115,7 @@
     key_piece = rotate_flat(kv_pair[:, :head_size], key_idx - key_off, head_size).astype(
         jnp.bfloat16
     )
+    key_piece, value_piece = lax.optimization_barrier((key_piece, value_piece))
     live = (key_seg[None, :] == row_seg[:, None]) & (key_idx[None, :] <= row_idx[:, None])
     scores = (
         jnp.einsum("rd,nd->rn", query_rows, key_piece, preferred_element_type=jnp.float32) * scale

time: 61.8 us -> 62.6 us (1.013)
  matrix products: 8.3 us -> 5.56 us
  waiting for transfers between devices: 26 us -> 28.3 us
  blocking collectives: 2.07 us -> 4.12 us
  starting transfers between devices: 13 us -> 11.9 us
  other arithmetic: 6.18 us -> 7.17 us
  local copies, waits for them, and re-layouts: 5 us -> 4.14 us
    ppermute x3, waiting for transfers between devices: 9.04 us -> 11.4 us  [body(): lax.ppermute(out_weight, 'chip', [(i, (i + s) % chips) for i in range(chi...]
    dot_general x1, matrix products: 2.81 us -> 0.55 us  [body(): jnp.einsum('rd,nd->rn', query_rows, key_piece, preferred_element_type=jnp...]
    all_gather x0 -> x1, blocking collectives: none -> 2.04 us  [body(): both = lax.all_gather(jnp.stack(got, 0), 'core', axis=0, tiled=False)]
    unnamed x17 -> x18, local copies, waits for them, and re-layouts: 2.87 us -> 1.29 us
    ppermute x3 -> x2, starting transfers between devices: 5.85 us -> 4.37 us  [body(): got.append(lax.ppermute(chip_kv, BLK, pairs))]
    dot_general x1, matrix products: 2.12 us -> 0.69 us  [body(): jnp.dot(probs.astype(jnp.bfloat16), value_piece, preferred_element_type=j...]
    reduce_sum x1, other arithmetic: 1.89 us -> 0.47 us  [body(): new_sum = jnp.sum(probs, axis=1)]
    dot_general x2 -> x3, matrix products: 2.05 us -> 3 us  [rotate_flat(): jnp.dot(field, half_swap(field.shape[1], head_size), preferred_element_ty...]
  transfers between devices with their start and end apart: 7 -> 6, of which waited for: 2 -> 2; matrix products, arithmetic and copies ran while one was open for 25% -> 19% of each run, Pallas kernels for 0% -> 0%
where the time goes in v12:
time: 62.6 us; the launch traced here: 62.2 us
  waiting for transfers between devices  28.3 us (45%)
  starting transfers between devices  11.9 us (19%)
  other arithmetic  7.17 us (11%)
  matrix products  5.56 us (9%)
  local copies, waits for them, and re-layouts  4.14 us (7%)
  blocking collectives  4.12 us (7%)
  between operations  0.99 us (2%)
    all_to_all x1, waiting for transfers between devices, body(): got = lax.all_to_all(routed, ('kv', 'core'), 0, 0, tiled=True)  16.9 us
    ppermute x3, waiting for transfers between devices, body(): lax.ppermute(out_weight, 'chip', [(i, (i + s) % chips) for i in range(chi...  11.4 us
    all_to_all x1, starting transfers between devices, body(): got = lax.all_to_all(routed, ('kv', 'core'), 0, 0, tiled=True)  5.01 us
    ppermute x2, starting transfers between devices, body(): got.append(lax.ppermute(chip_kv, BLK, pairs))  4.37 us
    dot_general x3, matrix products, rotate_flat(): jnp.dot(field, half_swap(field.shape[1], head_size), preferred_element_ty...  3 us
    ppermute x3, starting transfers between devices, body(): lax.ppermute(out_weight, 'chip', [(i, (i + s) % chips) for i in range(chi...  2.53 us
    all_gather x1, blocking collectives, body(): lax.all_gather(jnp.concatenate([queries, keys, values], axis=1), 'core',...  2.07 us
    all_gather x1, blocking collectives, body(): both = lax.all_gather(jnp.stack(got, 0), 'core', axis=0, tiled=False)  2.04 us
  transfers between devices with their start and end apart: 6, of which 2 were waited for; matrix products, arithmetic and copies ran while one was open for 19% of the time, Pallas kernels for 0%

profile of v12, /device:TPU:0, one launch (start us, length us, event | category | flops | bytes accessed | tf_op | source)
XLA Modules:
  0.0 62.2 jit_solution(15440160315776530208)
XLA Ops:
  0.6 0.9 %pad_maximum_fusion.4 = bf16[80,768]{1,0:T(8,128)(2,1)S(1)} fusion(bf16[80,128]{1,0:T(8,128)(2,1)} %param.10, bf16[80,128]{1,0:T(8,128)(2,1)} %param.9, bf16[80,512]{1,0:T(8,128)(2,1)} %param.8), kind=kLoop, calls=%fused_computation.54 | loop fusion | flops 368640 | bytes 245760 | tf_op jit(solution)/shard_map/concatenate | solution.py:63
  1.6 2.1 %all_gather.9 = bf16[160,768]{1,0:T(8,128)(2,1)S(1)} all-gather(bf16[80,768]{1,0:T(8,128)(2,1)S(1)} %pad_maximum_fusion.4), channel_id=1, replica_groups=mesh['kv'=4,'chip'=4,'core'=2] {'core'}, dimensions={0}, use_global_device_ids=true | all-gather | bytes 368640 | tf_op jit(solution)/shard_map/all_gather | solution.py:62
  3.6 0.6 %slice.97 = bf16[160,256]{1,0:T(8,128)(2,1)} slice(bf16[160,768]{1,0:T(8,128)(2,1)S(1)} %all_gather.9), slice={[0:160], [512:768]} | slice | bytes 163840 | tf_op jit(solution)/shard_map/slice | solution.py:65
  4.3 2.8 %collective-permute-start = (bf16[160,256]{1,0:T(8,128)(2,1)}, bf16[160,256]{1,0:T(8,128)(2,1)}, u32[]{:S(2)}, u32[]{:S(2)}) collective-permute-start(bf16[160,256]{1,0:T(8,128)(2,1)} %slice.97), channel_id=1, source_target_pairs={{0,2},{1,7},{2,4},{3,1},{4,6},{5,3},{6,0},{7,5},{8,10},{9,15},{10,... | collective-permute-start | bytes 245768 | tf_op jit(solution)/shard_map/ppermute | solution.py:76
  7.1 1.5 %collective-permute-start.1 = (bf16[160,256]{1,0:T(8,128)(2,1)}, bf16[160,256]{1,0:T(8,128)(2,1)}, u32[]{:S(2)}, u32[]{:S(2)}) collective-permute-start(bf16[160,256]{1,0:T(8,128)(2,1)} %slice.97), channel_id=1, source_target_pairs={{0,4},{1,5},{2,6},{3,7},{4,0},{5,1},{6,2},{7,3},{8,12},{9,13},{10,... | collective-permute-start | bytes 245768 | tf_op jit(solution)/shard_map/ppermute | solution.py:76
  8.7 1.4 %collective-permute-start.2 = (bf16[512,512]{1,0:T(8,128)(2,1)}, bf16[512,512]{1,0:T(8,128)(2,1)S(1)}, u32[]{:S(2)}, u32[]{:S(2)}) collective-permute-start(bf16[512,512]{1,0:T(8,128)(2,1)} %param.12), channel_id=1, source_target_pairs={{0,6},{2,0},{4,2},{6,4},{1,7},{3,1},{5,3},{7,5},{8,14},{10,8},{12,... | collective-permute-start | bytes 1572872 | tf_op jit(solution)/shard_map/ppermute | solution.py:89
  10.1 1.1 %collective-permute-start.4 = (bf16[512,512]{1,0:T(8,128)(2,1)}, bf16[512,512]{1,0:T(8,128)(2,1)S(1)}, u32[]{:S(2)}, u32[]{:S(2)}) collective-permute-start(bf16[512,512]{1,0:T(8,128)(2,1)} %param.12), channel_id=1, source_target_pairs={{0,2},{2,4},{4,6},{6,0},{1,3},{3,5},{5,7},{7,1},{8,10},{10,12},{12... | collective-permute-start | bytes 1572872 | tf_op jit(solution)/shard_map/ppermute | solution.py:89
  11.4 0.7 %select_reduce_fusion.1 = s32[5]{0:T(128)S(1)} fusion(s32[4]{0:T(128)} %param.11, s32[5]{0:T(128)S(1)} %iota_add_fusion.3), kind=kLoop, calls=%fused_computation.76 | loop fusion | flops 55 | bytes 56 | tf_op jit(solution)/shard_map/reduce_sum | solution.py:53
  12.6 0.6 %multiply_cosine_fusion = (f32[640,64]{0,1:T(8,128)S(1)}, f32[640,64]{0,1:T(8,128)S(1)}) fusion(f32[64]{0:T(128)S(1)} %negate_power_fusion, f32[640]{0:T(1024)S(1)} %get-tuple-element.33), kind=kLoop, calls=%fused_computation.42 | loop fusion | flops 40960 | bytes 330496 | tf_op jit(solution)/shard_map/cos | solution.py:36
  13.3 0.6 subtract_convert_fusion.1
  14.7 1.3 %fusion.4 = bf16[160,512]{1,0:T(8,128)(2,1)S(1)} fusion(f32[160,512]{1,0:T(8,128)S(1)} %tile.33, bf16[512,512]{1,0:T(8,128)(2,1)} %constant.64.clone, f32[160,512]{1,0:T(8,128)S(1)} %tile.31, bf16[160,768]{1,0:T(8,128)(2,1)S(1)} %all_gather.9), kind=kOutput, calls=%fused_computation.14 | convolution fusion | flops 84295680 | bytes 1671168 | tf_op jit(solution)/shard_map/dot_general | solution.py:38
  16.4 0.7 %tile.28 = s32[4,160]{1,0:T(4,128)S(1)} broadcast(s32[160]{0:T(256)} %get-tuple-element.36), dimensions={1} | broadcast | bytes 3200 | tf_op jit(solution)/shard_map/tile | solution.py:108
  17.3 0.9 %pad_maximum_fusion.2 = bf16[2,160,256]{2,1,0:T(8,128)(2,1)S(1)} fusion(bf16[1,160,256]{2,1,0:T(8,128)(2,1)} %bitcast.1, bf16[1,160,256]{2,1,0:T(8,128)(2,1)} %bitcast), kind=kLoop, calls=%fused_computation.52 | loop fusion | flops 81920 | bytes 327680 | tf_op jit(solution)/shard_map/stack | solution.py:77
  18.3 2.0 %all-gather = bf16[4,160,256]{2,1,0:T(8,128)(2,1)S(1)} all-gather(bf16[2,160,256]{2,1,0:T(8,128)(2,1)S(1)} %pad_maximum_fusion.2), channel_id=2, replica_groups=mesh['kv'=4,'chip'=4,'core'=2] {'core'}, dimensions={0}, use_global_device_ids=true | all-gather | bytes 491520 | tf_op jit(solution)/shard_map/all_gather | solution.py:77
  20.3 0.9 %pad_maximum_fusion.1 = bf16[640,256]{1,0:T(8,128)(2,1)S(1)} fusion(bf16[160,256]{1,0:T(8,128)(2,1)S(1)} %get-tuple-element.15, bf16[160,256]{1,0:T(8,128)(2,1)S(1)} %get-tuple-element.16, bf16[160,256]{1,0:T(8,128)(2,1)S(1)} %get-tuple-element.14, bf16[160,256]{1,0:T(8,128)(2,1)} %slice.97), kind=kLoop, calls=%fused_computation.40 | loop fusion | flops 1310720 | bytes 655360 | tf_op jit(solution)/shard_map/concatenate | solution.py:82
  21.3 1.0 %fusion.2 = bf16[640,128]{1,0:T(8,128)(2,1)S(1)} fusion(f32[640,128]{1,0:T(8,128)S(1)} %copy.24, bf16[128,128]{1,0:T(8,128)(2,1)} %constant.63.clone, f32[640,128]{1,0:T(8,128)S(1)} %copy.23, bf16[640,256]{1,0:T(8,128)(2,1)S(1)} %pad_maximum_fusion.1), kind=kOutput, calls=%fused_computation.8 | convolution fusion | flops 21381120 | bytes 1179648 | tf_op jit(solution)/shard_map/dot_general | solution.py:38
  22.2 0.6 fusion.40
  23.3 0.7 %fusion.3 = bf16[640,128]{1,0:T(8,128)(2,1)S(1)} fusion(bf16[640,128]{1,0:T(8,128)(2,1)S(1)} %slice.102, f32[640,640]{0,1:T(8,128)S(1)} %get-tuple-element.32, f32[640]{0:T(1024)S(1)} %get-tuple-element.31, s32[640]{0:T(1024)S(1)} %le.61, s32[640]{0:T(1024)S(1)} %eq.26, s32[640]{0:T(1024)S(1)} %add.104, s32[640]{0:T(1024)S(1)} %get-tuple-element.34, ...), kind=kOutput, calls=%fused_computation.13 | convolution fusion | flops 107479040 | bytes 1981440 | tf_op jit(solution)/shard_map/dot_general | solution.py:127
  24.0 11.4 %collective-permute-done.3 = bf16[512,512]{1,0:T(8,128)(2,1)S(1)} collective-permute-done((bf16[512,512]{1,0:T(8,128)(2,1)}, bf16[512,512]{1,0:T(8,128)(2,1)S(1)}, u32[]{:S(2)}, u32[]{:S(2)}) %collective-permute-start.3) | collective-permute-done | bytes 524320 | tf_op jit(solution)/shard_map/ppermute | solution.py:89
  37.1 0.9 %pad_maximum_fusion = bf16[4,160,512]{2,1,0:T(8,128)(2,1)} fusion(bf16[1,160,512]{2,1,0:T(8,128)(2,1)S(1)} %fusion.8, bf16[1,160,512]{2,1,0:T(8,128)(2,1)S(1)} %fusion.7, bf16[1,160,512]{2,1,0:T(8,128)(2,1)S(1)} %fusion.6, bf16[1,160,512]{2,1,0:T(8,128)(2,1)S(1)} %fusion.5), kind=kLoop, calls=%fused_computation.27 | loop fusion | flops 983040 | bytes 1310720 | tf_op jit(solution)/shard_map/stack | solution.py:136
  38.0 5.0 %all-to-all-start = ((bf16[8,80,512]{2,1,0:T(8,128)(2,1)}), bf16[8,80,512]{2,1,0:T(8,128)(2,1)S(1)}, u32[]{:S(2)}, u32[]{:S(2)}) async-start(bf16[8,80,512]{2,1,0:T(8,128)(2,1)} %bitcast.20), calls=%async_computation | async-start | bytes 1310720 | tf_op jit(solution)/shard_map/all_to_all | solution.py:147
  43.6 0.8 %fusion.11 = bf16[80,128]{1,0:T(8,128)(2,1)} fusion(f32[80,128]{1,0:T(8,128)S(1)} %copy.27, bf16[80,128]{1,0:T(8,128)(2,1)S(1)} %copy-done.2, bf16[128,128]{1,0:T(8,128)(2,1)S(1)} %copy-done.1, f32[80,128]{1,0:T(8,128)S(1)} %copy.26), kind=kOutput, calls=%fused_computation.22 | convolution fusion | flops 2672640 | bytes 155648 | tf_op jit(solution)/shard_map/dot_general | solution.py:38
  44.3 16.9 %all-to-all-done = bf16[8,80,512]{2,1,0:T(8,128)(2,1)S(1)} async-done(((bf16[8,80,512]{2,1,0:T(8,128)(2,1)}), bf16[8,80,512]{2,1,0:T(8,128)(2,1)S(1)}, u32[]{:S(2)}, u32[]{:S(2)}) %all-to-all-start) | async-done | bytes 655392 | tf_op jit(solution)/shard_map/all_to_all | solution.py:147
  61.5 0.7 %copy.28 = bf16[10,8,2,512]{3,1,2,0:T(8,128)(2,1)} copy(bf16[10,8,2,512]{3,2,1,0:T(2,128)(2,1)S(1)} %bitcast.72) | data formatting | bytes 327680
  (64 shorter events, 5.0 us)
Async XLA Ops:
  4.3 13.0 %collective-permute-start = (bf16[160,256]{1,0:T(8,128)(2,1)}, bf16[160,256]{1,0:T(8,128)(2,1)}, u32[]{:S(2)}, u32[]{:S(2)}) collective-permute-start(bf16[160,256]{1,0:T(8,128)(2,1)} %slice.97), channel_id=1, source_target_pairs={{0,2},{1,7},{2,4},{3,1},{4,6},{5,3},{6,0},{7,5},{8,10},{9,15},{10,... | collective-permute-start | bytes 245768 | tf_op jit(solution)/shard_map/ppermute | solution.py:76
  7.1 10.2 %collective-permute-start.1 = (bf16[160,256]{1,0:T(8,128)(2,1)}, bf16[160,256]{1,0:T(8,128)(2,1)}, u32[]{:S(2)}, u32[]{:S(2)}) collective-permute-start(bf16[160,256]{1,0:T(8,128)(2,1)} %slice.97), channel_id=1, source_target_pairs={{0,4},{1,5},{2,6},{3,7},{4,0},{5,1},{6,2},{7,3},{8,12},{9,13},{10,... | collective-permute-start | bytes 245768 | tf_op jit(solution)/shard_map/ppermute | solution.py:76
  8.7 15.3 %collective-permute-start.2 = (bf16[512,512]{1,0:T(8,128)(2,1)}, bf16[512,512]{1,0:T(8,128)(2,1)S(1)}, u32[]{:S(2)}, u32[]{:S(2)}) collective-permute-start(bf16[512,512]{1,0:T(8,128)(2,1)} %param.12), channel_id=1, source_target_pairs={{0,6},{2,0},{4,2},{6,4},{1,7},{3,1},{5,3},{7,5},{8,14},{10,8},{12,... | collective-permute-start | bytes 1572872 | tf_op jit(solution)/shard_map/ppermute | solution.py:89
  10.1 25.3 %collective-permute-start.3 = (bf16[512,512]{1,0:T(8,128)(2,1)}, bf16[512,512]{1,0:T(8,128)(2,1)S(1)}, u32[]{:S(2)}, u32[]{:S(2)}) collective-permute-start(bf16[512,512]{1,0:T(8,128)(2,1)} %param.12), channel_id=1, source_target_pairs={{0,4},{2,6},{4,0},{6,2},{1,5},{3,7},{5,1},{7,3},{8,12},{10,14},{12... | collective-permute-start | bytes 1572872 | tf_op jit(solution)/shard_map/ppermute | solution.py:89
  10.1 25.3 %collective-permute-start.4 = (bf16[512,512]{1,0:T(8,128)(2,1)}, bf16[512,512]{1,0:T(8,128)(2,1)S(1)}, u32[]{:S(2)}, u32[]{:S(2)}) collective-permute-start(bf16[512,512]{1,0:T(8,128)(2,1)} %param.12), channel_id=1, source_target_pairs={{0,2},{2,4},{4,6},{6,0},{1,3},{3,5},{5,7},{7,1},{8,10},{10,12},{12... | collective-permute-start | bytes 1572872 | tf_op jit(solution)/shard_map/ppermute | solution.py:89
  12.1 0.5 copy-start.3
  23.2 12.3 %copy-start = (bf16[512,512]{1,0:T(8,128)(2,1)S(1)}, bf16[512,512]{1,0:T(8,128)(2,1)}, u32[]{:S(2)}) copy-start(bf16[512,512]{1,0:T(8,128)(2,1)} %param.12) | copy-start | bytes 1572868
  35.7 7.4 %copy-start.4 = (s32[5]{0:T(128)S(1)}, s32[5]{0:T(128)}, u32[]{:S(2)}) copy-start(s32[5]{0:T(128)} %copy-done.3) | copy-start | bytes 64
  35.7 7.8 %copy-start.1 = (bf16[128,128]{1,0:T(8,128)(2,1)S(1)}, bf16[128,128]{1,0:T(8,128)(2,1)}, u32[]{:S(2)}) copy-start(bf16[128,128]{1,0:T(8,128)(2,1)} %constant.63.clone) | copy-start | bytes 98308
  35.7 7.8 %copy-start.2 = (bf16[80,128]{1,0:T(8,128)(2,1)S(1)}, bf16[80,128]{1,0:T(8,128)(2,1)}, u32[]{:S(2)}) copy-start(bf16[80,128]{1,0:T(8,128)(2,1)} %param.9) | copy-start | bytes 61444
  38.0 23.2 %all-to-all-start = ((bf16[8,80,512]{2,1,0:T(8,128)(2,1)}), bf16[8,80,512]{2,1,0:T(8,128)(2,1)S(1)}, u32[]{:S(2)}, u32[]{:S(2)}) async-start(bf16[8,80,512]{2,1,0:T(8,128)(2,1)} %bitcast.20), calls=%async_computation | async-start | bytes 1310720 | tf_op jit(solution)/shard_map/all_to_all | solution.py:147

commit v13 on v7

--- a/solution.py
+++ b/solution.py
@@ -122,26 +122,28 @@
     )
     kvs = lax.axis_size("kv")
     per_c = w_share.shape[0] // kvs
-    routed = jnp.stack(
-        [
-            jnp.dot(
-                chip_att,
-                w_share[c * per_c:(c + 1) * per_c].T,
-                preferred_element_type=jnp.float32,
-            ).astype(jnp.bfloat16)
-            for c in range(kvs)
-        ],
-        axis=0,
-    ).reshape(kvs * cores, tok_rows, per_c)
+    routed = (
+        jnp.einsum(
+            "ctk,cnk->ctn",
+            jnp.broadcast_to(chip_att, (kvs,) + chip_att.shape),
+            w_share.reshape(kvs, per_c, w_share.shape[1]),
+            preferred_element_type=jnp.float32,
+        )
+        .astype(jnp.bfloat16)
+        .reshape(kvs * cores, tok_rows, per_c)
+    )
     got = lax.all_to_all(routed, ("kv", "core"), 0, 0, tiled=True)
     total = jnp.sum(got.reshape(kvs, cores, tok_rows, per_c).astype(jnp.float32), axis=0)
     rows = out_weight.shape[0]
-    hidden = (
-        total.reshape(cores, tok_rows, per_c // rows, rows)
-        .transpose(1, 2, 0, 3)
-        .reshape(tok_rows, cores * per_c)
-        .astype(jnp.bfloat16)
-    )
+    if per_c == rows:
+        hidden = jnp.concatenate([total[k] for k in range(cores)], axis=1).astype(jnp.bfloat16)
+    else:
+        hidden = (
+            total.reshape(cores, tok_rows, per_c // rows, rows)
+            .transpose(1, 2, 0, 3)
+            .reshape(tok_rows, cores * per_c)
+            .astype(jnp.bfloat16)
+        )
     return (hidden, rot_keys)
 
 

time: 60.7 us -> 59.9 us (0.987)
  waiting for transfers between devices: 14.5 us -> 17 us
  matrix products: 4.79 us -> 2.44 us
  local copies, waits for them, and re-layouts: 2.08 us -> 1.27 us
    ppermute x3, waiting for transfers between devices: 14.4 us -> 17 us  [body(): lax.ppermute(chip_kv, 'chip', [(i, (i + s) % chips) for i in range(chips)])]
    dot_general x2, matrix products: 2.23 us -> 0.35 us  [rotate_flat(): jnp.dot(field, half_swap(field.shape[1], head_size), preferred_element_ty...]
    concatenate x1, other arithmetic: 0.74 us -> 0.01 us  [body(): jnp.concatenate([rot_queries, rot_keys, values], axis=1)]
    concatenate x0 -> x2, other arithmetic: none -> 0.7 us  [the longest x1 0.68 us: body(): jnp.concatenate([total[k] for k in range(cores)], axis=1)]
    unnamed x12 -> x21, local copies, waits for them, and re-layouts: 0.95 us -> 0.3 us
    dot_general x4 -> x1, matrix products: 1.32 us -> 0.84 us  [body(): jnp.einsum('ctk,cnk->ctn', jnp.broadcast_to(chip_att, (kvs,) + chip_att.s...]
  transfers between devices with their start and end apart: 6 -> 6, of which waited for: 2 -> 2; matrix products, arithmetic and copies ran while one was open for 12% -> 7% of each run, Pallas kernels for 0% -> 0%
where the time goes in v13:
time: 59.9 us; the launch traced here: 59.7 us
  blocking collectives  24.8 us (41%)
  waiting for transfers between devices  17 us (28%)
  starting transfers between devices  10.5 us (18%)
  other arithmetic  2.61 us (4%)
  matrix products  2.44 us (4%)
  local copies, waits for them, and re-layouts  1.27 us (2%)
  between operations  1.04 us (2%)
    all_to_all x1, blocking collectives, body(): got = lax.all_to_all(routed, ('kv', 'core'), 0, 0, tiled=True)  22.8 us
    ppermute x3, waiting for transfers between devices, body(): lax.ppermute(chip_kv, 'chip', [(i, (i + s) % chips) for i in range(chips)])  17 us
    ppermute x3, starting transfers between devices, body(): lax.ppermute(out_weight, 'chip', [(i, (i + s) % chips) for i in range(chi...  6.9 us
    ppermute x3, starting transfers between devices, body(): lax.ppermute(chip_kv, 'chip', [(i, (i + s) % chips) for i in range(chips)])  3.59 us
    all_gather x1, blocking collectives, body(): lax.all_gather(jnp.concatenate([rot_queries, rot_keys, values], axis=1),...  1.98 us
  transfers between devices with their start and end apart: 6, of which 2 were waited for; matrix products, arithmetic and copies ran while one was open for 7% of the time, Pallas kernels for 0%

profile of v13, /device:TPU:0, one launch (start us, length us, event | category | flops | bytes accessed | tf_op | source)
XLA Modules:
  0.0 59.7 jit_solution(4415469854756031407)
XLA Ops:
  0.7 3.9 %collective-permute-start.3 = (bf16[512,512]{1,0:T(8,128)(2,1)}, bf16[512,512]{1,0:T(8,128)(2,1)S(1)}, u32[]{:S(2)}, u32[]{:S(2)}) collective-permute-start(bf16[512,512]{1,0:T(8,128)(2,1)} %param.11), channel_id=1, source_target_pairs={{0,6},{2,0},{4,2},{6,4},{1,7},{3,1},{5,3},{7,5},{8,14},{10,8},{12,... | collective-permute-start | bytes 1572872 | tf_op jit(solution)/shard_map/ppermute | solution.py:62
  4.6 0.5 collective-permute-start.4
  5.1 0.7 %select_reduce_fusion.1 = s32[5]{0:T(128)S(1)} fusion(s32[4]{0:T(128)} %param.10, s32[5]{0:T(128)S(1)} %iota_add_fusion.3), kind=kLoop, calls=%fused_computation.53 | loop fusion | flops 55 | bytes 56 | tf_op jit(solution)/shard_map/reduce_sum | solution.py:53
  5.9 0.1 select_reduce_fusion
  6.0 0.2 multiply_cosine_fusion
  6.6 0.1 tile.25
  6.8 0.1 tile.23
  6.9 0.1 fusion.11
  7.1 0.2 fusion.8
  7.4 2.0 %all_gather.3 = bf16[160,768]{1,0:T(8,128)(2,1)S(1)} all-gather(bf16[80,768]{1,0:T(8,128)(2,1)S(1)} %pad_maximum_fusion.3), channel_id=1, replica_groups=mesh['kv'=4,'chip'=4,'core'=2] {'core'}, dimensions={0}, use_global_device_ids=true | all-gather | bytes 368640 | tf_op jit(solution)/shard_map/all_gather | solution.py:75
  9.4 0.1 collective-permute-start.2
  9.5 2.0 %collective-permute-start.1 = (bf16[160,256]{1,0:T(8,128)(2,1)S(1)}, bf16[160,256]{1,0:T(8,128)(2,1)S(1)}, u32[]{:S(2)}, u32[]{:S(2)}) collective-permute-start(bf16[160,256]{1,0:T(8,128)(2,1)S(1)} %slice.63), channel_id=1, source_target_pairs={{0,4},{2,6},{4,0},{6,2},{1,5},{3,7},{5,1},{7,3},{8,12},{10,14},{12... | collective-permute-start | bytes 245768 | tf_op jit(solution)/shard_map/ppermute | solution.py:83
  11.5 1.5 %collective-permute-start = (bf16[160,256]{1,0:T(8,128)(2,1)S(1)}, bf16[160,256]{1,0:T(8,128)(2,1)S(1)}, u32[]{:S(2)}, u32[]{:S(2)}) collective-permute-start(bf16[160,256]{1,0:T(8,128)(2,1)S(1)} %slice.63), channel_id=1, source_target_pairs={{0,2},{2,4},{4,6},{6,0},{1,3},{3,5},{5,7},{7,1},{8,10},{10,12},{12... | collective-permute-start | bytes 245768 | tf_op jit(solution)/shard_map/ppermute | solution.py:83
  13.2 0.1 convert_reduce_fusion.1
  13.5 5.2 %collective-permute-done.2 = bf16[160,256]{1,0:T(8,128)(2,1)S(1)} collective-permute-done((bf16[160,256]{1,0:T(8,128)(2,1)S(1)}, bf16[160,256]{1,0:T(8,128)(2,1)S(1)}, u32[]{:S(2)}, u32[]{:S(2)}) %collective-permute-start.2) | collective-permute-done | bytes 81952 | tf_op jit(solution)/shard_map/ppermute | solution.py:83
  18.7 2.4 %collective-permute-start.5 = (bf16[512,512]{1,0:T(8,128)(2,1)S(1)}, bf16[512,512]{1,0:T(8,128)(2,1)S(1)}, u32[]{:S(2)}, u32[]{:S(2)}) collective-permute-start(bf16[512,512]{1,0:T(8,128)(2,1)S(1)} %copy-done), channel_id=1, source_target_pairs={{0,2},{2,4},{4,6},{6,0},{1,3},{3,5},{5,7},{7,1},{8,10},{10,12},{12... | collective-permute-start | bytes 1572872 | tf_op jit(solution)/shard_map/ppermute | solution.py:62
  21.1 11.8 %collective-permute-done.1 = bf16[160,256]{1,0:T(8,128)(2,1)S(1)} collective-permute-done((bf16[160,256]{1,0:T(8,128)(2,1)S(1)}, bf16[160,256]{1,0:T(8,128)(2,1)S(1)}, u32[]{:S(2)}, u32[]{:S(2)}) %collective-permute-start.1) | collective-permute-done | bytes 81952 | tf_op jit(solution)/shard_map/ppermute | solution.py:83
  33.0 0.6 fusion.34
  33.6 0.5 fusion.12
  34.0 0.7 %fusion.5 = bf16[640,128]{1,0:T(8,128)(2,1)S(1)} fusion(f32[640,640]{0,1:T(8,128)S(1)} %get-tuple-element.15, f32[640]{0:T(1024)S(1)} %get-tuple-element.14, s32[640]{0:T(1024)S(1)} %le.61, s32[640]{0:T(1024)S(1)} %eq.26, s32[640]{0:T(1024)S(1)} %add.94, s32[640]{0:T(1024)S(1)} %broadcast_add_fusion, bf16[640,256]{1,0:T(8,128)(2,1)S(1)} %pad_maximum_fusion, ...), kind=kOutput, calls=%fused_computation.7 | convolution fusion | flops 107479040 | bytes 1990656 | tf_op jit(solution)/shard_map/dot_general | solution.py:116
  35.2 0.8 %fusion.2 = bf16[4,160,512]{2,1,0:T(8,128)(2,1)S(1)} fusion(bf16[8,512,512]{2,1,0:T(8,128)(2,1)S(1)} %bitcast_dynamic-update-slice_fusion.1, s32[]{:T(128)S(6)} %select_n.43, bf16[160,512]{1,0:T(8,128)(2,1)S(1)} %pad_maximum_fusion.1), kind=kOutput, calls=%fused_computation.5 | convolution fusion | flops 335872000 | bytes 2916356 | tf_op jit(solution)/shard_map/ctk,cnk->ctn/dot_general | solution.py:126
  36.0 22.8 %all_to_all.5 = bf16[8,80,512]{2,1,0:T(8,128)(2,1)S(1)} all-to-all(bf16[8,80,512]{2,1,0:T(8,128)(2,1)S(1)} %bitcast.41), channel_id=1, replica_groups=mesh['kv'=4,'chip'=4,'core'=2] {'kv','core'}, dimensions={0} | all-to-all | bytes 1310720 | tf_op jit(solution)/shard_map/all_to_all | solution.py:135
  58.9 0.1 reduce
  59.0 0.7 %pad_maximum_fusion.2 = bf16[80,1024]{1,0:T(8,128)(2,1)} fusion(bf16[80,512]{1,0:T(8,128)(2,1)S(1)} %get-tuple-element.7, bf16[80,512]{1,0:T(8,128)(2,1)S(1)} %get-tuple-element.6), kind=kLoop, calls=%fused_computation.40 | loop fusion | flops 327680 | bytes 327680 | tf_op jit(solution)/shard_map/concatenate | solution.py:139
  (57 shorter events, 1.3 us)
Async XLA Ops:
  0.6 6.3 %copy-start.4 = (bf16[128,128]{1,0:T(8,128)(2,1)S(1)}, bf16[128,128]{1,0:T(8,128)(2,1)}, u32[]{:S(2)}) copy-start(bf16[128,128]{1,0:T(8,128)(2,1)} %constant.63.clone) | copy-start | bytes 98308
  0.6 6.4 %copy-start.1 = (bf16[512,512]{1,0:T(8,128)(2,1)S(1)}, bf16[512,512]{1,0:T(8,128)(2,1)}, u32[]{:S(2)}) copy-start(bf16[512,512]{1,0:T(8,128)(2,1)} %constant.64.clone) | copy-start | bytes 1572868
  0.7 6.3 %copy-start.5 = (bf16[80,128]{1,0:T(8,128)(2,1)S(1)}, bf16[80,128]{1,0:T(8,128)(2,1)}, u32[]{:S(2)}) copy-start(bf16[80,128]{1,0:T(8,128)(2,1)} %param.8) | copy-start | bytes 61444
  0.7 6.4 %copy-start.3 = (bf16[80,512]{1,0:T(8,128)(2,1)S(1)}, bf16[80,512]{1,0:T(8,128)(2,1)}, u32[]{:S(2)}) copy-start(bf16[80,512]{1,0:T(8,128)(2,1)} %param.7) | copy-start | bytes 245764
  0.7 34.1 %collective-permute-start.3 = (bf16[512,512]{1,0:T(8,128)(2,1)}, bf16[512,512]{1,0:T(8,128)(2,1)S(1)}, u32[]{:S(2)}, u32[]{:S(2)}) collective-permute-start(bf16[512,512]{1,0:T(8,128)(2,1)} %param.11), channel_id=1, source_target_pairs={{0,6},{2,0},{4,2},{6,4},{1,7},{3,1},{5,3},{7,5},{8,14},{10,8},{12,... | collective-permute-start | bytes 1572872 | tf_op jit(solution)/shard_map/ppermute | solution.py:62
  4.6 30.2 %collective-permute-start.4 = (bf16[512,512]{1,0:T(8,128)(2,1)}, bf16[512,512]{1,0:T(8,128)(2,1)S(1)}, u32[]{:S(2)}, u32[]{:S(2)}) collective-permute-start(bf16[512,512]{1,0:T(8,128)(2,1)} %param.11), channel_id=1, source_target_pairs={{0,4},{2,6},{4,0},{6,2},{1,5},{3,7},{5,1},{7,3},{8,12},{10,14},{12... | collective-permute-start | bytes 1572872 | tf_op jit(solution)/shard_map/ppermute | solution.py:62
  6.3 1.0 %copy-start.6 = (bf16[80,128]{1,0:T(8,128)(2,1)S(1)}, bf16[80,128]{1,0:T(8,128)(2,1)}, u32[]{:S(2)}) copy-start(bf16[80,128]{1,0:T(8,128)(2,1)} %param.9) | copy-start | bytes 61444
  6.7 12.0 %copy-start = (bf16[512,512]{1,0:T(8,128)(2,1)S(1)}, bf16[512,512]{1,0:T(8,128)(2,1)}, u32[]{:S(2)}) copy-start(bf16[512,512]{1,0:T(8,128)(2,1)} %param.11) | copy-start | bytes 1572868
  7.1 26.5 %copy-start.2 = (bf16[80,128]{1,0:T(8,128)(2,1)}, bf16[80,128]{1,0:T(8,128)(2,1)S(1)}, u32[]{:S(2)}) copy-start(bf16[80,128]{1,0:T(8,128)(2,1)S(1)} %fusion.11) | copy-start | bytes 61444
  9.4 9.3 %collective-permute-start.2 = (bf16[160,256]{1,0:T(8,128)(2,1)S(1)}, bf16[160,256]{1,0:T(8,128)(2,1)S(1)}, u32[]{:S(2)}, u32[]{:S(2)}) collective-permute-start(bf16[160,256]{1,0:T(8,128)(2,1)S(1)} %slice.63), channel_id=1, source_target_pairs={{0,6},{2,0},{4,2},{6,4},{1,7},{3,1},{5,3},{7,5},{8,14},{10,8},{12,... | collective-permute-start | bytes 245768 | tf_op jit(solution)/shard_map/ppermute | solution.py:83
  9.5 23.5 %collective-permute-start.1 = (bf16[160,256]{1,0:T(8,128)(2,1)S(1)}, bf16[160,256]{1,0:T(8,128)(2,1)S(1)}, u32[]{:S(2)}, u32[]{:S(2)}) collective-permute-start(bf16[160,256]{1,0:T(8,128)(2,1)S(1)} %slice.63), channel_id=1, source_target_pairs={{0,4},{2,6},{4,0},{6,2},{1,5},{3,7},{5,1},{7,3},{8,12},{10,14},{12... | collective-permute-start | bytes 245768 | tf_op jit(solution)/shard_map/ppermute | solution.py:83
  11.5 21.5 %collective-permute-start = (bf16[160,256]{1,0:T(8,128)(2,1)S(1)}, bf16[160,256]{1,0:T(8,128)(2,1)S(1)}, u32[]{:S(2)}, u32[]{:S(2)}) collective-permute-start(bf16[160,256]{1,0:T(8,128)(2,1)S(1)} %slice.63), channel_id=1, source_target_pairs={{0,2},{2,4},{4,6},{6,0},{1,3},{3,5},{5,7},{7,1},{8,10},{10,12},{12... | collective-permute-start | bytes 245768 | tf_op jit(solution)/shard_map/ppermute | solution.py:83
  18.7 16.2 %collective-permute-start.5 = (bf16[512,512]{1,0:T(8,128)(2,1)S(1)}, bf16[512,512]{1,0:T(8,128)(2,1)S(1)}, u32[]{:S(2)}, u32[]{:S(2)}) collective-permute-start(bf16[512,512]{1,0:T(8,128)(2,1)S(1)} %copy-done), channel_id=1, source_target_pairs={{0,2},{2,4},{4,6},{6,0},{1,3},{3,5},{5,7},{7,1},{8,10},{10,12},{12... | collective-permute-start | bytes 1572872 | tf_op jit(solution)/shard_map/ppermute | solution.py:62

commit v14 on v13

--- a/solution.py
+++ b/solution.py
@@ -77,14 +77,21 @@
     )
     chip_kv = chip_rows[:, width:]
     if chips <= 8:
-        kv_pair = jnp.concatenate(
-            [chip_kv]
-            + [
-                lax.ppermute(chip_kv, "chip", [(i, (i + s) % chips) for i in range(chips)])
-                for s in range(1, chips)
-            ],
-            axis=0,
-        )
+        reach = chips // 2
+        mine = [list(range(1, reach + 1)), [chips - p for p in range(1, reach + 1)]]
+        fetched = []
+        for p in range(reach):
+            pairs = []
+            for i in range(chips):
+                for k in range(cores):
+                    pairs.append((i * cores + k, ((i + mine[k][p]) % chips) * cores + k))
+            fetched.append(lax.ppermute(chip_kv, BLK, pairs))
+        both = lax.all_gather(jnp.stack(fetched, 0), "core", axis=0, tiled=False)
+        pieces = {0: chip_kv}
+        for k in range(cores):
+            for p in range(reach):
+                pieces.setdefault(mine[k][p], both[k, p])
+        kv_pair = jnp.concatenate([pieces[s] for s in range(chips)], axis=0)
         src_chip = (lax.axis_index("chip") - jnp.arange(chips)) % chips
     else:
         kv_pair = lax.all_gather(chip_kv, "chip", axis=0, tiled=True)

time: 59.9 us -> 62 us (1.035)
  starting transfers between devices: 10.5 us -> 8 us
  blocking collectives: 24.8 us -> 26.9 us
  waiting for transfers between devices: 17 us -> 18.6 us
  local copies, waits for them, and re-layouts: 1.27 us -> 2.15 us
    all_gather x0 -> x1, blocking collectives: none -> 2.04 us  [body(): both = lax.all_gather(jnp.stack(fetched, 0), 'core', axis=0, tiled=False)]
    ppermute x3, starting transfers between devices: 6.9 us -> 5.04 us  [body(): lax.ppermute(out_weight, 'chip', [(i, (i + s) % chips) for i in range(chi...]
    ppermute x3 -> x2, waiting for transfers between devices: 17 us -> 18.6 us  [body(): fetched.append(lax.ppermute(chip_kv, BLK, pairs))]
    unnamed x21, local copies, waits for them, and re-layouts: 0.3 us -> 1.16 us
    ppermute x3 -> x2, starting transfers between devices: 3.59 us -> 2.95 us  [body(): fetched.append(lax.ppermute(chip_kv, BLK, pairs))]
  transfers between devices with their start and end apart: 6 -> 5, of which waited for: 2 -> 1; matrix products, arithmetic and copies ran while one was open for 7% -> 7% of each run, Pallas kernels for 0% -> 0%
where the time goes in v14:
time: 62 us; the launch traced here: 61.7 us
  blocking collectives  26.9 us (43%)
  waiting for transfers between devices  18.6 us (30%)
  starting transfers between devices  8 us (13%)
  other arithmetic  2.63 us (4%)
  matrix products  2.43 us (4%)
  local copies, waits for them, and re-layouts  2.15 us (3%)
  between operations  1.05 us (2%)
    all_to_all x1, blocking collectives, body(): got = lax.all_to_all(routed, ('kv', 'core'), 0, 0, tiled=True)  22.8 us
    ppermute x2, waiting for transfers between devices, body(): fetched.append(lax.ppermute(chip_kv, BLK, pairs))  18.6 us
    ppermute x3, starting transfers between devices, body(): lax.ppermute(out_weight, 'chip', [(i, (i + s) % chips) for i in range(chi...  5.04 us
    ppermute x2, starting transfers between devices, body(): fetched.append(lax.ppermute(chip_kv, BLK, pairs))  2.95 us
    all_gather x1, blocking collectives, body(): both = lax.all_gather(jnp.stack(fetched, 0), 'core', axis=0, tiled=False)  2.04 us
    all_gather x1, blocking collectives, body(): lax.all_gather(jnp.concatenate([rot_queries, rot_keys, values], axis=1),...  1.98 us
  transfers between devices with their start and end apart: 5, of which 1 were waited for; matrix products, arithmetic and copies ran while one was open for 7% of the time, Pallas kernels for 0%

profile of v14, /device:TPU:0, one launch (start us, length us, event | category | flops | bytes accessed | tf_op | source)
XLA Modules:
  0.0 61.7 jit_solution(3021483342336866377)
XLA Ops:
  0.7 3.9 %collective-permute-start.2 = (bf16[512,512]{1,0:T(8,128)(2,1)}, bf16[512,512]{1,0:T(8,128)(2,1)S(1)}, u32[]{:S(2)}, u32[]{:S(2)}) collective-permute-start(bf16[512,512]{1,0:T(8,128)(2,1)} %param.11), channel_id=1, source_target_pairs={{0,6},{2,0},{4,2},{6,4},{1,7},{3,1},{5,3},{7,5},{8,14},{10,8},{12,... | collective-permute-start | bytes 1572872 | tf_op jit(solution)/shard_map/ppermute | solution.py:62
  4.6 0.5 collective-permute-start.3
  5.1 0.6 collective-permute-start.4
  5.7 0.7 %select_reduce_fusion.1 = s32[5]{0:T(128)S(1)} fusion(s32[4]{0:T(128)} %param.10, s32[5]{0:T(128)S(1)} %iota_add_fusion.3), kind=kLoop, calls=%fused_computation.57 | loop fusion | flops 55 | bytes 56 | tf_op jit(solution)/shard_map/reduce_sum | solution.py:53
  6.5 0.1 select_reduce_fusion
  6.6 0.2 multiply_cosine_fusion
  7.2 0.1 tile.25
  7.4 0.1 tile.23
  7.5 0.1 fusion.11
  7.7 0.2 fusion.8
  8.0 2.0 %all_gather.9 = bf16[160,768]{1,0:T(8,128)(2,1)S(1)} all-gather(bf16[80,768]{1,0:T(8,128)(2,1)S(1)} %pad_maximum_fusion.4), channel_id=1, replica_groups=mesh['kv'=4,'chip'=4,'core'=2] {'core'}, dimensions={0}, use_global_device_ids=true | all-gather | bytes 368640 | tf_op jit(solution)/shard_map/all_gather | solution.py:75
  9.9 1.0 %collective-permute-start.1 = (bf16[160,256]{1,0:T(8,128)(2,1)S(1)}, bf16[160,256]{1,0:T(8,128)(2,1)S(1)}, u32[]{:S(2)}, u32[]{:S(2)}) collective-permute-start(bf16[160,256]{1,0:T(8,128)(2,1)S(1)} %slice.75), channel_id=1, source_target_pairs={{0,4},{1,5},{2,6},{3,7},{4,0},{5,1},{6,2},{7,3},{8,12},{9,13},{10,... | collective-permute-start | bytes 245768 | tf_op jit(solution)/shard_map/ppermute | solution.py:88
  10.9 1.9 %collective-permute-start = (bf16[160,256]{1,0:T(8,128)(2,1)S(1)}, bf16[160,256]{1,0:T(8,128)(2,1)S(1)}, u32[]{:S(2)}, u32[]{:S(2)}) collective-permute-start(bf16[160,256]{1,0:T(8,128)(2,1)S(1)} %slice.75), channel_id=1, source_target_pairs={{0,2},{1,7},{2,4},{3,1},{4,6},{5,3},{6,0},{7,5},{8,10},{9,15},{10,... | collective-permute-start | bytes 245768 | tf_op jit(solution)/shard_map/ppermute | solution.py:88
  13.1 0.1 convert_reduce_fusion.1
  13.5 18.6 %collective-permute-done.1 = bf16[160,256]{1,0:T(8,128)(2,1)S(1)} collective-permute-done((bf16[160,256]{1,0:T(8,128)(2,1)S(1)}, bf16[160,256]{1,0:T(8,128)(2,1)S(1)}, u32[]{:S(2)}, u32[]{:S(2)}) %collective-permute-start.1) | collective-permute-done | bytes 81952 | tf_op jit(solution)/shard_map/ppermute | solution.py:88
  32.1 2.0 %all-gather = bf16[4,160,256]{2,1,0:T(8,128)(2,1)S(1)} all-gather(bf16[2,160,256]{2,1,0:T(8,128)(2,1)S(1)} %pad_maximum_fusion.1), channel_id=2, replica_groups=mesh['kv'=4,'chip'=4,'core'=2] {'core'}, dimensions={0}, use_global_device_ids=true | all-gather | bytes 491520 | tf_op jit(solution)/shard_map/all_gather | solution.py:89
  34.2 0.6 fusion.34
  34.8 0.5 fusion.12
  35.2 0.7 %fusion.5 = bf16[640,128]{1,0:T(8,128)(2,1)S(1)} fusion(f32[640,640]{0,1:T(8,128)S(1)} %get-tuple-element.18, f32[640]{0:T(1024)S(1)} %get-tuple-element.17, s32[640]{0:T(1024)S(1)} %le.61, s32[640]{0:T(1024)S(1)} %eq.26, s32[640]{0:T(1024)S(1)} %add.94, s32[640]{0:T(1024)S(1)} %broadcast_add_fusion, bf16[640,256]{1,0:T(8,128)(2,1)S(1)} %pad_maximum_fusion, ...), kind=kOutput, calls=%fused_computation.7 | convolution fusion | flops 107479040 | bytes 1990656 | tf_op jit(solution)/shard_map/dot_general | solution.py:123
  36.2 0.9 %copy-done = bf16[512,512]{1,0:T(8,128)(2,1)S(1)} copy-done((bf16[512,512]{1,0:T(8,128)(2,1)S(1)}, bf16[512,512]{1,0:T(8,128)(2,1)}, u32[]{:S(2)}) %copy-start) | copy-done | bytes 524312
  37.2 0.8 %fusion.2 = bf16[4,160,512]{2,1,0:T(8,128)(2,1)S(1)} fusion(bf16[8,512,512]{2,1,0:T(8,128)(2,1)S(1)} %bitcast_dynamic-update-slice_fusion.1, s32[]{:T(128)S(6)} %select_n.43, bf16[160,512]{1,0:T(8,128)(2,1)S(1)} %pad_maximum_fusion.2), kind=kOutput, calls=%fused_computation.5 | convolution fusion | flops 335872000 | bytes 2916356 | tf_op jit(solution)/shard_map/ctk,cnk->ctn/dot_general | solution.py:133
  38.1 22.8 %all_to_all.5 = bf16[8,80,512]{2,1,0:T(8,128)(2,1)S(1)} all-to-all(bf16[8,80,512]{2,1,0:T(8,128)(2,1)S(1)} %bitcast.50), channel_id=1, replica_groups=mesh['kv'=4,'chip'=4,'core'=2] {'kv','core'}, dimensions={0} | all-to-all | bytes 1310720 | tf_op jit(solution)/shard_map/all_to_all | solution.py:142
  60.9 0.1 reduce
  61.1 0.7 %pad_maximum_fusion.3 = bf16[80,1024]{1,0:T(8,128)(2,1)} fusion(bf16[80,512]{1,0:T(8,128)(2,1)S(1)} %get-tuple-element.10, bf16[80,512]{1,0:T(8,128)(2,1)S(1)} %get-tuple-element.9), kind=kLoop, calls=%fused_computation.41 | loop fusion | flops 327680 | bytes 327680 | tf_op jit(solution)/shard_map/concatenate | solution.py:146
  (58 shorter events, 1.3 us)
Async XLA Ops:
  0.6 6.9 %copy-start.4 = (bf16[128,128]{1,0:T(8,128)(2,1)S(1)}, bf16[128,128]{1,0:T(8,128)(2,1)}, u32[]{:S(2)}) copy-start(bf16[128,128]{1,0:T(8,128)(2,1)} %constant.63.clone) | copy-start | bytes 98308
  0.6 7.0 %copy-start.1 = (bf16[512,512]{1,0:T(8,128)(2,1)S(1)}, bf16[512,512]{1,0:T(8,128)(2,1)}, u32[]{:S(2)}) copy-start(bf16[512,512]{1,0:T(8,128)(2,1)} %constant.64.clone) | copy-start | bytes 1572868
  0.7 6.9 %copy-start.5 = (bf16[80,128]{1,0:T(8,128)(2,1)S(1)}, bf16[80,128]{1,0:T(8,128)(2,1)}, u32[]{:S(2)}) copy-start(bf16[80,128]{1,0:T(8,128)(2,1)} %param.8) | copy-start | bytes 61444
  0.7 7.0 %copy-start.3 = (bf16[80,512]{1,0:T(8,128)(2,1)S(1)}, bf16[80,512]{1,0:T(8,128)(2,1)}, u32[]{:S(2)}) copy-start(bf16[80,512]{1,0:T(8,128)(2,1)} %param.7) | copy-start | bytes 245764
  0.7 35.3 %collective-permute-start.2 = (bf16[512,512]{1,0:T(8,128)(2,1)}, bf16[512,512]{1,0:T(8,128)(2,1)S(1)}, u32[]{:S(2)}, u32[]{:S(2)}) collective-permute-start(bf16[512,512]{1,0:T(8,128)(2,1)} %param.11), channel_id=1, source_target_pairs={{0,6},{2,0},{4,2},{6,4},{1,7},{3,1},{5,3},{7,5},{8,14},{10,8},{12,... | collective-permute-start | bytes 1572872 | tf_op jit(solution)/shard_map/ppermute | solution.py:62
  4.6 31.4 %collective-permute-start.3 = (bf16[512,512]{1,0:T(8,128)(2,1)}, bf16[512,512]{1,0:T(8,128)(2,1)S(1)}, u32[]{:S(2)}, u32[]{:S(2)}) collective-permute-start(bf16[512,512]{1,0:T(8,128)(2,1)} %param.11), channel_id=1, source_target_pairs={{0,4},{2,6},{4,0},{6,2},{1,5},{3,7},{5,1},{7,3},{8,12},{10,14},{12... | collective-permute-start | bytes 1572872 | tf_op jit(solution)/shard_map/ppermute | solution.py:62
  5.1 31.0 %collective-permute-start.4 = (bf16[512,512]{1,0:T(8,128)(2,1)}, bf16[512,512]{1,0:T(8,128)(2,1)S(1)}, u32[]{:S(2)}, u32[]{:S(2)}) collective-permute-start(bf16[512,512]{1,0:T(8,128)(2,1)} %param.11), channel_id=1, source_target_pairs={{0,2},{2,4},{4,6},{6,0},{1,3},{3,5},{5,7},{7,1},{8,10},{10,12},{12... | collective-permute-start | bytes 1572872 | tf_op jit(solution)/shard_map/ppermute | solution.py:62
  6.9 1.0 %copy-start.6 = (bf16[80,128]{1,0:T(8,128)(2,1)S(1)}, bf16[80,128]{1,0:T(8,128)(2,1)}, u32[]{:S(2)}) copy-start(bf16[80,128]{1,0:T(8,128)(2,1)} %param.9) | copy-start | bytes 61444
  7.7 26.5 %copy-start.2 = (bf16[80,128]{1,0:T(8,128)(2,1)}, bf16[80,128]{1,0:T(8,128)(2,1)S(1)}, u32[]{:S(2)}) copy-start(bf16[80,128]{1,0:T(8,128)(2,1)S(1)} %fusion.11) | copy-start | bytes 61444
  9.9 22.1 %collective-permute-start.1 = (bf16[160,256]{1,0:T(8,128)(2,1)S(1)}, bf16[160,256]{1,0:T(8,128)(2,1)S(1)}, u32[]{:S(2)}, u32[]{:S(2)}) collective-permute-start(bf16[160,256]{1,0:T(8,128)(2,1)S(1)} %slice.75), channel_id=1, source_target_pairs={{0,4},{1,5},{2,6},{3,7},{4,0},{5,1},{6,2},{7,3},{8,12},{9,13},{10,... | collective-permute-start | bytes 245768 | tf_op jit(solution)/shard_map/ppermute | solution.py:88
  10.9 21.1 %collective-permute-start = (bf16[160,256]{1,0:T(8,128)(2,1)S(1)}, bf16[160,256]{1,0:T(8,128)(2,1)S(1)}, u32[]{:S(2)}, u32[]{:S(2)}) collective-permute-start(bf16[160,256]{1,0:T(8,128)(2,1)S(1)} %slice.75), channel_id=1, source_target_pairs={{0,2},{1,7},{2,4},{3,1},{4,6},{5,3},{6,0},{7,5},{8,10},{9,15},{10,... | collective-permute-start | bytes 245768 | tf_op jit(solution)/shard_map/ppermute | solution.py:88
  36.0 1.0 %copy-start = (bf16[512,512]{1,0:T(8,128)(2,1)S(1)}, bf16[512,512]{1,0:T(8,128)(2,1)}, u32[]{:S(2)}) copy-start(bf16[512,512]{1,0:T(8,128)(2,1)} %param.11) | copy-start | bytes 1572868

commit v15 on v14

--- a/solution.py
+++ b/solution.py
@@ -57,7 +57,12 @@
     query_idx = first_tok + jnp.arange(tok_rows)
     query_seg, query_off = locate(query_idx, starts)
     positions = query_idx - query_off
-    if chips <= 8:
+    kvs = lax.axis_size("kv")
+    xor_plan = chips == 4 and kvs == chips
+    if xor_plan:
+        w_x = lax.ppermute(out_weight, "chip", [(i, i ^ 1) for i in range(chips)])
+        w_y = lax.ppermute(out_weight, "chip", [(i, i ^ 2) for i in range(chips)])
+    elif chips <= 8:
         held = [out_weight] + [
             lax.ppermute(out_weight, "chip", [(i, (i + s) % chips) for i in range(chips)])
             for s in range(1, chips)
@@ -127,18 +132,31 @@
     chip_att = jnp.concatenate(
         [att_rows[h * chip_tok:(h + 1) * chip_tok] for h in range(groups)], axis=1
     )
-    kvs = lax.axis_size("kv")
-    per_c = w_share.shape[0] // kvs
-    routed = (
-        jnp.einsum(
-            "ctk,cnk->ctn",
-            jnp.broadcast_to(chip_att, (kvs,) + chip_att.shape),
-            w_share.reshape(kvs, per_c, w_share.shape[1]),
-            preferred_element_type=jnp.float32,
+    if xor_plan:
+        per_c = out_weight.shape[0]
+
+        def part(att, w):
+            return jnp.dot(att, w.T, preferred_element_type=jnp.float32).astype(jnp.bfloat16)
+
+        att_x = lax.ppermute(chip_att, "chip", [(i, i ^ 1) for i in range(chips)])
+        diag = lax.ppermute(part(att_x, w_y), "chip", [(i, i ^ 1) for i in range(chips)])
+        by_dist = jnp.stack([part(chip_att, out_weight), part(chip_att, w_x), part(chip_att, w_y), diag])
+        here = lax.axis_index("chip")
+        routed = jnp.stack(
+            [lax.dynamic_index_in_dim(by_dist, here ^ c, 0, keepdims=False) for c in range(kvs)]
+        ).reshape(kvs * cores, tok_rows, per_c)
+    else:
+        per_c = w_share.shape[0] // kvs
+        routed = (
+            jnp.einsum(
+                "ctk,cnk->ctn",
+                jnp.broadcast_to(chip_att, (kvs,) + chip_att.shape),
+                w_share.reshape(kvs, per_c, w_share.shape[1]),
+                preferred_element_type=jnp.float32,
+            )
+            .astype(jnp.bfloat16)
+            .reshape(kvs * cores, tok_rows, per_c)
         )
-        .astype(jnp.bfloat16)
-        .reshape(kvs * cores, tok_rows, per_c)
-    )
     got = lax.all_to_all(routed, ("kv", "core"), 0, 0, tiled=True)
     total = jnp.sum(got.reshape(kvs, cores, tok_rows, per_c).astype(jnp.float32), axis=0)
     rows = out_weight.shape[0]

time: 62 us -> 62.7 us (1.011)
  local copies, waits for them, and re-layouts: 2.15 us -> 1.05 us
  waiting for transfers between devices: 18.6 us -> 19.7 us
    ppermute x3 -> x4, waiting for transfers between devices: 0.01 us -> 16.6 us  [the longest x1 9.4 us: body(): w_x = lax.ppermute(out_weight, 'chip', [(i, i ^ 1) for i in range(chips)])]
    ppermute x2, waiting for transfers between devices: 18.6 us -> 3.05 us  [body(): fetched.append(lax.ppermute(chip_kv, BLK, pairs))]
    ppermute x2, starting transfers between devices: 2.95 us -> 4.41 us  [body(): fetched.append(lax.ppermute(chip_kv, BLK, pairs))]
    ppermute x3 -> x4, starting transfers between devices: 5.04 us -> 3.66 us  [the longest x1 1.18 us: body(): att_x = lax.ppermute(chip_att, 'chip', [(i, i ^ 1) for i in range(chips)])]
    unnamed x21 -> x14, local copies, waits for them, and re-layouts: 1.16 us -> 0.04 us
    dot_general x1 -> x4, matrix products: 0.84 us -> 1.28 us  [part(): jnp.dot(att, w.T, preferred_element_type=jnp.float32).astype(jnp.bfloat16)]
  transfers between devices with their start and end apart: 5 -> 6, of which waited for: 1 -> 6; matrix products, arithmetic and copies ran while one was open for 7% -> 6% of each run, Pallas kernels for 0% -> 0%
where the time goes in v15:
time: 62.7 us; the launch traced here: 62.5 us
  blocking collectives  27 us (43%)
  waiting for transfers between devices  19.7 us (31%)
  starting transfers between devices  8.07 us (13%)
  matrix products  2.88 us (5%)
  other arithmetic  2.86 us (5%)
  local copies, waits for them, and re-layouts  1.05 us (2%)
  between operations  1.03 us (2%)
    all_to_all x1, blocking collectives, body(): got = lax.all_to_all(routed, ('kv', 'core'), 0, 0, tiled=True)  22.9 us
    ppermute x1, waiting for transfers between devices, body(): w_x = lax.ppermute(out_weight, 'chip', [(i, i ^ 1) for i in range(chips)])  9.4 us
    ppermute x1, waiting for transfers between devices, body(): att_x = lax.ppermute(chip_att, 'chip', [(i, i ^ 1) for i in range(chips)])  4.69 us
    ppermute x2, starting transfers between devices, body(): fetched.append(lax.ppermute(chip_kv, BLK, pairs))  4.41 us
    ppermute x2, waiting for transfers between devices, body(): fetched.append(lax.ppermute(chip_kv, BLK, pairs))  3.05 us
    ppermute x1, waiting for transfers between devices, body(): lax.ppermute(part(att_x, w_y), 'chip', [(i, i ^ 1) for i in range(chips)])  2.4 us
    all_gather x1, blocking collectives, body(): lax.all_gather(jnp.concatenate([rot_queries, rot_keys, values], axis=1),...  2.07 us
    all_gather x1, blocking collectives, body(): both = lax.all_gather(jnp.stack(fetched, 0), 'core', axis=0, tiled=False)  2.04 us
  transfers between devices with their start and end apart: 6, of which 6 were waited for; matrix products, arithmetic and copies ran while one was open for 6% of the time, Pallas kernels for 0%

profile of v15, /device:TPU:0, one launch (start us, length us, event | category | flops | bytes accessed | tf_op | source)
XLA Modules:
  0.0 62.5 jit_solution(6505049615390387358)
XLA Ops:
  0.7 0.8 %select_reduce_fusion.1 = s32[5]{0:T(128)S(1)} fusion(s32[4]{0:T(128)} %param.10, s32[5]{0:T(128)S(1)} %iota_add_fusion.3), kind=kLoop, calls=%fused_computation.54 | loop fusion | flops 55 | bytes 56 | tf_op jit(solution)/shard_map/reduce_sum | solution.py:53
  2.8 0.2 fusion.6
  3.0 2.1 %all_gather.9 = bf16[160,768]{1,0:T(8,128)(2,1)S(1)} all-gather(bf16[80,768]{1,0:T(8,128)(2,1)S(1)} %pad_maximum_fusion.6), channel_id=1, replica_groups=mesh['kv'=4,'chip'=4,'core'=2] {'core'}, dimensions={0}, use_global_device_ids=true | all-gather | bytes 368640 | tf_op jit(solution)/shard_map/all_gather | solution.py:80
  5.1 2.9 %collective-permute-start = (bf16[160,256]{1,0:T(8,128)(2,1)S(1)}, bf16[160,256]{1,0:T(8,128)(2,1)S(1)}, u32[]{:S(2)}, u32[]{:S(2)}) collective-permute-start(bf16[160,256]{1,0:T(8,128)(2,1)S(1)} %slice.75), channel_id=1, source_target_pairs={{0,2},{1,7},{2,4},{3,1},{4,6},{5,3},{6,0},{7,5},{8,10},{9,15},{10,... | collective-permute-start | bytes 245768 | tf_op jit(solution)/shard_map/ppermute | solution.py:93
  8.0 1.5 %collective-permute-start.1 = (bf16[160,256]{1,0:T(8,128)(2,1)S(1)}, bf16[160,256]{1,0:T(8,128)(2,1)S(1)}, u32[]{:S(2)}, u32[]{:S(2)}) collective-permute-start(bf16[160,256]{1,0:T(8,128)(2,1)S(1)} %slice.75), channel_id=1, source_target_pairs={{0,4},{1,5},{2,6},{3,7},{4,0},{5,1},{6,2},{7,3},{8,12},{9,13},{10,... | collective-permute-start | bytes 245768 | tf_op jit(solution)/shard_map/ppermute | solution.py:93
  9.5 0.5 collective-permute-start.3
  10.6 1.4 %collective-permute-done = bf16[160,256]{1,0:T(8,128)(2,1)S(1)} collective-permute-done((bf16[160,256]{1,0:T(8,128)(2,1)S(1)}, bf16[160,256]{1,0:T(8,128)(2,1)S(1)}, u32[]{:S(2)}, u32[]{:S(2)}) %collective-permute-start) | collective-permute-done | bytes 81952 | tf_op jit(solution)/shard_map/ppermute | solution.py:93
  12.0 1.6 %collective-permute-done.1 = bf16[160,256]{1,0:T(8,128)(2,1)S(1)} collective-permute-done((bf16[160,256]{1,0:T(8,128)(2,1)S(1)}, bf16[160,256]{1,0:T(8,128)(2,1)S(1)}, u32[]{:S(2)}, u32[]{:S(2)}) %collective-permute-start.1) | collective-permute-done | bytes 81952 | tf_op jit(solution)/shard_map/ppermute | solution.py:93
  13.7 2.0 %all-gather = bf16[4,160,256]{2,1,0:T(8,128)(2,1)S(1)} all-gather(bf16[2,160,256]{2,1,0:T(8,128)(2,1)S(1)} %pad_maximum_fusion.3), channel_id=2, replica_groups=mesh['kv'=4,'chip'=4,'core'=2] {'core'}, dimensions={0}, use_global_device_ids=true | all-gather | bytes 491520 | tf_op jit(solution)/shard_map/all_gather | solution.py:94
  15.8 0.6 fusion.30
  16.3 0.5 fusion.10
  16.8 0.7 %fusion = bf16[640,128]{1,0:T(8,128)(2,1)S(1)} fusion(f32[640,640]{0,1:T(8,128)S(1)} %get-tuple-element.22, f32[640]{0:T(1024)S(1)} %get-tuple-element.21, s32[640]{0:T(1024)S(1)} %le.61, s32[640]{0:T(1024)S(1)} %eq.26, s32[640]{0:T(1024)S(1)} %add.103, s32[640]{0:T(1024)S(1)} %broadcast_add_fusion, bf16[640,256]{1,0:T(8,128)(2,1)S(1)} %pad_maximum_fusion.2, ...), kind=kOutput, calls=%fused_computation.8 | convolution fusion | flops 107479040 | bytes 1990656 | tf_op jit(solution)/shard_map/dot_general | solution.py:128
  17.5 1.2 %collective-permute-start.4 = (bf16[160,512]{1,0:T(8,128)(2,1)S(1)}, bf16[160,512]{1,0:T(8,128)(2,1)S(1)}, u32[]{:S(2)}, u32[]{:S(2)}) collective-permute-start(bf16[160,512]{1,0:T(8,128)(2,1)S(1)} %pad_maximum_fusion.4), channel_id=1, source_target_pairs={{0,2},{2,0},{4,6},{6,4},{1,3},{3,1},{5,7},{7,5},{8,10},{10,8},{12,... | collective-permute-start | bytes 491528 | tf_op jit(solution)/shard_map/ppermute | solution.py:141
  18.7 0.9 %collective-permute-start.2 = (bf16[512,512]{1,0:T(8,128)(2,1)S(1)}, bf16[512,512]{1,0:T(8,128)(2,1)S(1)}, u32[]{:S(2)}, u32[]{:S(2)}) collective-permute-start(bf16[512,512]{1,0:T(8,128)(2,1)S(1)} %copy-done.6), channel_id=1, source_target_pairs={{0,2},{2,0},{4,6},{6,4},{1,3},{3,1},{5,7},{7,5},{8,10},{10,8},{12,... | collective-permute-start | bytes 1572872 | tf_op jit(solution)/shard_map/ppermute | solution.py:63
  19.6 0.3 fusion.1
  20.0 4.7 %collective-permute-done.4 = bf16[160,512]{1,0:T(8,128)(2,1)S(1)} collective-permute-done((bf16[160,512]{1,0:T(8,128)(2,1)S(1)}, bf16[160,512]{1,0:T(8,128)(2,1)S(1)}, u32[]{:S(2)}, u32[]{:S(2)}) %collective-permute-start.4) | collective-permute-done | bytes 163872 | tf_op jit(solution)/shard_map/ppermute | solution.py:141
  24.8 0.3 convolution_convert_fusion
  25.1 1.1 %collective-permute-start.5 = (bf16[160,512]{1,0:T(8,128)(2,1)S(1)}, bf16[160,512]{1,0:T(8,128)(2,1)S(1)}, u32[]{:S(2)}, u32[]{:S(2)}) collective-permute-start(bf16[160,512]{1,0:T(8,128)(2,1)S(1)} %convolution_convert_fusion), channel_id=1, source_target_pairs={{0,2},{2,0},{4,6},{6,4},{1,3},{3,1},{5,7},{7,5},{8,10},{10,8},{12,... | collective-permute-start | bytes 491528 | tf_op jit(solution)/shard_map/ppermute | solution.py:142
  26.2 0.3 fusion.3
  26.5 9.4 %collective-permute-done.2 = bf16[512,512]{1,0:T(8,128)(2,1)S(1)} collective-permute-done((bf16[512,512]{1,0:T(8,128)(2,1)S(1)}, bf16[512,512]{1,0:T(8,128)(2,1)S(1)}, u32[]{:S(2)}, u32[]{:S(2)}) %collective-permute-start.2) | collective-permute-done | bytes 524320 | tf_op jit(solution)/shard_map/ppermute | solution.py:63
  35.9 0.3 fusion.2
  36.2 2.4 %collective-permute-done.5 = bf16[160,512]{1,0:T(8,128)(2,1)S(1)} collective-permute-done((bf16[160,512]{1,0:T(8,128)(2,1)S(1)}, bf16[160,512]{1,0:T(8,128)(2,1)S(1)}, u32[]{:S(2)}, u32[]{:S(2)}) %collective-permute-start.5) | collective-permute-done | bytes 163872 | tf_op jit(solution)/shard_map/ppermute | solution.py:142
  38.9 22.9 %all_to_all.5 = bf16[8,80,512]{2,1,0:T(8,128)(2,1)S(1)} all-to-all(bf16[8,80,512]{2,1,0:T(8,128)(2,1)S(1)} %bitcast.49), channel_id=1, replica_groups=mesh['kv'=4,'chip'=4,'core'=2] {'kv','core'}, dimensions={0} | all-to-all | bytes 1310720 | tf_op jit(solution)/shard_map/all_to_all | solution.py:160
  61.8 0.7 %pad_maximum_fusion.5 = bf16[80,1024]{1,0:T(8,128)(2,1)} fusion(bf16[80,512]{1,0:T(8,128)(2,1)S(1)} %get-tuple-element.14, bf16[80,512]{1,0:T(8,128)(2,1)S(1)} %get-tuple-element.13), kind=kLoop, calls=%fused_computation.38 | loop fusion | flops 327680 | bytes 327680 | tf_op jit(solution)/shard_map/concatenate | solution.py:164
  (58 shorter events, 2.2 us)
Async XLA Ops:
  0.6 1.9 %copy-start.3 = (bf16[128,128]{1,0:T(8,128)(2,1)S(1)}, bf16[128,128]{1,0:T(8,128)(2,1)}, u32[]{:S(2)}) copy-start(bf16[128,128]{1,0:T(8,128)(2,1)} %constant.72.clone) | copy-start | bytes 98308
  0.6 2.1 %copy-start = (bf16[512,512]{1,0:T(8,128)(2,1)S(1)}, bf16[512,512]{1,0:T(8,128)(2,1)}, u32[]{:S(2)}) copy-start(bf16[512,512]{1,0:T(8,128)(2,1)} %constant.73.clone) | copy-start | bytes 1572868
  0.7 1.9 %copy-start.4 = (bf16[80,128]{1,0:T(8,128)(2,1)S(1)}, bf16[80,128]{1,0:T(8,128)(2,1)}, u32[]{:S(2)}) copy-start(bf16[80,128]{1,0:T(8,128)(2,1)} %param.8) | copy-start | bytes 61444
  0.7 2.1 %copy-start.2 = (bf16[80,512]{1,0:T(8,128)(2,1)S(1)}, bf16[80,512]{1,0:T(8,128)(2,1)}, u32[]{:S(2)}) copy-start(bf16[80,512]{1,0:T(8,128)(2,1)} %param.7) | copy-start | bytes 245764
  1.9 1.0 %copy-start.5 = (bf16[80,128]{1,0:T(8,128)(2,1)S(1)}, bf16[80,128]{1,0:T(8,128)(2,1)}, u32[]{:S(2)}) copy-start(bf16[80,128]{1,0:T(8,128)(2,1)} %param.9) | copy-start | bytes 61444
  2.2 7.3 %copy-start.6 = (bf16[512,512]{1,0:T(8,128)(2,1)S(1)}, bf16[512,512]{1,0:T(8,128)(2,1)}, u32[]{:S(2)}) copy-start(bf16[512,512]{1,0:T(8,128)(2,1)} %param.11) | copy-start | bytes 1572868
  2.7 13.0 %copy-start.1 = (bf16[80,128]{1,0:T(8,128)(2,1)}, bf16[80,128]{1,0:T(8,128)(2,1)S(1)}, u32[]{:S(2)}) copy-start(bf16[80,128]{1,0:T(8,128)(2,1)S(1)} %fusion.9) | copy-start | bytes 61444
  5.1 6.9 %collective-permute-start = (bf16[160,256]{1,0:T(8,128)(2,1)S(1)}, bf16[160,256]{1,0:T(8,128)(2,1)S(1)}, u32[]{:S(2)}, u32[]{:S(2)}) collective-permute-start(bf16[160,256]{1,0:T(8,128)(2,1)S(1)} %slice.75), channel_id=1, source_target_pairs={{0,2},{1,7},{2,4},{3,1},{4,6},{5,3},{6,0},{7,5},{8,10},{9,15},{10,... | collective-permute-start | bytes 245768 | tf_op jit(solution)/shard_map/ppermute | solution.py:93
  8.0 5.7 %collective-permute-start.1 = (bf16[160,256]{1,0:T(8,128)(2,1)S(1)}, bf16[160,256]{1,0:T(8,128)(2,1)S(1)}, u32[]{:S(2)}, u32[]{:S(2)}) collective-permute-start(bf16[160,256]{1,0:T(8,128)(2,1)S(1)} %slice.75), channel_id=1, source_target_pairs={{0,4},{1,5},{2,6},{3,7},{4,0},{5,1},{6,2},{7,3},{8,12},{9,13},{10,... | collective-permute-start | bytes 245768 | tf_op jit(solution)/shard_map/ppermute | solution.py:93
  9.5 15.3 %collective-permute-start.3 = (bf16[512,512]{1,0:T(8,128)(2,1)S(1)}, bf16[512,512]{1,0:T(8,128)(2,1)S(1)}, u32[]{:S(2)}, u32[]{:S(2)}) collective-permute-start(bf16[512,512]{1,0:T(8,128)(2,1)S(1)} %copy-done.6), channel_id=1, source_target_pairs={{0,4},{2,6},{4,0},{6,2},{1,5},{3,7},{5,1},{7,3},{8,12},{10,14},{12... | collective-permute-start | bytes 1572872 | tf_op jit(solution)/shard_map/ppermute | solution.py:64
  17.5 7.1 %collective-permute-start.4 = (bf16[160,512]{1,0:T(8,128)(2,1)S(1)}, bf16[160,512]{1,0:T(8,128)(2,1)S(1)}, u32[]{:S(2)}, u32[]{:S(2)}) collective-permute-start(bf16[160,512]{1,0:T(8,128)(2,1)S(1)} %pad_maximum_fusion.4), channel_id=1, source_target_pairs={{0,2},{2,0},{4,6},{6,4},{1,3},{3,1},{5,7},{7,5},{8,10},{10,8},{12,... | collective-permute-start | bytes 491528 | tf_op jit(solution)/shard_map/ppermute | solution.py:141
  18.7 17.2 %collective-permute-start.2 = (bf16[512,512]{1,0:T(8,128)(2,1)S(1)}, bf16[512,512]{1,0:T(8,128)(2,1)S(1)}, u32[]{:S(2)}, u32[]{:S(2)}) collective-permute-start(bf16[512,512]{1,0:T(8,128)(2,1)S(1)} %copy-done.6), channel_id=1, source_target_pairs={{0,2},{2,0},{4,6},{6,4},{1,3},{3,1},{5,7},{7,5},{8,10},{10,8},{12,... | collective-permute-start | bytes 1572872 | tf_op jit(solution)/shard_map/ppermute | solution.py:63
  25.1 13.5 %collective-permute-start.5 = (bf16[160,512]{1,0:T(8,128)(2,1)S(1)}, bf16[160,512]{1,0:T(8,128)(2,1)S(1)}, u32[]{:S(2)}, u32[]{:S(2)}) collective-permute-start(bf16[160,512]{1,0:T(8,128)(2,1)S(1)} %convolution_convert_fusion), channel_id=1, source_target_pairs={{0,2},{2,0},{4,6},{6,4},{1,3},{3,1},{5,7},{7,5},{8,10},{10,8},{12,... | collective-permute-start | bytes 491528 | tf_op jit(solution)/shard_map/ppermute | solution.py:142

commit v16 on v15

--- a/solution.py
+++ b/solution.py
@@ -138,6 +138,7 @@
         def part(att, w):
             return jnp.dot(att, w.T, preferred_element_type=jnp.float32).astype(jnp.bfloat16)
 
+        w_x, w_y, chip_att = lax.optimization_barrier((w_x, w_y, chip_att))
         att_x = lax.ppermute(chip_att, "chip", [(i, i ^ 1) for i in range(chips)])
         diag = lax.ppermute(part(att_x, w_y), "chip", [(i, i ^ 1) for i in range(chips)])
         by_dist = jnp.stack([part(chip_att, out_weight), part(chip_att, w_x), part(chip_att, w_y), diag])

time: 62.7 us -> 60.9 us (0.971)
  waiting for transfers between devices: 19.7 us -> 18.6 us
  starting transfers between devices: 8.07 us -> 7.12 us
    ppermute x1, waiting for transfers between devices: 9.4 us -> 5.58 us  [body(): w_x = lax.ppermute(out_weight, 'chip', [(i, i ^ 1) for i in range(chips)])]
    ppermute x1, waiting for transfers between devices: 2.4 us -> 4.39 us  [body(): lax.ppermute(part(att_x, w_y), 'chip', [(i, i ^ 1) for i in range(chips)])]
    ppermute x1, waiting for transfers between devices: 0.13 us -> 1.66 us  [body(): w_y = lax.ppermute(out_weight, 'chip', [(i, i ^ 2) for i in range(chips)])]
    ppermute x2, waiting for transfers between devices: 3.05 us -> 1.56 us  [body(): fetched.append(lax.ppermute(chip_kv, BLK, pairs))]
    ppermute x1, starting transfers between devices: 0.51 us -> 1.92 us  [body(): w_y = lax.ppermute(out_weight, 'chip', [(i, i ^ 2) for i in range(chips)])]
    ppermute x1, starting transfers between devices: 0.91 us -> 0.08 us  [body(): w_x = lax.ppermute(out_weight, 'chip', [(i, i ^ 1) for i in range(chips)])]
    ppermute x1, starting transfers between devices: 1.18 us -> 0.36 us  [body(): att_x = lax.ppermute(chip_att, 'chip', [(i, i ^ 1) for i in range(chips)])]
    ppermute x1, waiting for transfers between devices: 4.69 us -> 5.44 us  [body(): att_x = lax.ppermute(chip_att, 'chip', [(i, i ^ 1) for i in range(chips)])]
  transfers between devices with their start and end apart: 6 -> 6, of which waited for: 6 -> 5; matrix products, arithmetic and copies ran while one was open for 6% -> 5% of each run, Pallas kernels for 0% -> 0%
where the time goes in v16:
time: 60.9 us; the launch traced here: 60.7 us
  blocking collectives  27.2 us (45%)
  waiting for transfers between devices  18.6 us (31%)
  starting transfers between devices  7.12 us (12%)
  other arithmetic  2.86 us (5%)
  matrix products  2.85 us (5%)
  local copies, waits for them, and re-layouts  1.05 us (2%)
  between operations  1.04 us (2%)
    all_to_all x1, blocking collectives, body(): got = lax.all_to_all(routed, ('kv', 'core'), 0, 0, tiled=True)  23.1 us
    ppermute x1, waiting for transfers between devices, body(): w_x = lax.ppermute(out_weight, 'chip', [(i, i ^ 1) for i in range(chips)])  5.58 us
    ppermute x1, waiting for transfers between devices, body(): att_x = lax.ppermute(chip_att, 'chip', [(i, i ^ 1) for i in range(chips)])  5.44 us
    ppermute x2, starting transfers between devices, body(): fetched.append(lax.ppermute(chip_kv, BLK, pairs))  4.41 us
    ppermute x1, waiting for transfers between devices, body(): lax.ppermute(part(att_x, w_y), 'chip', [(i, i ^ 1) for i in range(chips)])  4.39 us
    all_gather x1, blocking collectives, body(): lax.all_gather(jnp.concatenate([rot_queries, rot_keys, values], axis=1),...  2.07 us
    all_gather x1, blocking collectives, body(): both = lax.all_gather(jnp.stack(fetched, 0), 'core', axis=0, tiled=False)  2.04 us
    ppermute x1, starting transfers between devices, body(): w_y = lax.ppermute(out_weight, 'chip', [(i, i ^ 2) for i in range(chips)])  1.92 us
  transfers between devices with their start and end apart: 6, of which 5 were waited for; matrix products, arithmetic and copies ran while one was open for 5% of the time, Pallas kernels for 0%

profile of v16, /device:TPU:0, one launch (start us, length us, event | category | flops | bytes accessed | tf_op | source)
XLA Modules:
  0.0 60.7 jit_solution(14353598653750442895)
XLA Ops:
  0.7 0.8 %select_reduce_fusion.1 = s32[5]{0:T(128)S(1)} fusion(s32[4]{0:T(128)} %param.10, s32[5]{0:T(128)S(1)} %iota_add_fusion.3), kind=kLoop, calls=%fused_computation.54 | loop fusion | flops 55 | bytes 56 | tf_op jit(solution)/shard_map/reduce_sum | solution.py:53
  1.6 0.2 multiply_cosine_fusion
  2.8 0.2 fusion.6
  3.0 2.1 %all_gather.9 = bf16[160,768]{1,0:T(8,128)(2,1)S(1)} all-gather(bf16[80,768]{1,0:T(8,128)(2,1)S(1)} %pad_maximum_fusion.6), channel_id=1, replica_groups=mesh['kv'=4,'chip'=4,'core'=2] {'core'}, dimensions={0}, use_global_device_ids=true | all-gather | bytes 368640 | tf_op jit(solution)/shard_map/all_gather | solution.py:80
  5.1 2.9 %collective-permute-start.2 = (bf16[160,256]{1,0:T(8,128)(2,1)S(1)}, bf16[160,256]{1,0:T(8,128)(2,1)S(1)}, u32[]{:S(2)}, u32[]{:S(2)}) collective-permute-start(bf16[160,256]{1,0:T(8,128)(2,1)S(1)} %slice.75), channel_id=1, source_target_pairs={{0,2},{1,7},{2,4},{3,1},{4,6},{5,3},{6,0},{7,5},{8,10},{9,15},{10,... | collective-permute-start | bytes 245768 | tf_op jit(solution)/shard_map/ppermute | solution.py:93
  8.0 1.5 %collective-permute-start.3 = (bf16[160,256]{1,0:T(8,128)(2,1)S(1)}, bf16[160,256]{1,0:T(8,128)(2,1)S(1)}, u32[]{:S(2)}, u32[]{:S(2)}) collective-permute-start(bf16[160,256]{1,0:T(8,128)(2,1)S(1)} %slice.75), channel_id=1, source_target_pairs={{0,4},{1,5},{2,6},{3,7},{4,0},{5,1},{6,2},{7,3},{8,12},{9,13},{10,... | collective-permute-start | bytes 245768 | tf_op jit(solution)/shard_map/ppermute | solution.py:93
  9.6 1.9 %collective-permute-start.1 = (bf16[512,512]{1,0:T(8,128)(2,1)S(1)}, bf16[512,512]{1,0:T(8,128)(2,1)S(1)}, u32[]{:S(2)}, u32[]{:S(2)}) collective-permute-start(bf16[512,512]{1,0:T(8,128)(2,1)S(1)} %copy-done.1), channel_id=1, source_target_pairs={{0,4},{2,6},{4,0},{6,2},{1,5},{3,7},{5,1},{7,3},{8,12},{10,14},{12... | collective-permute-start | bytes 1572872 | tf_op jit(solution)/shard_map/ppermute | solution.py:64
  12.1 1.6 %collective-permute-done.3 = bf16[160,256]{1,0:T(8,128)(2,1)S(1)} collective-permute-done((bf16[160,256]{1,0:T(8,128)(2,1)S(1)}, bf16[160,256]{1,0:T(8,128)(2,1)S(1)}, u32[]{:S(2)}, u32[]{:S(2)}) %collective-permute-start.3) | collective-permute-done | bytes 81952 | tf_op jit(solution)/shard_map/ppermute | solution.py:93
  13.7 2.0 %all-gather = bf16[4,160,256]{2,1,0:T(8,128)(2,1)S(1)} all-gather(bf16[2,160,256]{2,1,0:T(8,128)(2,1)S(1)} %pad_maximum_fusion.3), channel_id=2, replica_groups=mesh['kv'=4,'chip'=4,'core'=2] {'core'}, dimensions={0}, use_global_device_ids=true | all-gather | bytes 491520 | tf_op jit(solution)/shard_map/all_gather | solution.py:94
  15.8 0.6 fusion.30
  16.3 0.5 fusion.10
  16.8 0.7 %fusion = bf16[640,128]{1,0:T(8,128)(2,1)S(1)} fusion(f32[640,640]{0,1:T(8,128)S(1)} %get-tuple-element.28, f32[640]{0:T(1024)S(1)} %get-tuple-element.27, s32[640]{0:T(1024)S(1)} %le.61, s32[640]{0:T(1024)S(1)} %eq.26, s32[640]{0:T(1024)S(1)} %add.103, s32[640]{0:T(1024)S(1)} %broadcast_add_fusion, bf16[640,256]{1,0:T(8,128)(2,1)S(1)} %pad_maximum_fusion.2, ...), kind=kOutput, calls=%fused_computation.8 | convolution fusion | flops 107479040 | bytes 1990656 | tf_op jit(solution)/shard_map/dot_general | solution.py:128
  17.5 5.6 %collective-permute-done = bf16[512,512]{1,0:T(8,128)(2,1)S(1)} collective-permute-done((bf16[512,512]{1,0:T(8,128)(2,1)S(1)}, bf16[512,512]{1,0:T(8,128)(2,1)S(1)}, u32[]{:S(2)}, u32[]{:S(2)}) %collective-permute-start) | collective-permute-done | bytes 524320 | tf_op jit(solution)/shard_map/ppermute | solution.py:63
  23.1 1.7 %collective-permute-done.1 = bf16[512,512]{1,0:T(8,128)(2,1)S(1)} collective-permute-done((bf16[512,512]{1,0:T(8,128)(2,1)S(1)}, bf16[512,512]{1,0:T(8,128)(2,1)S(1)}, u32[]{:S(2)}, u32[]{:S(2)}) %collective-permute-start.1) | collective-permute-done | bytes 524320 | tf_op jit(solution)/shard_map/ppermute | solution.py:64
  24.8 0.4 collective-permute-start.4
  25.1 0.3 fusion.3
  25.5 5.4 %collective-permute-done.4 = bf16[160,512]{1,0:T(8,128)(2,1)S(1)} collective-permute-done((bf16[160,512]{1,0:T(8,128)(2,1)S(1)}, bf16[160,512]{1,0:T(8,128)(2,1)S(1)}, u32[]{:S(2)}, u32[]{:S(2)}) %collective-permute-start.4) | collective-permute-done | bytes 163872 | tf_op jit(solution)/shard_map/ppermute | solution.py:142
  30.9 0.3 convolution_convert_fusion
  31.2 0.3 collective-permute-start.5
  31.6 0.3 fusion.1
  31.9 0.3 fusion.2
  32.2 4.4 %collective-permute-done.5 = bf16[160,512]{1,0:T(8,128)(2,1)S(1)} collective-permute-done((bf16[160,512]{1,0:T(8,128)(2,1)S(1)}, bf16[160,512]{1,0:T(8,128)(2,1)S(1)}, u32[]{:S(2)}, u32[]{:S(2)}) %collective-permute-start.5) | collective-permute-done | bytes 163872 | tf_op jit(solution)/shard_map/ppermute | solution.py:143
  36.9 23.1 %all_to_all.5 = bf16[8,80,512]{2,1,0:T(8,128)(2,1)S(1)} all-to-all(bf16[8,80,512]{2,1,0:T(8,128)(2,1)S(1)} %bitcast.52), channel_id=1, replica_groups=mesh['kv'=4,'chip'=4,'core'=2] {'kv','core'}, dimensions={0} | all-to-all | bytes 1310720 | tf_op jit(solution)/shard_map/all_to_all | solution.py:161
  60.1 0.7 %pad_maximum_fusion.5 = bf16[80,1024]{1,0:T(8,128)(2,1)} fusion(bf16[80,512]{1,0:T(8,128)(2,1)S(1)} %get-tuple-element.20, bf16[80,512]{1,0:T(8,128)(2,1)S(1)} %get-tuple-element.19), kind=kLoop, calls=%fused_computation.38 | loop fusion | flops 327680 | bytes 327680 | tf_op jit(solution)/shard_map/concatenate | solution.py:165
  (58 shorter events, 2.0 us)
Async XLA Ops:
  0.6 1.9 %copy-start.4 = (bf16[128,128]{1,0:T(8,128)(2,1)S(1)}, bf16[128,128]{1,0:T(8,128)(2,1)}, u32[]{:S(2)}) copy-start(bf16[128,128]{1,0:T(8,128)(2,1)} %constant.72.clone) | copy-start | bytes 98308
  0.6 2.1 %copy-start = (bf16[512,512]{1,0:T(8,128)(2,1)S(1)}, bf16[512,512]{1,0:T(8,128)(2,1)}, u32[]{:S(2)}) copy-start(bf16[512,512]{1,0:T(8,128)(2,1)} %constant.73.clone) | copy-start | bytes 1572868
  0.7 1.9 %copy-start.5 = (bf16[80,128]{1,0:T(8,128)(2,1)S(1)}, bf16[80,128]{1,0:T(8,128)(2,1)}, u32[]{:S(2)}) copy-start(bf16[80,128]{1,0:T(8,128)(2,1)} %param.8) | copy-start | bytes 61444
  0.7 2.1 %copy-start.3 = (bf16[80,512]{1,0:T(8,128)(2,1)S(1)}, bf16[80,512]{1,0:T(8,128)(2,1)}, u32[]{:S(2)}) copy-start(bf16[80,512]{1,0:T(8,128)(2,1)} %param.7) | copy-start | bytes 245764
  1.9 1.0 %copy-start.6 = (bf16[80,128]{1,0:T(8,128)(2,1)S(1)}, bf16[80,128]{1,0:T(8,128)(2,1)}, u32[]{:S(2)}) copy-start(bf16[80,128]{1,0:T(8,128)(2,1)} %param.9) | copy-start | bytes 61444
  2.2 7.3 %copy-start.1 = (bf16[512,512]{1,0:T(8,128)(2,1)S(1)}, bf16[512,512]{1,0:T(8,128)(2,1)}, u32[]{:S(2)}) copy-start(bf16[512,512]{1,0:T(8,128)(2,1)} %param.11) | copy-start | bytes 1572868
  2.7 13.0 %copy-start.2 = (bf16[80,128]{1,0:T(8,128)(2,1)}, bf16[80,128]{1,0:T(8,128)(2,1)S(1)}, u32[]{:S(2)}) copy-start(bf16[80,128]{1,0:T(8,128)(2,1)S(1)} %fusion.9) | copy-start | bytes 61444
  5.1 7.0 %collective-permute-start.2 = (bf16[160,256]{1,0:T(8,128)(2,1)S(1)}, bf16[160,256]{1,0:T(8,128)(2,1)S(1)}, u32[]{:S(2)}, u32[]{:S(2)}) collective-permute-start(bf16[160,256]{1,0:T(8,128)(2,1)S(1)} %slice.75), channel_id=1, source_target_pairs={{0,2},{1,7},{2,4},{3,1},{4,6},{5,3},{6,0},{7,5},{8,10},{9,15},{10,... | collective-permute-start | bytes 245768 | tf_op jit(solution)/shard_map/ppermute | solution.py:93
  8.0 5.7 %collective-permute-start.3 = (bf16[160,256]{1,0:T(8,128)(2,1)S(1)}, bf16[160,256]{1,0:T(8,128)(2,1)S(1)}, u32[]{:S(2)}, u32[]{:S(2)}) collective-permute-start(bf16[160,256]{1,0:T(8,128)(2,1)S(1)} %slice.75), channel_id=1, source_target_pairs={{0,4},{1,5},{2,6},{3,7},{4,0},{5,1},{6,2},{7,3},{8,12},{9,13},{10,... | collective-permute-start | bytes 245768 | tf_op jit(solution)/shard_map/ppermute | solution.py:93
  9.5 13.6 %collective-permute-start = (bf16[512,512]{1,0:T(8,128)(2,1)S(1)}, bf16[512,512]{1,0:T(8,128)(2,1)S(1)}, u32[]{:S(2)}, u32[]{:S(2)}) collective-permute-start(bf16[512,512]{1,0:T(8,128)(2,1)S(1)} %copy-done.1), channel_id=1, source_target_pairs={{0,2},{2,0},{4,6},{6,4},{1,3},{3,1},{5,7},{7,5},{8,10},{10,8},{12,... | collective-permute-start | bytes 1572872 | tf_op jit(solution)/shard_map/ppermute | solution.py:63
  9.6 15.2 %collective-permute-start.1 = (bf16[512,512]{1,0:T(8,128)(2,1)S(1)}, bf16[512,512]{1,0:T(8,128)(2,1)S(1)}, u32[]{:S(2)}, u32[]{:S(2)}) collective-permute-start(bf16[512,512]{1,0:T(8,128)(2,1)S(1)} %copy-done.1), channel_id=1, source_target_pairs={{0,4},{2,6},{4,0},{6,2},{1,5},{3,7},{5,1},{7,3},{8,12},{10,14},{12... | collective-permute-start | bytes 1572872 | tf_op jit(solution)/shard_map/ppermute | solution.py:64
  24.8 6.1 %collective-permute-start.4 = (bf16[160,512]{1,0:T(8,128)(2,1)S(1)}, bf16[160,512]{1,0:T(8,128)(2,1)S(1)}, u32[]{:S(2)}, u32[]{:S(2)}) collective-permute-start(bf16[160,512]{1,0:T(8,128)(2,1)S(1)} %pad_maximum_fusion.4), channel_id=1, source_target_pairs={{0,2},{2,0},{4,6},{6,4},{1,3},{3,1},{5,7},{7,5},{8,10},{10,8},{12,... | collective-permute-start | bytes 491528 | tf_op jit(solution)/shard_map/ppermute | solution.py:142
  31.2 5.4 %collective-permute-start.5 = (bf16[160,512]{1,0:T(8,128)(2,1)S(1)}, bf16[160,512]{1,0:T(8,128)(2,1)S(1)}, u32[]{:S(2)}, u32[]{:S(2)}) collective-permute-start(bf16[160,512]{1,0:T(8,128)(2,1)S(1)} %convolution_convert_fusion), channel_id=1, source_target_pairs={{0,2},{2,0},{4,6},{6,4},{1,3},{3,1},{5,7},{7,5},{8,10},{10,8},{12,... | collective-permute-start | bytes 491528 | tf_op jit(solution)/shard_map/ppermute | solution.py:143

commit v17 on v15

--- a/solution.py
+++ b/solution.py
@@ -139,6 +139,7 @@
             return jnp.dot(att, w.T, preferred_element_type=jnp.float32).astype(jnp.bfloat16)
 
         att_x = lax.ppermute(chip_att, "chip", [(i, i ^ 1) for i in range(chips)])
+        w_x, w_y, att_x = lax.optimization_barrier((w_x, w_y, att_x))
         diag = lax.ppermute(part(att_x, w_y), "chip", [(i, i ^ 1) for i in range(chips)])
         by_dist = jnp.stack([part(chip_att, out_weight), part(chip_att, w_x), part(chip_att, w_y), diag])
         here = lax.axis_index("chip")

time: 62.7 us -> 56.7 us (0.904)
  waiting for transfers between devices: 19.7 us -> 13.2 us
  starting transfers between devices: 8.07 us -> 8.7 us
    ppermute x1, waiting for transfers between devices: 9.4 us -> 0.01 us  [body(): w_x = lax.ppermute(out_weight, 'chip', [(i, i ^ 1) for i in range(chips)])]
    ppermute x1, waiting for transfers between devices: 4.69 us -> 7.84 us  [body(): att_x = lax.ppermute(chip_att, 'chip', [(i, i ^ 1) for i in range(chips)])]
    ppermute x2, waiting for transfers between devices: 3.05 us -> 1.56 us  [body(): fetched.append(lax.ppermute(chip_kv, BLK, pairs))]
    ppermute x1, waiting for transfers between devices: 2.4 us -> 3.84 us  [body(): lax.ppermute(part(att_x, w_y), 'chip', [(i, i ^ 1) for i in range(chips)])]
    ppermute x1, starting transfers between devices: 0.51 us -> 1.92 us  [body(): w_y = lax.ppermute(out_weight, 'chip', [(i, i ^ 2) for i in range(chips)])]
    ppermute x1, starting transfers between devices: 0.91 us -> 0.08 us  [body(): w_x = lax.ppermute(out_weight, 'chip', [(i, i ^ 1) for i in range(chips)])]
  transfers between devices with their start and end apart: 6 -> 6, of which waited for: 6 -> 3; matrix products, arithmetic and copies ran while one was open for 6% -> 6% of each run, Pallas kernels for 0% -> 0%
where the time goes in v17:
time: 56.7 us; the launch traced here: 56.5 us
  blocking collectives  26.7 us (47%)
  waiting for transfers between devices  13.2 us (23%)
  starting transfers between devices  8.7 us (15%)
  matrix products  2.88 us (5%)
  other arithmetic  2.86 us (5%)
  local copies, waits for them, and re-layouts  1.05 us (2%)
  between operations  1.03 us (2%)
    all_to_all x1, blocking collectives, body(): got = lax.all_to_all(routed, ('kv', 'core'), 0, 0, tiled=True)  22.6 us
    ppermute x1, waiting for transfers between devices, body(): att_x = lax.ppermute(chip_att, 'chip', [(i, i ^ 1) for i in range(chips)])  7.84 us
    ppermute x2, starting transfers between devices, body(): fetched.append(lax.ppermute(chip_kv, BLK, pairs))  4.41 us
    ppermute x1, waiting for transfers between devices, body(): lax.ppermute(part(att_x, w_y), 'chip', [(i, i ^ 1) for i in range(chips)])  3.84 us
    all_gather x1, blocking collectives, body(): lax.all_gather(jnp.concatenate([rot_queries, rot_keys, values], axis=1),...  2.07 us
    all_gather x1, blocking collectives, body(): both = lax.all_gather(jnp.stack(fetched, 0), 'core', axis=0, tiled=False)  2.04 us
    ppermute x1, starting transfers between devices, body(): w_y = lax.ppermute(out_weight, 'chip', [(i, i ^ 2) for i in range(chips)])  1.92 us
    ppermute x2, waiting for transfers between devices, body(): fetched.append(lax.ppermute(chip_kv, BLK, pairs))  1.56 us
  transfers between devices with their start and end apart: 6, of which 3 were waited for; matrix products, arithmetic and copies ran while one was open for 6% of the time, Pallas kernels for 0%

profile of v17, /device:TPU:0, one launch (start us, length us, event | category | flops | bytes accessed | tf_op | source)
XLA Modules:
  0.0 56.5 jit_solution(729830141397900832)
XLA Ops:
  0.7 0.8 %select_reduce_fusion.1 = s32[5]{0:T(128)S(1)} fusion(s32[4]{0:T(128)} %param.10, s32[5]{0:T(128)S(1)} %iota_add_fusion.3), kind=kLoop, calls=%fused_computation.54 | loop fusion | flops 55 | bytes 56 | tf_op jit(solution)/shard_map/reduce_sum | solution.py:53
  1.6 0.2 multiply_cosine_fusion
  2.3 0.1 tile.23
  2.6 0.1 fusion.9
  2.8 0.2 fusion.6
  3.0 2.1 %all_gather.9 = bf16[160,768]{1,0:T(8,128)(2,1)S(1)} all-gather(bf16[80,768]{1,0:T(8,128)(2,1)S(1)} %pad_maximum_fusion.6), channel_id=1, replica_groups=mesh['kv'=4,'chip'=4,'core'=2] {'core'}, dimensions={0}, use_global_device_ids=true | all-gather | bytes 368640 | tf_op jit(solution)/shard_map/all_gather | solution.py:80
  5.1 2.9 %collective-permute-start = (bf16[160,256]{1,0:T(8,128)(2,1)S(1)}, bf16[160,256]{1,0:T(8,128)(2,1)S(1)}, u32[]{:S(2)}, u32[]{:S(2)}) collective-permute-start(bf16[160,256]{1,0:T(8,128)(2,1)S(1)} %slice.75), channel_id=1, source_target_pairs={{0,2},{1,7},{2,4},{3,1},{4,6},{5,3},{6,0},{7,5},{8,10},{9,15},{10,... | collective-permute-start | bytes 245768 | tf_op jit(solution)/shard_map/ppermute | solution.py:93
  8.0 1.5 %collective-permute-start.1 = (bf16[160,256]{1,0:T(8,128)(2,1)S(1)}, bf16[160,256]{1,0:T(8,128)(2,1)S(1)}, u32[]{:S(2)}, u32[]{:S(2)}) collective-permute-start(bf16[160,256]{1,0:T(8,128)(2,1)S(1)} %slice.75), channel_id=1, source_target_pairs={{0,4},{1,5},{2,6},{3,7},{4,0},{5,1},{6,2},{7,3},{8,12},{9,13},{10,... | collective-permute-start | bytes 245768 | tf_op jit(solution)/shard_map/ppermute | solution.py:93
  9.6 1.9 %collective-permute-start.3 = (bf16[512,512]{1,0:T(8,128)(2,1)S(1)}, bf16[512,512]{1,0:T(8,128)(2,1)S(1)}, u32[]{:S(2)}, u32[]{:S(2)}) collective-permute-start(bf16[512,512]{1,0:T(8,128)(2,1)S(1)} %copy-done.6), channel_id=1, source_target_pairs={{0,4},{2,6},{4,0},{6,2},{1,5},{3,7},{5,1},{7,3},{8,12},{10,14},{12... | collective-permute-start | bytes 1572872 | tf_op jit(solution)/shard_map/ppermute | solution.py:64
  12.1 1.6 %collective-permute-done.1 = bf16[160,256]{1,0:T(8,128)(2,1)S(1)} collective-permute-done((bf16[160,256]{1,0:T(8,128)(2,1)S(1)}, bf16[160,256]{1,0:T(8,128)(2,1)S(1)}, u32[]{:S(2)}, u32[]{:S(2)}) %collective-permute-start.1) | collective-permute-done | bytes 81952 | tf_op jit(solution)/shard_map/ppermute | solution.py:93
  13.7 2.0 %all-gather = bf16[4,160,256]{2,1,0:T(8,128)(2,1)S(1)} all-gather(bf16[2,160,256]{2,1,0:T(8,128)(2,1)S(1)} %pad_maximum_fusion.3), channel_id=2, replica_groups=mesh['kv'=4,'chip'=4,'core'=2] {'core'}, dimensions={0}, use_global_device_ids=true | all-gather | bytes 491520 | tf_op jit(solution)/shard_map/all_gather | solution.py:94
  15.8 0.6 fusion.30
  16.3 0.5 fusion.10
  16.8 0.7 %fusion = bf16[640,128]{1,0:T(8,128)(2,1)S(1)} fusion(f32[640,640]{0,1:T(8,128)S(1)} %get-tuple-element.28, f32[640]{0:T(1024)S(1)} %get-tuple-element.27, s32[640]{0:T(1024)S(1)} %le.61, s32[640]{0:T(1024)S(1)} %eq.26, s32[640]{0:T(1024)S(1)} %add.103, s32[640]{0:T(1024)S(1)} %broadcast_add_fusion, bf16[640,256]{1,0:T(8,128)(2,1)S(1)} %pad_maximum_fusion.2, ...), kind=kOutput, calls=%fused_computation.8 | convolution fusion | flops 107479040 | bytes 1990656 | tf_op jit(solution)/shard_map/dot_general | solution.py:128
  17.5 0.9 %collective-permute-start.4 = (bf16[160,512]{1,0:T(8,128)(2,1)S(1)}, bf16[160,512]{1,0:T(8,128)(2,1)S(1)}, u32[]{:S(2)}, u32[]{:S(2)}) collective-permute-start(bf16[160,512]{1,0:T(8,128)(2,1)S(1)} %pad_maximum_fusion.4), channel_id=1, source_target_pairs={{0,2},{2,0},{4,6},{6,4},{1,3},{3,1},{5,7},{7,5},{8,10},{10,8},{12,... | collective-permute-start | bytes 491528 | tf_op jit(solution)/shard_map/ppermute | solution.py:141
  18.5 0.3 fusion.1
  18.8 7.8 %collective-permute-done.4 = bf16[160,512]{1,0:T(8,128)(2,1)S(1)} collective-permute-done((bf16[160,512]{1,0:T(8,128)(2,1)S(1)}, bf16[160,512]{1,0:T(8,128)(2,1)S(1)}, u32[]{:S(2)}, u32[]{:S(2)}) %collective-permute-start.4) | collective-permute-done | bytes 163872 | tf_op jit(solution)/shard_map/ppermute | solution.py:141
  26.6 0.3 convolution_convert_fusion
  27.0 1.4 %collective-permute-start.5 = (bf16[160,512]{1,0:T(8,128)(2,1)S(1)}, bf16[160,512]{1,0:T(8,128)(2,1)S(1)}, u32[]{:S(2)}, u32[]{:S(2)}) collective-permute-start(bf16[160,512]{1,0:T(8,128)(2,1)S(1)} %convolution_convert_fusion), channel_id=1, source_target_pairs={{0,2},{2,0},{4,6},{6,4},{1,3},{3,1},{5,7},{7,5},{8,10},{10,8},{12,... | collective-permute-start | bytes 491528 | tf_op jit(solution)/shard_map/ppermute | solution.py:143
  28.3 0.3 fusion.3
  28.7 0.3 fusion.2
  29.0 3.8 %collective-permute-done.5 = bf16[160,512]{1,0:T(8,128)(2,1)S(1)} collective-permute-done((bf16[160,512]{1,0:T(8,128)(2,1)S(1)}, bf16[160,512]{1,0:T(8,128)(2,1)S(1)}, u32[]{:S(2)}, u32[]{:S(2)}) %collective-permute-start.5) | collective-permute-done | bytes 163872 | tf_op jit(solution)/shard_map/ppermute | solution.py:143
  33.1 22.6 %all_to_all.5 = bf16[8,80,512]{2,1,0:T(8,128)(2,1)S(1)} all-to-all(bf16[8,80,512]{2,1,0:T(8,128)(2,1)S(1)} %bitcast.49), channel_id=1, replica_groups=mesh['kv'=4,'chip'=4,'core'=2] {'kv','core'}, dimensions={0} | all-to-all | bytes 1310720 | tf_op jit(solution)/shard_map/all_to_all | solution.py:161
  55.8 0.7 %pad_maximum_fusion.5 = bf16[80,1024]{1,0:T(8,128)(2,1)} fusion(bf16[80,512]{1,0:T(8,128)(2,1)S(1)} %get-tuple-element.20, bf16[80,512]{1,0:T(8,128)(2,1)S(1)} %get-tuple-element.19), kind=kLoop, calls=%fused_computation.38 | loop fusion | flops 327680 | bytes 327680 | tf_op jit(solution)/shard_map/concatenate | solution.py:165
  (58 shorter events, 1.7 us)
Async XLA Ops:
  0.6 1.9 %copy-start.3 = (bf16[128,128]{1,0:T(8,128)(2,1)S(1)}, bf16[128,128]{1,0:T(8,128)(2,1)}, u32[]{:S(2)}) copy-start(bf16[128,128]{1,0:T(8,128)(2,1)} %constant.72.clone) | copy-start | bytes 98308
  0.6 2.1 %copy-start = (bf16[512,512]{1,0:T(8,128)(2,1)S(1)}, bf16[512,512]{1,0:T(8,128)(2,1)}, u32[]{:S(2)}) copy-start(bf16[512,512]{1,0:T(8,128)(2,1)} %constant.73.clone) | copy-start | bytes 1572868
  0.7 1.9 %copy-start.4 = (bf16[80,128]{1,0:T(8,128)(2,1)S(1)}, bf16[80,128]{1,0:T(8,128)(2,1)}, u32[]{:S(2)}) copy-start(bf16[80,128]{1,0:T(8,128)(2,1)} %param.8) | copy-start | bytes 61444
  0.7 2.1 %copy-start.2 = (bf16[80,512]{1,0:T(8,128)(2,1)S(1)}, bf16[80,512]{1,0:T(8,128)(2,1)}, u32[]{:S(2)}) copy-start(bf16[80,512]{1,0:T(8,128)(2,1)} %param.7) | copy-start | bytes 245764
  1.9 1.0 %copy-start.5 = (bf16[80,128]{1,0:T(8,128)(2,1)S(1)}, bf16[80,128]{1,0:T(8,128)(2,1)}, u32[]{:S(2)}) copy-start(bf16[80,128]{1,0:T(8,128)(2,1)} %param.9) | copy-start | bytes 61444
  2.2 7.3 %copy-start.6 = (bf16[512,512]{1,0:T(8,128)(2,1)S(1)}, bf16[512,512]{1,0:T(8,128)(2,1)}, u32[]{:S(2)}) copy-start(bf16[512,512]{1,0:T(8,128)(2,1)} %param.11) | copy-start | bytes 1572868
  2.7 13.0 %copy-start.1 = (bf16[80,128]{1,0:T(8,128)(2,1)}, bf16[80,128]{1,0:T(8,128)(2,1)S(1)}, u32[]{:S(2)}) copy-start(bf16[80,128]{1,0:T(8,128)(2,1)S(1)} %fusion.9) | copy-start | bytes 61444
  5.1 7.0 %collective-permute-start = (bf16[160,256]{1,0:T(8,128)(2,1)S(1)}, bf16[160,256]{1,0:T(8,128)(2,1)S(1)}, u32[]{:S(2)}, u32[]{:S(2)}) collective-permute-start(bf16[160,256]{1,0:T(8,128)(2,1)S(1)} %slice.75), channel_id=1, source_target_pairs={{0,2},{1,7},{2,4},{3,1},{4,6},{5,3},{6,0},{7,5},{8,10},{9,15},{10,... | collective-permute-start | bytes 245768 | tf_op jit(solution)/shard_map/ppermute | solution.py:93
  8.0 5.7 %collective-permute-start.1 = (bf16[160,256]{1,0:T(8,128)(2,1)S(1)}, bf16[160,256]{1,0:T(8,128)(2,1)S(1)}, u32[]{:S(2)}, u32[]{:S(2)}) collective-permute-start(bf16[160,256]{1,0:T(8,128)(2,1)S(1)} %slice.75), channel_id=1, source_target_pairs={{0,4},{1,5},{2,6},{3,7},{4,0},{5,1},{6,2},{7,3},{8,12},{9,13},{10,... | collective-permute-start | bytes 245768 | tf_op jit(solution)/shard_map/ppermute | solution.py:93
  9.5 17.1 %collective-permute-start.2 = (bf16[512,512]{1,0:T(8,128)(2,1)S(1)}, bf16[512,512]{1,0:T(8,128)(2,1)S(1)}, u32[]{:S(2)}, u32[]{:S(2)}) collective-permute-start(bf16[512,512]{1,0:T(8,128)(2,1)S(1)} %copy-done.6), channel_id=1, source_target_pairs={{0,2},{2,0},{4,6},{6,4},{1,3},{3,1},{5,7},{7,5},{8,10},{10,8},{12,... | collective-permute-start | bytes 1572872 | tf_op jit(solution)/shard_map/ppermute | solution.py:63
  9.6 17.1 %collective-permute-start.3 = (bf16[512,512]{1,0:T(8,128)(2,1)S(1)}, bf16[512,512]{1,0:T(8,128)(2,1)S(1)}, u32[]{:S(2)}, u32[]{:S(2)}) collective-permute-start(bf16[512,512]{1,0:T(8,128)(2,1)S(1)} %copy-done.6), channel_id=1, source_target_pairs={{0,4},{2,6},{4,0},{6,2},{1,5},{3,7},{5,1},{7,3},{8,12},{10,14},{12... | collective-permute-start | bytes 1572872 | tf_op jit(solution)/shard_map/ppermute | solution.py:64
  17.5 9.1 %collective-permute-start.4 = (bf16[160,512]{1,0:T(8,128)(2,1)S(1)}, bf16[160,512]{1,0:T(8,128)(2,1)S(1)}, u32[]{:S(2)}, u32[]{:S(2)}) collective-permute-start(bf16[160,512]{1,0:T(8,128)(2,1)S(1)} %pad_maximum_fusion.4), channel_id=1, source_target_pairs={{0,2},{2,0},{4,6},{6,4},{1,3},{3,1},{5,7},{7,5},{8,10},{10,8},{12,... | collective-permute-start | bytes 491528 | tf_op jit(solution)/shard_map/ppermute | solution.py:141
  27.0 5.9 %collective-permute-start.5 = (bf16[160,512]{1,0:T(8,128)(2,1)S(1)}, bf16[160,512]{1,0:T(8,128)(2,1)S(1)}, u32[]{:S(2)}, u32[]{:S(2)}) collective-permute-start(bf16[160,512]{1,0:T(8,128)(2,1)S(1)} %convolution_convert_fusion), channel_id=1, source_target_pairs={{0,2},{2,0},{4,6},{6,4},{1,3},{3,1},{5,7},{7,5},{8,10},{10,8},{12,... | collective-permute-start | bytes 491528 | tf_op jit(solution)/shard_map/ppermute | solution.py:143

commit v18 on v15

--- a/solution.py
+++ b/solution.py
@@ -138,8 +138,15 @@
         def part(att, w):
             return jnp.dot(att, w.T, preferred_element_type=jnp.float32).astype(jnp.bfloat16)
 
-        att_x = lax.ppermute(chip_att, "chip", [(i, i ^ 1) for i in range(chips)])
-        diag = lax.ppermute(part(att_x, w_y), "chip", [(i, i ^ 1) for i in range(chips)])
+        x_pairs = [(i, i ^ 1) for i in range(chips)]
+        y_pairs = [(i, i ^ 2) for i in range(chips)]
+        att_x = lax.ppermute(chip_att, "chip", x_pairs)
+        att_y = lax.ppermute(chip_att, "chip", y_pairs)
+        w_x, w_y, att_x, att_y = lax.optimization_barrier((w_x, w_y, att_x, att_y))
+        cut = per_c // 2
+        back_x = lax.ppermute(part(att_x, w_y[:cut]), "chip", x_pairs)
+        back_y = lax.ppermute(part(att_y, w_x[cut:]), "chip", y_pairs)
+        diag = jnp.concatenate([back_x, back_y], axis=1)
         by_dist = jnp.stack([part(chip_att, out_weight), part(chip_att, w_x), part(chip_att, w_y), diag])
         here = lax.axis_index("chip")
         routed = jnp.stack(

time: 62.7 us -> 58.1 us (0.927)
  waiting for transfers between devices: 19.7 us -> 13.2 us
  starting transfers between devices: 8.07 us -> 9.81 us
    ppermute x1, waiting for transfers between devices: 9.4 us -> 0.01 us  [body(): w_x = lax.ppermute(out_weight, 'chip', [(i, i ^ 1) for i in range(chips)])]
    ppermute x2 -> x4, waiting for transfers between devices: 7.09 us -> 11.6 us  [the longest x1 7.03 us: body(): att_x = lax.ppermute(chip_att, 'chip', x_pairs)]
    ppermute x2, waiting for transfers between devices: 3.05 us -> 1.56 us  [body(): fetched.append(lax.ppermute(chip_kv, BLK, pairs))]
    ppermute x1, starting transfers between devices: 0.51 us -> 1.92 us  [body(): w_y = lax.ppermute(out_weight, 'chip', [(i, i ^ 2) for i in range(chips)])]
    ppermute x2 -> x4, starting transfers between devices: 2.25 us -> 3.4 us  [the longest x1 1.25 us: body(): back_y = lax.ppermute(part(att_y, w_x[cut:]), 'chip', y_pairs)]
    ppermute x1, starting transfers between devices: 0.91 us -> 0.08 us  [body(): w_x = lax.ppermute(out_weight, 'chip', [(i, i ^ 1) for i in range(chips)])]
    dot_general x4 -> x5, matrix products: 1.28 us -> 1.4 us  [part(): jnp.dot(att, w.T, preferred_element_type=jnp.float32).astype(jnp.bfloat16)]
  transfers between devices with their start and end apart: 6 -> 8, of which waited for: 6 -> 5; matrix products, arithmetic and copies ran while one was open for 6% -> 6% of each run, Pallas kernels for 0% -> 0%
where the time goes in v18:
time: 58.1 us; the launch traced here: 57.9 us
  blocking collectives  27 us (46%)
  waiting for transfers between devices  13.2 us (23%)
  starting transfers between devices  9.81 us (17%)
  matrix products  3 us (5%)
  other arithmetic  2.87 us (5%)
  local copies, waits for them, and re-layouts  1.05 us (2%)
  between operations  1.05 us (2%)
    all_to_all x1, blocking collectives, body(): got = lax.all_to_all(routed, ('kv', 'core'), 0, 0, tiled=True)  22.8 us
    ppermute x1, waiting for transfers between devices, body(): att_x = lax.ppermute(chip_att, 'chip', x_pairs)  7.03 us
    ppermute x2, starting transfers between devices, body(): fetched.append(lax.ppermute(chip_kv, BLK, pairs))  4.41 us
    ppermute x1, waiting for transfers between devices, body(): back_x = lax.ppermute(part(att_x, w_y[:cut]), 'chip', x_pairs)  2.27 us
    all_gather x1, blocking collectives, body(): lax.all_gather(jnp.concatenate([rot_queries, rot_keys, values], axis=1),...  2.07 us
    all_gather x1, blocking collectives, body(): both = lax.all_gather(jnp.stack(fetched, 0), 'core', axis=0, tiled=False)  2.04 us
    ppermute x1, starting transfers between devices, body(): w_y = lax.ppermute(out_weight, 'chip', [(i, i ^ 2) for i in range(chips)])  1.92 us
    ppermute x1, waiting for transfers between devices, body(): att_y = lax.ppermute(chip_att, 'chip', y_pairs)  1.66 us
  transfers between devices with their start and end apart: 8, of which 5 were waited for; matrix products, arithmetic and copies ran while one was open for 6% of the time, Pallas kernels for 0%

profile of v18, /device:TPU:0, one launch (start us, length us, event | category | flops | bytes accessed | tf_op | source)
XLA Modules:
  0.0 57.9 jit_solution(17380618278668088378)
XLA Ops:
  0.7 0.8 %select_reduce_fusion.1 = s32[5]{0:T(128)S(1)} fusion(s32[4]{0:T(128)} %param.10, s32[5]{0:T(128)S(1)} %iota_add_fusion.3), kind=kLoop, calls=%fused_computation.58 | loop fusion | flops 55 | bytes 56 | tf_op jit(solution)/shard_map/reduce_sum | solution.py:53
  3.0 2.1 %all_gather.9 = bf16[160,768]{1,0:T(8,128)(2,1)S(1)} all-gather(bf16[80,768]{1,0:T(8,128)(2,1)S(1)} %pad_maximum_fusion.6), channel_id=1, replica_groups=mesh['kv'=4,'chip'=4,'core'=2] {'core'}, dimensions={0}, use_global_device_ids=true | all-gather | bytes 368640 | tf_op jit(solution)/shard_map/all_gather | solution.py:80
  5.1 2.9 %collective-permute-start = (bf16[160,256]{1,0:T(8,128)(2,1)S(1)}, bf16[160,256]{1,0:T(8,128)(2,1)S(1)}, u32[]{:S(2)}, u32[]{:S(2)}) collective-permute-start(bf16[160,256]{1,0:T(8,128)(2,1)S(1)} %slice.83), channel_id=1, source_target_pairs={{0,2},{1,7},{2,4},{3,1},{4,6},{5,3},{6,0},{7,5},{8,10},{9,15},{10,... | collective-permute-start | bytes 245768 | tf_op jit(solution)/shard_map/ppermute | solution.py:93
  8.0 1.5 %collective-permute-start.1 = (bf16[160,256]{1,0:T(8,128)(2,1)S(1)}, bf16[160,256]{1,0:T(8,128)(2,1)S(1)}, u32[]{:S(2)}, u32[]{:S(2)}) collective-permute-start(bf16[160,256]{1,0:T(8,128)(2,1)S(1)} %slice.83), channel_id=1, source_target_pairs={{0,4},{1,5},{2,6},{3,7},{4,0},{5,1},{6,2},{7,3},{8,12},{9,13},{10,... | collective-permute-start | bytes 245768 | tf_op jit(solution)/shard_map/ppermute | solution.py:93
  9.6 1.9 %collective-permute-start.3 = (bf16[512,512]{1,0:T(8,128)(2,1)S(1)}, bf16[512,512]{1,0:T(8,128)(2,1)S(1)}, u32[]{:S(2)}, u32[]{:S(2)}) collective-permute-start(bf16[512,512]{1,0:T(8,128)(2,1)S(1)} %copy-done.6), channel_id=1, source_target_pairs={{0,4},{2,6},{4,0},{6,2},{1,5},{3,7},{5,1},{7,3},{8,12},{10,14},{12... | collective-permute-start | bytes 1572872 | tf_op jit(solution)/shard_map/ppermute | solution.py:64
  12.1 1.6 %collective-permute-done.1 = bf16[160,256]{1,0:T(8,128)(2,1)S(1)} collective-permute-done((bf16[160,256]{1,0:T(8,128)(2,1)S(1)}, bf16[160,256]{1,0:T(8,128)(2,1)S(1)}, u32[]{:S(2)}, u32[]{:S(2)}) %collective-permute-start.1) | collective-permute-done | bytes 81952 | tf_op jit(solution)/shard_map/ppermute | solution.py:93
  13.7 2.0 %all-gather = bf16[4,160,256]{2,1,0:T(8,128)(2,1)S(1)} all-gather(bf16[2,160,256]{2,1,0:T(8,128)(2,1)S(1)} %pad_maximum_fusion.3), channel_id=2, replica_groups=mesh['kv'=4,'chip'=4,'core'=2] {'core'}, dimensions={0}, use_global_device_ids=true | all-gather | bytes 491520 | tf_op jit(solution)/shard_map/all_gather | solution.py:94
  15.8 0.6 fusion.32
  16.3 0.5 fusion.10
  16.8 0.7 %fusion = bf16[640,128]{1,0:T(8,128)(2,1)S(1)} fusion(f32[640,640]{0,1:T(8,128)S(1)} %get-tuple-element.30, f32[640]{0:T(1024)S(1)} %get-tuple-element.29, s32[640]{0:T(1024)S(1)} %le.61, s32[640]{0:T(1024)S(1)} %eq.26, s32[640]{0:T(1024)S(1)} %add.103, s32[640]{0:T(1024)S(1)} %broadcast_add_fusion, bf16[640,256]{1,0:T(8,128)(2,1)S(1)} %pad_maximum_fusion.2, ...), kind=kOutput, calls=%fused_computation.7 | convolution fusion | flops 107479040 | bytes 1990656 | tf_op jit(solution)/shard_map/dot_general | solution.py:128
  17.5 0.9 %collective-permute-start.4 = (bf16[160,512]{1,0:T(8,128)(2,1)S(1)}, bf16[160,512]{1,0:T(8,128)(2,1)S(1)}, u32[]{:S(2)}, u32[]{:S(2)}) collective-permute-start(bf16[160,512]{1,0:T(8,128)(2,1)S(1)} %pad_maximum_fusion.4), channel_id=1, source_target_pairs={{0,2},{2,0},{4,6},{6,4},{1,3},{3,1},{5,7},{7,5},{8,10},{10,8},{12,... | collective-permute-start | bytes 491528 | tf_op jit(solution)/shard_map/ppermute | solution.py:143
  18.5 0.8 %collective-permute-start.5 = (bf16[160,512]{1,0:T(8,128)(2,1)S(1)}, bf16[160,512]{1,0:T(8,128)(2,1)S(1)}, u32[]{:S(2)}, u32[]{:S(2)}) collective-permute-start(bf16[160,512]{1,0:T(8,128)(2,1)S(1)} %pad_maximum_fusion.4), channel_id=1, source_target_pairs={{0,4},{2,6},{4,0},{6,2},{1,5},{3,7},{5,1},{7,3},{8,12},{10,14},{12... | collective-permute-start | bytes 491528 | tf_op jit(solution)/shard_map/ppermute | solution.py:144
  19.3 0.3 fusion.1
  19.6 7.0 %collective-permute-done.4 = bf16[160,512]{1,0:T(8,128)(2,1)S(1)} collective-permute-done((bf16[160,512]{1,0:T(8,128)(2,1)S(1)}, bf16[160,512]{1,0:T(8,128)(2,1)S(1)}, u32[]{:S(2)}, u32[]{:S(2)}) %collective-permute-start.4) | collective-permute-done | bytes 163872 | tf_op jit(solution)/shard_map/ppermute | solution.py:143
  26.6 1.7 %collective-permute-done.5 = bf16[160,512]{1,0:T(8,128)(2,1)S(1)} collective-permute-done((bf16[160,512]{1,0:T(8,128)(2,1)S(1)}, bf16[160,512]{1,0:T(8,128)(2,1)S(1)}, u32[]{:S(2)}, u32[]{:S(2)}) %collective-permute-start.5) | collective-permute-done | bytes 163872 | tf_op jit(solution)/shard_map/ppermute | solution.py:144
  28.3 0.3 fusion.2
  28.6 0.2 convolution_convert_fusion.4
  28.9 0.4 collective-permute-start.6
  29.5 1.2 %collective-permute-start.7 = (bf16[160,256]{1,0:T(8,128)(2,1)S(1)}, bf16[160,256]{1,0:T(8,128)(2,1)S(1)}, u32[]{:S(2)}, u32[]{:S(2)}) collective-permute-start(bf16[160,256]{1,0:T(8,128)(2,1)S(1)} %convolution_convert_fusion.3), channel_id=1, source_target_pairs={{0,4},{2,6},{4,0},{6,2},{1,5},{3,7},{5,1},{7,3},{8,12},{10,14},{12... | collective-permute-start | bytes 245768 | tf_op jit(solution)/shard_map/ppermute | solution.py:148
  30.8 0.3 fusion.3
  31.1 2.3 %collective-permute-done.6 = bf16[160,256]{1,0:T(8,128)(2,1)S(1)} collective-permute-done((bf16[160,256]{1,0:T(8,128)(2,1)S(1)}, bf16[160,256]{1,0:T(8,128)(2,1)S(1)}, u32[]{:S(2)}, u32[]{:S(2)}) %collective-permute-start.6) | collective-permute-done | bytes 81952 | tf_op jit(solution)/shard_map/ppermute | solution.py:147
  33.4 0.7 %collective-permute-done.7 = bf16[160,256]{1,0:T(8,128)(2,1)S(1)} collective-permute-done((bf16[160,256]{1,0:T(8,128)(2,1)S(1)}, bf16[160,256]{1,0:T(8,128)(2,1)S(1)}, u32[]{:S(2)}, u32[]{:S(2)}) %collective-permute-start.7) | collective-permute-done | bytes 81952 | tf_op jit(solution)/shard_map/ppermute | solution.py:148
  34.3 22.8 %all_to_all.5 = bf16[8,80,512]{2,1,0:T(8,128)(2,1)S(1)} all-to-all(bf16[8,80,512]{2,1,0:T(8,128)(2,1)S(1)} %bitcast.50), channel_id=1, replica_groups=mesh['kv'=4,'chip'=4,'core'=2] {'kv','core'}, dimensions={0} | all-to-all | bytes 1310720 | tf_op jit(solution)/shard_map/all_to_all | solution.py:167
  57.3 0.7 %pad_maximum_fusion.5 = bf16[80,1024]{1,0:T(8,128)(2,1)} fusion(bf16[80,512]{1,0:T(8,128)(2,1)S(1)} %get-tuple-element.22, bf16[80,512]{1,0:T(8,128)(2,1)S(1)} %get-tuple-element.21), kind=kLoop, calls=%fused_computation.42 | loop fusion | flops 327680 | bytes 327680 | tf_op jit(solution)/shard_map/concatenate | solution.py:171
  (64 shorter events, 2.6 us)
Async XLA Ops:
  0.6 1.9 %copy-start.3 = (bf16[128,128]{1,0:T(8,128)(2,1)S(1)}, bf16[128,128]{1,0:T(8,128)(2,1)}, u32[]{:S(2)}) copy-start(bf16[128,128]{1,0:T(8,128)(2,1)} %constant.72.clone) | copy-start | bytes 98308
  0.6 2.1 %copy-start = (bf16[512,512]{1,0:T(8,128)(2,1)S(1)}, bf16[512,512]{1,0:T(8,128)(2,1)}, u32[]{:S(2)}) copy-start(bf16[512,512]{1,0:T(8,128)(2,1)} %constant.73.clone) | copy-start | bytes 1572868
  0.7 1.9 %copy-start.4 = (bf16[80,128]{1,0:T(8,128)(2,1)S(1)}, bf16[80,128]{1,0:T(8,128)(2,1)}, u32[]{:S(2)}) copy-start(bf16[80,128]{1,0:T(8,128)(2,1)} %param.8) | copy-start | bytes 61444
  0.7 2.1 %copy-start.2 = (bf16[80,512]{1,0:T(8,128)(2,1)S(1)}, bf16[80,512]{1,0:T(8,128)(2,1)}, u32[]{:S(2)}) copy-start(bf16[80,512]{1,0:T(8,128)(2,1)} %param.7) | copy-start | bytes 245764
  1.9 1.0 %copy-start.5 = (bf16[80,128]{1,0:T(8,128)(2,1)S(1)}, bf16[80,128]{1,0:T(8,128)(2,1)}, u32[]{:S(2)}) copy-start(bf16[80,128]{1,0:T(8,128)(2,1)} %param.9) | copy-start | bytes 61444
  2.2 7.3 %copy-start.6 = (bf16[512,512]{1,0:T(8,128)(2,1)S(1)}, bf16[512,512]{1,0:T(8,128)(2,1)}, u32[]{:S(2)}) copy-start(bf16[512,512]{1,0:T(8,128)(2,1)} %param.11) | copy-start | bytes 1572868
  2.7 13.0 %copy-start.1 = (bf16[80,128]{1,0:T(8,128)(2,1)}, bf16[80,128]{1,0:T(8,128)(2,1)S(1)}, u32[]{:S(2)}) copy-start(bf16[80,128]{1,0:T(8,128)(2,1)S(1)} %fusion.9) | copy-start | bytes 61444
  5.1 7.0 %collective-permute-start = (bf16[160,256]{1,0:T(8,128)(2,1)S(1)}, bf16[160,256]{1,0:T(8,128)(2,1)S(1)}, u32[]{:S(2)}, u32[]{:S(2)}) collective-permute-start(bf16[160,256]{1,0:T(8,128)(2,1)S(1)} %slice.83), channel_id=1, source_target_pairs={{0,2},{1,7},{2,4},{3,1},{4,6},{5,3},{6,0},{7,5},{8,10},{9,15},{10,... | collective-permute-start | bytes 245768 | tf_op jit(solution)/shard_map/ppermute | solution.py:93
  8.0 5.7 %collective-permute-start.1 = (bf16[160,256]{1,0:T(8,128)(2,1)S(1)}, bf16[160,256]{1,0:T(8,128)(2,1)S(1)}, u32[]{:S(2)}, u32[]{:S(2)}) collective-permute-start(bf16[160,256]{1,0:T(8,128)(2,1)S(1)} %slice.83), channel_id=1, source_target_pairs={{0,4},{1,5},{2,6},{3,7},{4,0},{5,1},{6,2},{7,3},{8,12},{9,13},{10,... | collective-permute-start | bytes 245768 | tf_op jit(solution)/shard_map/ppermute | solution.py:93
  9.5 18.8 %collective-permute-start.2 = (bf16[512,512]{1,0:T(8,128)(2,1)S(1)}, bf16[512,512]{1,0:T(8,128)(2,1)S(1)}, u32[]{:S(2)}, u32[]{:S(2)}) collective-permute-start(bf16[512,512]{1,0:T(8,128)(2,1)S(1)} %copy-done.6), channel_id=1, source_target_pairs={{0,2},{2,0},{4,6},{6,4},{1,3},{3,1},{5,7},{7,5},{8,10},{10,8},{12,... | collective-permute-start | bytes 1572872 | tf_op jit(solution)/shard_map/ppermute | solution.py:63
  9.6 18.7 %collective-permute-start.3 = (bf16[512,512]{1,0:T(8,128)(2,1)S(1)}, bf16[512,512]{1,0:T(8,128)(2,1)S(1)}, u32[]{:S(2)}, u32[]{:S(2)}) collective-permute-start(bf16[512,512]{1,0:T(8,128)(2,1)S(1)} %copy-done.6), channel_id=1, source_target_pairs={{0,4},{2,6},{4,0},{6,2},{1,5},{3,7},{5,1},{7,3},{8,12},{10,14},{12... | collective-permute-start | bytes 1572872 | tf_op jit(solution)/shard_map/ppermute | solution.py:64
  17.5 9.1 %collective-permute-start.4 = (bf16[160,512]{1,0:T(8,128)(2,1)S(1)}, bf16[160,512]{1,0:T(8,128)(2,1)S(1)}, u32[]{:S(2)}, u32[]{:S(2)}) collective-permute-start(bf16[160,512]{1,0:T(8,128)(2,1)S(1)} %pad_maximum_fusion.4), channel_id=1, source_target_pairs={{0,2},{2,0},{4,6},{6,4},{1,3},{3,1},{5,7},{7,5},{8,10},{10,8},{12,... | collective-permute-start | bytes 491528 | tf_op jit(solution)/shard_map/ppermute | solution.py:143
  18.5 9.8 %collective-permute-start.5 = (bf16[160,512]{1,0:T(8,128)(2,1)S(1)}, bf16[160,512]{1,0:T(8,128)(2,1)S(1)}, u32[]{:S(2)}, u32[]{:S(2)}) collective-permute-start(bf16[160,512]{1,0:T(8,128)(2,1)S(1)} %pad_maximum_fusion.4), channel_id=1, source_target_pairs={{0,4},{2,6},{4,0},{6,2},{1,5},{3,7},{5,1},{7,3},{8,12},{10,14},{12... | collective-permute-start | bytes 491528 | tf_op jit(solution)/shard_map/ppermute | solution.py:144
  28.9 4.5 %collective-permute-start.6 = (bf16[160,256]{1,0:T(8,128)(2,1)S(1)}, bf16[160,256]{1,0:T(8,128)(2,1)S(1)}, u32[]{:S(2)}, u32[]{:S(2)}) collective-permute-start(bf16[160,256]{1,0:T(8,128)(2,1)S(1)} %convolution_convert_fusion.4), channel_id=1, source_target_pairs={{0,2},{2,0},{4,6},{6,4},{1,3},{3,1},{5,7},{7,5},{8,10},{10,8},{12,... | collective-permute-start | bytes 245768 | tf_op jit(solution)/shard_map/ppermute | solution.py:147
  29.5 4.5 %collective-permute-start.7 = (bf16[160,256]{1,0:T(8,128)(2,1)S(1)}, bf16[160,256]{1,0:T(8,128)(2,1)S(1)}, u32[]{:S(2)}, u32[]{:S(2)}) collective-permute-start(bf16[160,256]{1,0:T(8,128)(2,1)S(1)} %convolution_convert_fusion.3), channel_id=1, source_target_pairs={{0,4},{2,6},{4,0},{6,2},{1,5},{3,7},{5,1},{7,3},{8,12},{10,14},{12... | collective-permute-start | bytes 245768 | tf_op jit(solution)/shard_map/ppermute | solution.py:148

commit v19 on v17

--- a/solution.py
+++ b/solution.py
@@ -82,21 +82,14 @@
     )
     chip_kv = chip_rows[:, width:]
     if chips <= 8:
-        reach = chips // 2
-        mine = [list(range(1, reach + 1)), [chips - p for p in range(1, reach + 1)]]
-        fetched = []
-        for p in range(reach):
-            pairs = []
-            for i in range(chips):
-                for k in range(cores):
-                    pairs.append((i * cores + k, ((i + mine[k][p]) % chips) * cores + k))
-            fetched.append(lax.ppermute(chip_kv, BLK, pairs))
-        both = lax.all_gather(jnp.stack(fetched, 0), "core", axis=0, tiled=False)
-        pieces = {0: chip_kv}
-        for k in range(cores):
-            for p in range(reach):
-                pieces.setdefault(mine[k][p], both[k, p])
-        kv_pair = jnp.concatenate([pieces[s] for s in range(chips)], axis=0)
+        kv_pair = jnp.concatenate(
+            [chip_kv]
+            + [
+                lax.ppermute(chip_kv, "chip", [(i, (i + s) % chips) for i in range(chips)])
+                for s in range(1, chips)
+            ],
+            axis=0,
+        )
         src_chip = (lax.axis_index("chip") - jnp.arange(chips)) % chips
     else:
         kv_pair = lax.all_gather(chip_kv, "chip", axis=0, tiled=True)

time: 56.7 us -> 58.2 us (1.026)
  waiting for transfers between devices: 13.2 us -> 16.1 us
  blocking collectives: 26.7 us -> 24.9 us
    ppermute x1, waiting for transfers between devices: 7.84 us -> 10.4 us  [body(): att_x = lax.ppermute(chip_att, 'chip', [(i, i ^ 1) for i in range(chips)])]
    all_gather x1 -> x0, blocking collectives: 2.04 us -> none  [body(): both = lax.all_gather(jnp.stack(fetched, 0), 'core', axis=0, tiled=False)]
    ppermute x2 -> x3, starting transfers between devices: 4.41 us -> 5.84 us  [body(): lax.ppermute(chip_kv, 'chip', [(i, (i + s) % chips) for i in range(chips)])]
    ppermute x1, starting transfers between devices: 1.92 us -> 0.51 us  [body(): w_y = lax.ppermute(out_weight, 'chip', [(i, i ^ 2) for i in range(chips)])]
    ppermute x2 -> x3, waiting for transfers between devices: 1.56 us -> 2.19 us  [body(): lax.ppermute(chip_kv, 'chip', [(i, (i + s) % chips) for i in range(chips)])]
  transfers between devices with their start and end apart: 6 -> 7, of which waited for: 3 -> 4; matrix products, arithmetic and copies ran while one was open for 6% -> 6% of each run, Pallas kernels for 0% -> 0%
where the time goes in v19:
time: 58.2 us; the launch traced here: 58 us
  blocking collectives  24.9 us (43%)
  waiting for transfers between devices  16.1 us (28%)
  starting transfers between devices  9.21 us (16%)
  matrix products  2.88 us (5%)
  other arithmetic  2.84 us (5%)
  local copies, waits for them, and re-layouts  1.03 us (2%)
  between operations  1.02 us (2%)
    all_to_all x1, blocking collectives, body(): got = lax.all_to_all(routed, ('kv', 'core'), 0, 0, tiled=True)  22.8 us
    ppermute x1, waiting for transfers between devices, body(): att_x = lax.ppermute(chip_att, 'chip', [(i, i ^ 1) for i in range(chips)])  10.4 us
    ppermute x3, starting transfers between devices, body(): lax.ppermute(chip_kv, 'chip', [(i, (i + s) % chips) for i in range(chips)])  5.84 us
    ppermute x1, waiting for transfers between devices, body(): lax.ppermute(part(att_x, w_y), 'chip', [(i, i ^ 1) for i in range(chips)])  3.52 us
    ppermute x3, waiting for transfers between devices, body(): lax.ppermute(chip_kv, 'chip', [(i, (i + s) % chips) for i in range(chips)])  2.19 us
    all_gather x1, blocking collectives, body(): lax.all_gather(jnp.concatenate([rot_queries, rot_keys, values], axis=1),...  2.07 us
    dot_general x4, matrix products, part(): jnp.dot(att, w.T, preferred_element_type=jnp.float32).astype(jnp.bfloat16)  1.28 us
    ppermute x1, starting transfers between devices, body(): lax.ppermute(part(att_x, w_y), 'chip', [(i, i ^ 1) for i in range(chips)])  1.22 us
  transfers between devices with their start and end apart: 7, of which 4 were waited for; matrix products, arithmetic and copies ran while one was open for 6% of the time, Pallas kernels for 0%

profile of v19, /device:TPU:0, one launch (start us, length us, event | category | flops | bytes accessed | tf_op | source)
XLA Modules:
  0.0 58.0 jit_solution(12066671840421447246)
XLA Ops:
  0.7 0.8 %select_reduce_fusion.1 = s32[5]{0:T(128)S(1)} fusion(s32[4]{0:T(128)} %param.10, s32[5]{0:T(128)S(1)} %iota_add_fusion.3), kind=kLoop, calls=%fused_computation.50 | loop fusion | flops 55 | bytes 56 | tf_op jit(solution)/shard_map/reduce_sum | solution.py:53
  1.6 0.2 multiply_cosine_fusion
  2.8 0.2 fusion.6
  3.0 2.1 %all_gather.3 = bf16[160,768]{1,0:T(8,128)(2,1)S(1)} all-gather(bf16[80,768]{1,0:T(8,128)(2,1)S(1)} %pad_maximum_fusion.5), channel_id=1, replica_groups=mesh['kv'=4,'chip'=4,'core'=2] {'core'}, dimensions={0}, use_global_device_ids=true | all-gather | bytes 368640 | tf_op jit(solution)/shard_map/all_gather | solution.py:80
  5.1 2.9 %collective-permute-start = (bf16[160,256]{1,0:T(8,128)(2,1)S(1)}, bf16[160,256]{1,0:T(8,128)(2,1)S(1)}, u32[]{:S(2)}, u32[]{:S(2)}) collective-permute-start(bf16[160,256]{1,0:T(8,128)(2,1)S(1)} %slice.63), channel_id=1, source_target_pairs={{0,2},{2,4},{4,6},{6,0},{1,3},{3,5},{5,7},{7,1},{8,10},{10,12},{12... | collective-permute-start | bytes 245768 | tf_op jit(solution)/shard_map/ppermute | solution.py:88
  8.0 1.5 %collective-permute-start.1 = (bf16[160,256]{1,0:T(8,128)(2,1)S(1)}, bf16[160,256]{1,0:T(8,128)(2,1)S(1)}, u32[]{:S(2)}, u32[]{:S(2)}) collective-permute-start(bf16[160,256]{1,0:T(8,128)(2,1)S(1)} %slice.63), channel_id=1, source_target_pairs={{0,4},{2,6},{4,0},{6,2},{1,5},{3,7},{5,1},{7,3},{8,12},{10,14},{12... | collective-permute-start | bytes 245768 | tf_op jit(solution)/shard_map/ppermute | solution.py:88
  9.5 1.4 %collective-permute-start.2 = (bf16[160,256]{1,0:T(8,128)(2,1)S(1)}, bf16[160,256]{1,0:T(8,128)(2,1)S(1)}, u32[]{:S(2)}, u32[]{:S(2)}) collective-permute-start(bf16[160,256]{1,0:T(8,128)(2,1)S(1)} %slice.63), channel_id=1, source_target_pairs={{0,6},{2,0},{4,2},{6,4},{1,7},{3,1},{5,3},{7,5},{8,14},{10,8},{12,... | collective-permute-start | bytes 245768 | tf_op jit(solution)/shard_map/ppermute | solution.py:88
  10.9 0.6 %collective-permute-start.3 = (bf16[512,512]{1,0:T(8,128)(2,1)S(1)}, bf16[512,512]{1,0:T(8,128)(2,1)S(1)}, u32[]{:S(2)}, u32[]{:S(2)}) collective-permute-start(bf16[512,512]{1,0:T(8,128)(2,1)S(1)} %copy-done.6), channel_id=1, source_target_pairs={{0,2},{2,0},{4,6},{6,4},{1,3},{3,1},{5,7},{7,5},{8,10},{10,8},{12,... | collective-permute-start | bytes 1572872 | tf_op jit(solution)/shard_map/ppermute | solution.py:63
  11.5 0.5 collective-permute-start.4
  12.6 0.9 %collective-permute-done.1 = bf16[160,256]{1,0:T(8,128)(2,1)S(1)} collective-permute-done((bf16[160,256]{1,0:T(8,128)(2,1)S(1)}, bf16[160,256]{1,0:T(8,128)(2,1)S(1)}, u32[]{:S(2)}, u32[]{:S(2)}) %collective-permute-start.1) | collective-permute-done | bytes 81952 | tf_op jit(solution)/shard_map/ppermute | solution.py:88
  13.5 1.3 %collective-permute-done.2 = bf16[160,256]{1,0:T(8,128)(2,1)S(1)} collective-permute-done((bf16[160,256]{1,0:T(8,128)(2,1)S(1)}, bf16[160,256]{1,0:T(8,128)(2,1)S(1)}, u32[]{:S(2)}, u32[]{:S(2)}) %collective-permute-start.2) | collective-permute-done | bytes 81952 | tf_op jit(solution)/shard_map/ppermute | solution.py:88
  14.8 0.6 fusion.30
  15.4 0.5 fusion.10
  15.9 0.7 %fusion = bf16[640,128]{1,0:T(8,128)(2,1)S(1)} fusion(f32[640,640]{0,1:T(8,128)S(1)} %get-tuple-element.25, f32[640]{0:T(1024)S(1)} %get-tuple-element.24, s32[640]{0:T(1024)S(1)} %le.61, s32[640]{0:T(1024)S(1)} %eq.26, s32[640]{0:T(1024)S(1)} %add.103, s32[640]{0:T(1024)S(1)} %broadcast_add_fusion, bf16[640,256]{1,0:T(8,128)(2,1)S(1)} %pad_maximum_fusion.2, ...), kind=kOutput, calls=%fused_computation.8 | convolution fusion | flops 107479040 | bytes 1990656 | tf_op jit(solution)/shard_map/dot_general | solution.py:121
  16.6 1.1 %collective-permute-start.5 = (bf16[160,512]{1,0:T(8,128)(2,1)S(1)}, bf16[160,512]{1,0:T(8,128)(2,1)S(1)}, u32[]{:S(2)}, u32[]{:S(2)}) collective-permute-start(bf16[160,512]{1,0:T(8,128)(2,1)S(1)} %pad_maximum_fusion.3), channel_id=1, source_target_pairs={{0,2},{2,0},{4,6},{6,4},{1,3},{3,1},{5,7},{7,5},{8,10},{10,8},{12,... | collective-permute-start | bytes 491528 | tf_op jit(solution)/shard_map/ppermute | solution.py:134
  17.7 0.3 fusion.1
  18.0 10.4 %collective-permute-done.5 = bf16[160,512]{1,0:T(8,128)(2,1)S(1)} collective-permute-done((bf16[160,512]{1,0:T(8,128)(2,1)S(1)}, bf16[160,512]{1,0:T(8,128)(2,1)S(1)}, u32[]{:S(2)}, u32[]{:S(2)}) %collective-permute-start.5) | collective-permute-done | bytes 163872 | tf_op jit(solution)/shard_map/ppermute | solution.py:134
  28.4 0.3 convolution_convert_fusion
  28.7 1.2 %collective-permute-start.6 = (bf16[160,512]{1,0:T(8,128)(2,1)S(1)}, bf16[160,512]{1,0:T(8,128)(2,1)S(1)}, u32[]{:S(2)}, u32[]{:S(2)}) collective-permute-start(bf16[160,512]{1,0:T(8,128)(2,1)S(1)} %convolution_convert_fusion), channel_id=1, source_target_pairs={{0,2},{2,0},{4,6},{6,4},{1,3},{3,1},{5,7},{7,5},{8,10},{10,8},{12,... | collective-permute-start | bytes 491528 | tf_op jit(solution)/shard_map/ppermute | solution.py:136
  30.0 0.3 fusion.3
  30.3 0.3 fusion.2
  30.6 3.5 %collective-permute-done.6 = bf16[160,512]{1,0:T(8,128)(2,1)S(1)} collective-permute-done((bf16[160,512]{1,0:T(8,128)(2,1)S(1)}, bf16[160,512]{1,0:T(8,128)(2,1)S(1)}, u32[]{:S(2)}, u32[]{:S(2)}) %collective-permute-start.6) | collective-permute-done | bytes 163872 | tf_op jit(solution)/shard_map/ppermute | solution.py:136
  34.4 22.8 %all_to_all.5 = bf16[8,80,512]{2,1,0:T(8,128)(2,1)S(1)} all-to-all(bf16[8,80,512]{2,1,0:T(8,128)(2,1)S(1)} %bitcast.40), channel_id=1, replica_groups=mesh['kv'=4,'chip'=4,'core'=2] {'kv','core'}, dimensions={0} | all-to-all | bytes 1310720 | tf_op jit(solution)/shard_map/all_to_all | solution.py:154
  57.3 0.7 %pad_maximum_fusion.4 = bf16[80,1024]{1,0:T(8,128)(2,1)} fusion(bf16[80,512]{1,0:T(8,128)(2,1)S(1)} %get-tuple-element.17, bf16[80,512]{1,0:T(8,128)(2,1)S(1)} %get-tuple-element.16), kind=kLoop, calls=%fused_computation.37 | loop fusion | flops 327680 | bytes 327680 | tf_op jit(solution)/shard_map/concatenate | solution.py:158
  (57 shorter events, 1.9 us)
Async XLA Ops:
  0.6 1.9 %copy-start.3 = (bf16[128,128]{1,0:T(8,128)(2,1)S(1)}, bf16[128,128]{1,0:T(8,128)(2,1)}, u32[]{:S(2)}) copy-start(bf16[128,128]{1,0:T(8,128)(2,1)} %constant.72.clone) | copy-start | bytes 98308
  0.6 2.1 %copy-start = (bf16[512,512]{1,0:T(8,128)(2,1)S(1)}, bf16[512,512]{1,0:T(8,128)(2,1)}, u32[]{:S(2)}) copy-start(bf16[512,512]{1,0:T(8,128)(2,1)} %constant.73.clone) | copy-start | bytes 1572868
  0.7 1.9 %copy-start.4 = (bf16[80,128]{1,0:T(8,128)(2,1)S(1)}, bf16[80,128]{1,0:T(8,128)(2,1)}, u32[]{:S(2)}) copy-start(bf16[80,128]{1,0:T(8,128)(2,1)} %param.8) | copy-start | bytes 61444
  0.7 2.1 %copy-start.2 = (bf16[80,512]{1,0:T(8,128)(2,1)S(1)}, bf16[80,512]{1,0:T(8,128)(2,1)}, u32[]{:S(2)}) copy-start(bf16[80,512]{1,0:T(8,128)(2,1)} %param.7) | copy-start | bytes 245764
  1.9 1.0 %copy-start.5 = (bf16[80,128]{1,0:T(8,128)(2,1)S(1)}, bf16[80,128]{1,0:T(8,128)(2,1)}, u32[]{:S(2)}) copy-start(bf16[80,128]{1,0:T(8,128)(2,1)} %param.9) | copy-start | bytes 61444
  2.2 8.7 %copy-start.6 = (bf16[512,512]{1,0:T(8,128)(2,1)S(1)}, bf16[512,512]{1,0:T(8,128)(2,1)}, u32[]{:S(2)}) copy-start(bf16[512,512]{1,0:T(8,128)(2,1)} %param.11) | copy-start | bytes 1572868
  2.7 12.7 %copy-start.1 = (bf16[80,128]{1,0:T(8,128)(2,1)}, bf16[80,128]{1,0:T(8,128)(2,1)S(1)}, u32[]{:S(2)}) copy-start(bf16[80,128]{1,0:T(8,128)(2,1)S(1)} %fusion.9) | copy-start | bytes 61444
  5.1 7.5 %collective-permute-start = (bf16[160,256]{1,0:T(8,128)(2,1)S(1)}, bf16[160,256]{1,0:T(8,128)(2,1)S(1)}, u32[]{:S(2)}, u32[]{:S(2)}) collective-permute-start(bf16[160,256]{1,0:T(8,128)(2,1)S(1)} %slice.63), channel_id=1, source_target_pairs={{0,2},{2,4},{4,6},{6,0},{1,3},{3,5},{5,7},{7,1},{8,10},{10,12},{12... | collective-permute-start | bytes 245768 | tf_op jit(solution)/shard_map/ppermute | solution.py:88
  8.0 5.5 %collective-permute-start.1 = (bf16[160,256]{1,0:T(8,128)(2,1)S(1)}, bf16[160,256]{1,0:T(8,128)(2,1)S(1)}, u32[]{:S(2)}, u32[]{:S(2)}) collective-permute-start(bf16[160,256]{1,0:T(8,128)(2,1)S(1)} %slice.63), channel_id=1, source_target_pairs={{0,4},{2,6},{4,0},{6,2},{1,5},{3,7},{5,1},{7,3},{8,12},{10,14},{12... | collective-permute-start | bytes 245768 | tf_op jit(solution)/shard_map/ppermute | solution.py:88
  9.5 5.3 %collective-permute-start.2 = (bf16[160,256]{1,0:T(8,128)(2,1)S(1)}, bf16[160,256]{1,0:T(8,128)(2,1)S(1)}, u32[]{:S(2)}, u32[]{:S(2)}) collective-permute-start(bf16[160,256]{1,0:T(8,128)(2,1)S(1)} %slice.63), channel_id=1, source_target_pairs={{0,6},{2,0},{4,2},{6,4},{1,7},{3,1},{5,3},{7,5},{8,14},{10,8},{12,... | collective-permute-start | bytes 245768 | tf_op jit(solution)/shard_map/ppermute | solution.py:88
  10.9 17.5 %collective-permute-start.3 = (bf16[512,512]{1,0:T(8,128)(2,1)S(1)}, bf16[512,512]{1,0:T(8,128)(2,1)S(1)}, u32[]{:S(2)}, u32[]{:S(2)}) collective-permute-start(bf16[512,512]{1,0:T(8,128)(2,1)S(1)} %copy-done.6), channel_id=1, source_target_pairs={{0,2},{2,0},{4,6},{6,4},{1,3},{3,1},{5,7},{7,5},{8,10},{10,8},{12,... | collective-permute-start | bytes 1572872 | tf_op jit(solution)/shard_map/ppermute | solution.py:63
  11.5 16.9 %collective-permute-start.4 = (bf16[512,512]{1,0:T(8,128)(2,1)S(1)}, bf16[512,512]{1,0:T(8,128)(2,1)S(1)}, u32[]{:S(2)}, u32[]{:S(2)}) collective-permute-start(bf16[512,512]{1,0:T(8,128)(2,1)S(1)} %copy-done.6), channel_id=1, source_target_pairs={{0,4},{2,6},{4,0},{6,2},{1,5},{3,7},{5,1},{7,3},{8,12},{10,14},{12... | collective-permute-start | bytes 1572872 | tf_op jit(solution)/shard_map/ppermute | solution.py:64
  16.6 11.8 %collective-permute-start.5 = (bf16[160,512]{1,0:T(8,128)(2,1)S(1)}, bf16[160,512]{1,0:T(8,128)(2,1)S(1)}, u32[]{:S(2)}, u32[]{:S(2)}) collective-permute-start(bf16[160,512]{1,0:T(8,128)(2,1)S(1)} %pad_maximum_fusion.3), channel_id=1, source_target_pairs={{0,2},{2,0},{4,6},{6,4},{1,3},{3,1},{5,7},{7,5},{8,10},{10,8},{12,... | collective-permute-start | bytes 491528 | tf_op jit(solution)/shard_map/ppermute | solution.py:134
  28.7 5.4 %collective-permute-start.6 = (bf16[160,512]{1,0:T(8,128)(2,1)S(1)}, bf16[160,512]{1,0:T(8,128)(2,1)S(1)}, u32[]{:S(2)}, u32[]{:S(2)}) collective-permute-start(bf16[160,512]{1,0:T(8,128)(2,1)S(1)} %convolution_convert_fusion), channel_id=1, source_target_pairs={{0,2},{2,0},{4,6},{6,4},{1,3},{3,1},{5,7},{7,5},{8,10},{10,8},{12,... | collective-permute-start | bytes 491528 | tf_op jit(solution)/shard_map/ppermute | solution.py:136

commit v20 on v15

--- a/solution.py
+++ b/solution.py
@@ -138,8 +138,9 @@
         def part(att, w):
             return jnp.dot(att, w.T, preferred_element_type=jnp.float32).astype(jnp.bfloat16)
 
-        att_x = lax.ppermute(chip_att, "chip", [(i, i ^ 1) for i in range(chips)])
-        diag = lax.ppermute(part(att_x, w_y), "chip", [(i, i ^ 1) for i in range(chips)])
+        att_y = lax.ppermute(chip_att, "chip", [(i, i ^ 2) for i in range(chips)])
+        w_x, w_y, att_y = lax.optimization_barrier((w_x, w_y, att_y))
+        diag = lax.ppermute(part(att_y, w_x), "chip", [(i, i ^ 2) for i in range(chips)])
         by_dist = jnp.stack([part(chip_att, out_weight), part(chip_att, w_x), part(chip_att, w_y), diag])
         here = lax.axis_index("chip")
         routed = jnp.stack(

time: 62.7 us -> 59.1 us (0.943)
  waiting for transfers between devices: 19.7 us -> 14.9 us
  starting transfers between devices: 8.07 us -> 9.06 us
    ppermute x1, waiting for transfers between devices: 9.4 us -> 0.01 us  [body(): w_x = lax.ppermute(out_weight, 'chip', [(i, i ^ 1) for i in range(chips)])]
    ppermute x2, waiting for transfers between devices: 7.09 us -> 13.3 us  [the longest x1 8.78 us: body(): att_y = lax.ppermute(chip_att, 'chip', [(i, i ^ 2) for i in range(chips)])]
    ppermute x2, waiting for transfers between devices: 3.05 us -> 1.56 us  [body(): fetched.append(lax.ppermute(chip_kv, BLK, pairs))]
    ppermute x1, starting transfers between devices: 0.51 us -> 1.92 us  [body(): w_y = lax.ppermute(out_weight, 'chip', [(i, i ^ 2) for i in range(chips)])]
    ppermute x1, starting transfers between devices: 0.91 us -> 0.08 us  [body(): w_x = lax.ppermute(out_weight, 'chip', [(i, i ^ 1) for i in range(chips)])]
  transfers between devices with their start and end apart: 6 -> 6, of which waited for: 6 -> 3; matrix products, arithmetic and copies ran while one was open for 6% -> 6% of each run, Pallas kernels for 0% -> 0%
where the time goes in v20:
time: 59.1 us; the launch traced here: 58.9 us
  blocking collectives  27.1 us (46%)
  waiting for transfers between devices  14.9 us (25%)
  starting transfers between devices  9.06 us (15%)
  matrix products  2.87 us (5%)
  other arithmetic  2.86 us (5%)
  local copies, waits for them, and re-layouts  1.05 us (2%)
  between operations  1.03 us (2%)
    all_to_all x1, blocking collectives, body(): got = lax.all_to_all(routed, ('kv', 'core'), 0, 0, tiled=True)  23 us
    ppermute x1, waiting for transfers between devices, body(): att_y = lax.ppermute(chip_att, 'chip', [(i, i ^ 2) for i in range(chips)])  8.78 us
    ppermute x1, waiting for transfers between devices, body(): lax.ppermute(part(att_y, w_x), 'chip', [(i, i ^ 2) for i in range(chips)])  4.53 us
    ppermute x2, starting transfers between devices, body(): fetched.append(lax.ppermute(chip_kv, BLK, pairs))  4.41 us
    all_gather x1, blocking collectives, body(): lax.all_gather(jnp.concatenate([rot_queries, rot_keys, values], axis=1),...  2.07 us
    all_gather x1, blocking collectives, body(): both = lax.all_gather(jnp.stack(fetched, 0), 'core', axis=0, tiled=False)  2.04 us
    ppermute x1, starting transfers between devices, body(): w_y = lax.ppermute(out_weight, 'chip', [(i, i ^ 2) for i in range(chips)])  1.92 us
    ppermute x1, starting transfers between devices, body(): att_y = lax.ppermute(chip_att, 'chip', [(i, i ^ 2) for i in range(chips)])  1.65 us
  transfers between devices with their start and end apart: 6, of which 3 were waited for; matrix products, arithmetic and copies ran while one was open for 6% of the time, Pallas kernels for 0%

profile of v20, /device:TPU:0, one launch (start us, length us, event | category | flops | bytes accessed | tf_op | source)
XLA Modules:
  0.0 58.9 jit_solution(3232922095390830773)
XLA Ops:
  0.7 0.8 %select_reduce_fusion.1 = s32[5]{0:T(128)S(1)} fusion(s32[4]{0:T(128)} %param.10, s32[5]{0:T(128)S(1)} %iota_add_fusion.3), kind=kLoop, calls=%fused_computation.54 | loop fusion | flops 55 | bytes 56 | tf_op jit(solution)/shard_map/reduce_sum | solution.py:53
  1.6 0.2 multiply_cosine_fusion
  2.3 0.1 tile.23
  2.6 0.1 fusion.9
  2.8 0.2 fusion.6
  3.0 2.1 %all_gather.9 = bf16[160,768]{1,0:T(8,128)(2,1)S(1)} all-gather(bf16[80,768]{1,0:T(8,128)(2,1)S(1)} %pad_maximum_fusion.6), channel_id=1, replica_groups=mesh['kv'=4,'chip'=4,'core'=2] {'core'}, dimensions={0}, use_global_device_ids=true | all-gather | bytes 368640 | tf_op jit(solution)/shard_map/all_gather | solution.py:80
  5.1 2.9 %collective-permute-start = (bf16[160,256]{1,0:T(8,128)(2,1)S(1)}, bf16[160,256]{1,0:T(8,128)(2,1)S(1)}, u32[]{:S(2)}, u32[]{:S(2)}) collective-permute-start(bf16[160,256]{1,0:T(8,128)(2,1)S(1)} %slice.75), channel_id=1, source_target_pairs={{0,2},{1,7},{2,4},{3,1},{4,6},{5,3},{6,0},{7,5},{8,10},{9,15},{10,... | collective-permute-start | bytes 245768 | tf_op jit(solution)/shard_map/ppermute | solution.py:93
  8.0 1.5 %collective-permute-start.1 = (bf16[160,256]{1,0:T(8,128)(2,1)S(1)}, bf16[160,256]{1,0:T(8,128)(2,1)S(1)}, u32[]{:S(2)}, u32[]{:S(2)}) collective-permute-start(bf16[160,256]{1,0:T(8,128)(2,1)S(1)} %slice.75), channel_id=1, source_target_pairs={{0,4},{1,5},{2,6},{3,7},{4,0},{5,1},{6,2},{7,3},{8,12},{9,13},{10,... | collective-permute-start | bytes 245768 | tf_op jit(solution)/shard_map/ppermute | solution.py:93
  9.6 1.9 %collective-permute-start.3 = (bf16[512,512]{1,0:T(8,128)(2,1)S(1)}, bf16[512,512]{1,0:T(8,128)(2,1)S(1)}, u32[]{:S(2)}, u32[]{:S(2)}) collective-permute-start(bf16[512,512]{1,0:T(8,128)(2,1)S(1)} %copy-done.6), channel_id=1, source_target_pairs={{0,4},{2,6},{4,0},{6,2},{1,5},{3,7},{5,1},{7,3},{8,12},{10,14},{12... | collective-permute-start | bytes 1572872 | tf_op jit(solution)/shard_map/ppermute | solution.py:64
  12.1 1.6 %collective-permute-done.1 = bf16[160,256]{1,0:T(8,128)(2,1)S(1)} collective-permute-done((bf16[160,256]{1,0:T(8,128)(2,1)S(1)}, bf16[160,256]{1,0:T(8,128)(2,1)S(1)}, u32[]{:S(2)}, u32[]{:S(2)}) %collective-permute-start.1) | collective-permute-done | bytes 81952 | tf_op jit(solution)/shard_map/ppermute | solution.py:93
  13.7 2.0 %all-gather = bf16[4,160,256]{2,1,0:T(8,128)(2,1)S(1)} all-gather(bf16[2,160,256]{2,1,0:T(8,128)(2,1)S(1)} %pad_maximum_fusion.3), channel_id=2, replica_groups=mesh['kv'=4,'chip'=4,'core'=2] {'core'}, dimensions={0}, use_global_device_ids=true | all-gather | bytes 491520 | tf_op jit(solution)/shard_map/all_gather | solution.py:94
  15.8 0.6 fusion.30
  16.3 0.5 fusion.10
  16.8 0.7 %fusion = bf16[640,128]{1,0:T(8,128)(2,1)S(1)} fusion(f32[640,640]{0,1:T(8,128)S(1)} %get-tuple-element.28, f32[640]{0:T(1024)S(1)} %get-tuple-element.27, s32[640]{0:T(1024)S(1)} %le.61, s32[640]{0:T(1024)S(1)} %eq.26, s32[640]{0:T(1024)S(1)} %add.103, s32[640]{0:T(1024)S(1)} %broadcast_add_fusion, bf16[640,256]{1,0:T(8,128)(2,1)S(1)} %pad_maximum_fusion.2, ...), kind=kOutput, calls=%fused_computation.8 | convolution fusion | flops 107479040 | bytes 1990656 | tf_op jit(solution)/shard_map/dot_general | solution.py:128
  17.5 1.6 %collective-permute-start.4 = (bf16[160,512]{1,0:T(8,128)(2,1)S(1)}, bf16[160,512]{1,0:T(8,128)(2,1)S(1)}, u32[]{:S(2)}, u32[]{:S(2)}) collective-permute-start(bf16[160,512]{1,0:T(8,128)(2,1)S(1)} %pad_maximum_fusion.4), channel_id=1, source_target_pairs={{0,4},{2,6},{4,0},{6,2},{1,5},{3,7},{5,1},{7,3},{8,12},{10,14},{12... | collective-permute-start | bytes 491528 | tf_op jit(solution)/shard_map/ppermute | solution.py:141
  19.2 0.3 fusion.1
  19.5 8.8 %collective-permute-done.4 = bf16[160,512]{1,0:T(8,128)(2,1)S(1)} collective-permute-done((bf16[160,512]{1,0:T(8,128)(2,1)S(1)}, bf16[160,512]{1,0:T(8,128)(2,1)S(1)}, u32[]{:S(2)}, u32[]{:S(2)}) %collective-permute-start.4) | collective-permute-done | bytes 163872 | tf_op jit(solution)/shard_map/ppermute | solution.py:141
  28.3 0.3 convolution_convert_fusion
  28.6 1.0 %collective-permute-start.5 = (bf16[160,512]{1,0:T(8,128)(2,1)S(1)}, bf16[160,512]{1,0:T(8,128)(2,1)S(1)}, u32[]{:S(2)}, u32[]{:S(2)}) collective-permute-start(bf16[160,512]{1,0:T(8,128)(2,1)S(1)} %convolution_convert_fusion), channel_id=1, source_target_pairs={{0,4},{2,6},{4,0},{6,2},{1,5},{3,7},{5,1},{7,3},{8,12},{10,14},{12... | collective-permute-start | bytes 491528 | tf_op jit(solution)/shard_map/ppermute | solution.py:143
  29.6 0.3 fusion.2
  29.9 0.3 fusion.3
  30.3 4.5 %collective-permute-done.5 = bf16[160,512]{1,0:T(8,128)(2,1)S(1)} collective-permute-done((bf16[160,512]{1,0:T(8,128)(2,1)S(1)}, bf16[160,512]{1,0:T(8,128)(2,1)S(1)}, u32[]{:S(2)}, u32[]{:S(2)}) %collective-permute-start.5) | collective-permute-done | bytes 163872 | tf_op jit(solution)/shard_map/ppermute | solution.py:143
  35.1 23.0 %all_to_all.5 = bf16[8,80,512]{2,1,0:T(8,128)(2,1)S(1)} all-to-all(bf16[8,80,512]{2,1,0:T(8,128)(2,1)S(1)} %bitcast.49), channel_id=1, replica_groups=mesh['kv'=4,'chip'=4,'core'=2] {'kv','core'}, dimensions={0} | all-to-all | bytes 1310720 | tf_op jit(solution)/shard_map/all_to_all | solution.py:161
  58.2 0.7 %pad_maximum_fusion.5 = bf16[80,1024]{1,0:T(8,128)(2,1)} fusion(bf16[80,512]{1,0:T(8,128)(2,1)S(1)} %get-tuple-element.20, bf16[80,512]{1,0:T(8,128)(2,1)S(1)} %get-tuple-element.19), kind=kLoop, calls=%fused_computation.38 | loop fusion | flops 327680 | bytes 327680 | tf_op jit(solution)/shard_map/concatenate | solution.py:165
  (58 shorter events, 1.7 us)
Async XLA Ops:
  0.6 1.9 %copy-start.3 = (bf16[128,128]{1,0:T(8,128)(2,1)S(1)}, bf16[128,128]{1,0:T(8,128)(2,1)}, u32[]{:S(2)}) copy-start(bf16[128,128]{1,0:T(8,128)(2,1)} %constant.72.clone) | copy-start | bytes 98308
  0.6 2.1 %copy-start = (bf16[512,512]{1,0:T(8,128)(2,1)S(1)}, bf16[512,512]{1,0:T(8,128)(2,1)}, u32[]{:S(2)}) copy-start(bf16[512,512]{1,0:T(8,128)(2,1)} %constant.73.clone) | copy-start | bytes 1572868
  0.7 1.9 %copy-start.4 = (bf16[80,128]{1,0:T(8,128)(2,1)S(1)}, bf16[80,128]{1,0:T(8,128)(2,1)}, u32[]{:S(2)}) copy-start(bf16[80,128]{1,0:T(8,128)(2,1)} %param.8) | copy-start | bytes 61444
  0.7 2.1 %copy-start.2 = (bf16[80,512]{1,0:T(8,128)(2,1)S(1)}, bf16[80,512]{1,0:T(8,128)(2,1)}, u32[]{:S(2)}) copy-start(bf16[80,512]{1,0:T(8,128)(2,1)} %param.7) | copy-start | bytes 245764
  1.9 1.0 %copy-start.5 = (bf16[80,128]{1,0:T(8,128)(2,1)S(1)}, bf16[80,128]{1,0:T(8,128)(2,1)}, u32[]{:S(2)}) copy-start(bf16[80,128]{1,0:T(8,128)(2,1)} %param.9) | copy-start | bytes 61444
  2.2 7.3 %copy-start.6 = (bf16[512,512]{1,0:T(8,128)(2,1)S(1)}, bf16[512,512]{1,0:T(8,128)(2,1)}, u32[]{:S(2)}) copy-start(bf16[512,512]{1,0:T(8,128)(2,1)} %param.11) | copy-start | bytes 1572868
  2.7 13.0 %copy-start.1 = (bf16[80,128]{1,0:T(8,128)(2,1)}, bf16[80,128]{1,0:T(8,128)(2,1)S(1)}, u32[]{:S(2)}) copy-start(bf16[80,128]{1,0:T(8,128)(2,1)S(1)} %fusion.9) | copy-start | bytes 61444
  5.1 7.0 %collective-permute-start = (bf16[160,256]{1,0:T(8,128)(2,1)S(1)}, bf16[160,256]{1,0:T(8,128)(2,1)S(1)}, u32[]{:S(2)}, u32[]{:S(2)}) collective-permute-start(bf16[160,256]{1,0:T(8,128)(2,1)S(1)} %slice.75), channel_id=1, source_target_pairs={{0,2},{1,7},{2,4},{3,1},{4,6},{5,3},{6,0},{7,5},{8,10},{9,15},{10,... | collective-permute-start | bytes 245768 | tf_op jit(solution)/shard_map/ppermute | solution.py:93
  8.0 5.7 %collective-permute-start.1 = (bf16[160,256]{1,0:T(8,128)(2,1)S(1)}, bf16[160,256]{1,0:T(8,128)(2,1)S(1)}, u32[]{:S(2)}, u32[]{:S(2)}) collective-permute-start(bf16[160,256]{1,0:T(8,128)(2,1)S(1)} %slice.75), channel_id=1, source_target_pairs={{0,4},{1,5},{2,6},{3,7},{4,0},{5,1},{6,2},{7,3},{8,12},{9,13},{10,... | collective-permute-start | bytes 245768 | tf_op jit(solution)/shard_map/ppermute | solution.py:93
  9.5 18.8 %collective-permute-start.2 = (bf16[512,512]{1,0:T(8,128)(2,1)S(1)}, bf16[512,512]{1,0:T(8,128)(2,1)S(1)}, u32[]{:S(2)}, u32[]{:S(2)}) collective-permute-start(bf16[512,512]{1,0:T(8,128)(2,1)S(1)} %copy-done.6), channel_id=1, source_target_pairs={{0,2},{2,0},{4,6},{6,4},{1,3},{3,1},{5,7},{7,5},{8,10},{10,8},{12,... | collective-permute-start | bytes 1572872 | tf_op jit(solution)/shard_map/ppermute | solution.py:63
  9.6 18.7 %collective-permute-start.3 = (bf16[512,512]{1,0:T(8,128)(2,1)S(1)}, bf16[512,512]{1,0:T(8,128)(2,1)S(1)}, u32[]{:S(2)}, u32[]{:S(2)}) collective-permute-start(bf16[512,512]{1,0:T(8,128)(2,1)S(1)} %copy-done.6), channel_id=1, source_target_pairs={{0,4},{2,6},{4,0},{6,2},{1,5},{3,7},{5,1},{7,3},{8,12},{10,14},{12... | collective-permute-start | bytes 1572872 | tf_op jit(solution)/shard_map/ppermute | solution.py:64
  17.5 10.7 %collective-permute-start.4 = (bf16[160,512]{1,0:T(8,128)(2,1)S(1)}, bf16[160,512]{1,0:T(8,128)(2,1)S(1)}, u32[]{:S(2)}, u32[]{:S(2)}) collective-permute-start(bf16[160,512]{1,0:T(8,128)(2,1)S(1)} %pad_maximum_fusion.4), channel_id=1, source_target_pairs={{0,4},{2,6},{4,0},{6,2},{1,5},{3,7},{5,1},{7,3},{8,12},{10,14},{12... | collective-permute-start | bytes 491528 | tf_op jit(solution)/shard_map/ppermute | solution.py:141
  28.6 6.2 %collective-permute-start.5 = (bf16[160,512]{1,0:T(8,128)(2,1)S(1)}, bf16[160,512]{1,0:T(8,128)(2,1)S(1)}, u32[]{:S(2)}, u32[]{:S(2)}) collective-permute-start(bf16[160,512]{1,0:T(8,128)(2,1)S(1)} %convolution_convert_fusion), channel_id=1, source_target_pairs={{0,4},{2,6},{4,0},{6,2},{1,5},{3,7},{5,1},{7,3},{8,12},{10,14},{12... | collective-permute-start | bytes 491528 | tf_op jit(solution)/shard_map/ppermute | solution.py:143
